TPU v7x, 512 devices: a whole 4x4x16 slice. The times are simulated.
512 devices in a mesh: req: 8 (over z_lo), row: 8 (over x, core), col: 8 (over y, z_hi).
Axes of the slice: x: 4, y: 4, z: 16 (z_hi: 2, z_lo: 8; z = z_hi * 8 + z_lo), core: 2. Of those that a mesh axis runs over, the one named last changes fastest.
Arguments:
- tokens: bfloat16 [1792, 32768], P('col', ('req', 'row')), may hold values from -6 to 6
- qkv_weight: bfloat16 [1792, 2304], P('col', 'row'), may hold values from -0.125 to 0.125
- out_weight: bfloat16 [1792, 1792], P('row', 'col'), may hold values from -0.125 to 0.125
- head_gain: float32 [1792], P('row'), may hold values from 0.1 to 1.9
- prefix_keys: bfloat16 [24, 256, 8192], P('req', 'row', 'col'), may hold values from -6 to 6
- prefix_values: bfloat16 [24, 1792, 8192], P('req', 'row', 'col'), may hold values from -6 to 6
- suffix_len: int32 [64], P(('req', 'col')), may hold values from 1 to 512, 24576 in all
- prefix_owner: int32 [64], P(('req', 'col')), may hold values from 0 to 23
Outputs:
- layer_out: bfloat16 [1792, 32768], P('col', ('req', 'row'))
Inputs may be any that keep to these rules, and one draw needn't show every extreme that they name: `suffix_len`: the longest suffix has exactly 512 live tokens.
All inputs are finite; a program needn't handle non-finite values. No bound on the sum of `suffix_len` on one device may be relied on, other than what follows from the above.
Results may differ from a plain program's by a relative error of at most 0.015.
Values may be sent and summed in bfloat16 or wider, within the bound.
No kernel may reach another device: no remote copies, remote signals or barrier semaphores. Data moves between devices by JAX's collectives and lax.ppermute only.
A program may use at most 64 MiB of HBM per device.

v0:
```python
import jax
import jax.numpy as jnp
from jax import lax
from jax.sharding import PartitionSpec as P

FEAT = 16
SLOTS = 512
HD = 112


epsilon = 1e-05


def feature_map(values_in):
    feature_count = values_in.shape[-1]
    squares = (values_in[..., :, None] * values_in[..., None, :]).reshape(
        values_in.shape[:-1] + (feature_count * feature_count,)
    )
    constant = jnp.ones(values_in.shape[:-1] + (1,), jnp.float32)
    linear = values_in * feature_count ** (-0.25)
    quadratic = squares * (0.5**0.5 / feature_count**0.5)
    return jnp.concatenate([constant, linear, quadratic], axis=-1).astype(jnp.bfloat16)


def feature_columns(values_in):
    feature_count = values_in.shape[-2]
    length = values_in.shape[-1]
    squares = (values_in[..., :, None, :] * values_in[..., None, :, :]).reshape(
        values_in.shape[:-2] + (feature_count * feature_count, length)
    )
    constant = jnp.ones(values_in.shape[:-2] + (1, length), jnp.float32)
    linear = values_in * feature_count ** (-0.25)
    quadratic = squares * (0.5**0.5 / feature_count**0.5)
    return jnp.concatenate([constant, linear, quadratic], axis=-2).astype(jnp.bfloat16)


def shards(
    tokens, qkv_weight, out_weight, head_gain, prefix_keys, prefix_values, suffix_len, prefix_owner
):
    heads_here = head_gain.shape[0] // HD
    partial_proj = lax.dot_general(
        lax.all_gather(tokens, "row", axis=1, tiled=True),
        qkv_weight,
        (((0,), (0,)), ((), ())),
        preferred_element_type=jnp.float32,
    )
    projected = lax.psum_scatter(
        partial_proj.astype(jnp.bfloat16), "col", scatter_dimension=0, tiled=True
    )
    requests = projected.shape[0] // SLOTS
    projected = projected.reshape(requests, SLOTS, heads_here, 2 * FEAT + HD)
    queries = projected[..., :FEAT]
    keys_now = projected[..., FEAT : 2 * FEAT]
    values_now = projected[..., 2 * FEAT :]
    pref_here = prefix_keys.shape[0]
    plen_here = prefix_keys.shape[2]
    feats_cached = feature_columns(
        prefix_keys.reshape(pref_here, heads_here, FEAT, plen_here).astype(jnp.float32)
    )
    values_cached = prefix_values.reshape(pref_here, heads_here, HD, plen_here)
    partial_state = jnp.einsum(
        "phet,phvt->phev", feats_cached, values_cached, preferred_element_type=jnp.float32
    )
    summed_state = lax.psum(partial_state.astype(jnp.bfloat16), "col").astype(jnp.float32)
    states = lax.all_gather(summed_state.astype(jnp.bfloat16), "req", axis=0, tiled=True).astype(
        summed_state.dtype
    )
    prefixes = states.shape[0]
    selector = (prefix_owner[:, None] == jnp.arange(prefixes, dtype=jnp.int32)[None, :]).astype(
        jnp.float32
    )
    chosen = jnp.einsum("rp,phev->rhev", selector, states, precision=lax.Precision.HIGHEST)
    feats_query = feature_map(queries.astype(jnp.float32)).astype(jnp.float32)
    carried = jnp.einsum("rthe,rhev->rthv", feats_query, chosen, precision=lax.Precision.HIGHEST)
    scores = jnp.einsum("rthf,rshf->rhts", queries, keys_now, preferred_element_type=jnp.float32)
    weights = 1.0 + scores * FEAT ** (-0.5) + scores * scores * (0.5 / FEAT)
    positions = jnp.arange(SLOTS, dtype=jnp.int32)
    allowed = (positions[None, None, :] <= positions[None, :, None]) & (
        positions[None, None, :] < suffix_len[:, None, None]
    )
    weights = jnp.where(allowed[:, None], weights, 0.0).astype(jnp.bfloat16)
    within = jnp.einsum("rhts,rshv->rthv", weights, values_now, preferred_element_type=jnp.float32)
    active = (positions[None, :] < suffix_len[:, None])[:, :, None, None]
    attended = jnp.where(active, carried + within, 0.0)
    inverse_rms = lax.rsqrt(jnp.mean(attended * attended, axis=-1, keepdims=True) + epsilon)
    gains = head_gain.reshape(heads_here, HD)
    normed = (
        (attended * inverse_rms * gains)
        .astype(jnp.bfloat16)
        .reshape(requests * SLOTS, heads_here * HD)
    )
    out_terms = lax.dot_general(
        out_weight,
        lax.all_gather(normed, "col", axis=0, tiled=True),
        (((0,), (1,)), ((), ())),
        preferred_element_type=jnp.float32,
    )
    mixed_sums = lax.psum_scatter(
        out_terms.astype(jnp.bfloat16), "row", scatter_dimension=1, tiled=True
    ).astype(jnp.float32)
    return (tokens.astype(jnp.float32) + mixed_sums).astype(jnp.bfloat16)


def solution(mesh):
    in_specs = (
        P("col", ("req", "row")),
        P("col", "row"),
        P("row", "col"),
        P("row"),
        P("req", "row", "col"),
        P("req", "row", "col"),
        P(("req", "col")),
        P(("req", "col")),
    )
    out_specs = P("col", ("req", "row"))
    return jax.shard_map(shards, mesh=mesh, in_specs=in_specs, out_specs=out_specs, check_vma=False)
```

profile of v0, /device:TPU:1, one launch (start us, length us, event | category | flops | bytes accessed | tf_op | source)
XLA Modules:
  0.0 531.5 jit_solution(16961379070519875924)
XLA Ops:
  7.4 0.0 copy-start
  7.4 0.0 all-reduce.2.cloned.1.call-start
  7.4 1.1 convert.24
  8.4 1.0 multiply_convert_fusion.3
  9.4 0.9 multiply_convert_fusion
  10.3 0.0 copy-done
  10.3 0.0 copy-start.2
  10.3 1.3 fusion.1
  11.7 1.1 copy.20
  12.7 0.0 all-reduce.2.cloned.1.call-update
  12.8 0.0 all-gather.6.cloned.1.call-start
  12.8 0.5 all-gather.6.cloned.1.call-update
  13.3 0.0 all-gather.4.cloned.1.call-start
  13.4 175.5 %all-reduce.2.cloned.1.call-done = bf16[3,2,273,112]{3,1,2,0:T(2,128)(2,1)} async-done(((bf16[3,2,273,112]{3,1,2,0:T(2,128)(2,1)}), bf16[3,2,273,112]{3,1,2,0:T(2,128)(2,1)}) %all-reduce.2.cloned.1.call-update) | async-done | bytes 366928 | tf_op jit(solution)/shard_map/psum | solution.py:64
  188.9 0.0 all-gather.4.cloned.1.call-update
  188.9 0.0 reduce-scatter.3.cloned.1.call-start
  188.9 0.0 all-gather.6.cloned.1.call-done
  189.0 0.0 copy-done.2
  189.0 3.7 convolution_convert_fusion
  192.7 0.0 copy-start.4
  192.7 0.0 reduce-scatter.3.cloned.1.call-update
  192.7 0.0 all-gather.8.cloned.1.call-start
  194.1 0.0 copy-done.4
  194.1 0.1 mul.133
  194.2 0.1 fusion.17
  194.2 134.1 %all-gather.4.cloned.1.call-done = bf16[24,2,273,112]{3,1,2,0:T(2,128)(2,1)} async-done(((bf16[3,2,273,112]{3,1,2,0:T(2,128)(2,1)}), bf16[24,2,273,112]{3,1,2,0:T(2,128)(2,1)}) %all-gather.4.cloned.1.call-update) | async-done | bytes 2935312 | tf_op jit(solution)/shard_map/all_gather | solution.py:65
  328.3 2.7 fusion.6
  331.0 48.0 %reduce-scatter.3.cloned.1.call-done = bf16[512,288]{0,1:T(8,128)(2,1)} async-done(((bf16[4096,288]{0,1:T(8,128)(2,1)}), bf16[512,288]{0,1:T(8,128)(2,1)}) %reduce-scatter.3.cloned.1.call-update) | async-done | bytes 294928 | tf_op jit(solution)/shard_map/reduce_scatter | solution.py:47
  379.0 0.8 convert_bitcast_fusion
  379.7 0.8 fusion.27
  380.5 1.9 fusion.9
  382.4 0.0 copy-start.3
  382.4 0.1 multiply_convert_fusion.1
  382.6 0.8 multiply_reduce_fusion
  383.4 0.8 multiply_convert_fusion.2
  384.2 0.0 all-gather.8.cloned.1.call-update
  384.2 0.0 copy-start.1
  384.2 0.0 reduce-scatter.5.cloned.1.call-start
  384.3 97.4 %all-gather.8.cloned.1.call-done = bf16[4096,224]{0,1:T(8,128)(2,1)} async-done(((bf16[512,224]{0,1:T(8,128)(2,1)}), bf16[4096,224]{0,1:T(8,128)(2,1)}) %all-gather.8.cloned.1.call-update) | async-done | bytes 1835024 | tf_op jit(solution)/shard_map/all_gather | solution.py:94
  481.7 0.0 copy-done.3
  481.7 3.4 fusion
  485.1 0.0 reduce-scatter.5.cloned.1.call-update
  485.2 37.3 %reduce-scatter.5.cloned.1.call-done = bf16[224,512]{1,0:T(8,128)(2,1)} async-done(((bf16[224,4096]{1,0:T(8,128)(2,1)}), bf16[224,512]{1,0:T(8,128)(2,1)}) %reduce-scatter.5.cloned.1.call-update) | async-done | bytes 229392 | tf_op jit(solution)/shard_map/reduce_scatter | solution.py:98
  522.4 0.0 copy-done.1
  522.4 1.7 add_convert_fusion
  (3 shorter events, 0.0 us)
Async XLA Ops:
  7.4 3.0 copy-start
  7.4 181.5 %all-reduce.2.cloned.1.call-start = ((), (), s32[]{:S(2)}) async-start(), calls=%async_computation.2 | async-start | bytes 838656 | tf_op jit(solution)/shard_map/psum | solution.py:64
  10.3 178.7 %copy-start.2 = (bf16[224,288]{0,1:T(8,128)(2,1)S(1)}, bf16[224,288]{0,1:T(8,128)(2,1)}, u32[]{:S(2)}) copy-start(bf16[224,288]{0,1:T(8,128)(2,1)} %param.9) | copy-start | bytes 387076
  12.8 176.2 %all-gather.6.cloned.1.call-start = ((), (), s32[]{:S(2)}) async-start(), calls=%async_computation.4 | async-start | bytes 2064384 | tf_op jit(solution)/shard_map/all_gather | solution.py:42
  13.3 315.0 %all-gather.4.cloned.1.call-start = ((), (), s32[]{:S(2)}) async-start(), calls=%async_computation.3 | async-start | bytes 3773952 | tf_op jit(solution)/shard_map/all_gather | solution.py:65
  188.9 190.1 %reduce-scatter.3.cloned.1.call-start = ((), (), s32[]{:S(2)}) async-start(), calls=%async_computation.5 | async-start | bytes 2654208 | tf_op jit(solution)/shard_map/reduce_scatter | solution.py:47
  192.7 1.4 copy-start.4
  192.7 289.0 %all-gather.8.cloned.1.call-start = ((), (), s32[]{:S(2)}) async-start(), calls=%async_computation.6 | async-start | bytes 2064384 | tf_op jit(solution)/shard_map/all_gather | solution.py:94
  382.4 99.3 %copy-start.3 = (bf16[224,224]{1,0:T(8,128)(2,1)S(1)}, bf16[224,224]{1,0:T(8,128)(2,1)}, u32[]{:S(2)}) copy-start(bf16[224,224]{1,0:T(8,128)(2,1)} %param.10) | copy-start | bytes 301060
  384.2 138.2 %copy-start.1 = (bf16[224,512]{1,0:T(8,128)(2,1)S(1)}, bf16[224,512]{1,0:T(8,128)(2,1)}, u32[]{:S(2)}) copy-start(bf16[224,512]{1,0:T(8,128)(2,1)} %param.8) | copy-start | bytes 688132
  384.2 138.2 %reduce-scatter.5.cloned.1.call-start = ((), (), s32[]{:S(2)}) async-start(), calls=%async_computation.7 | async-start | bytes 2064384 | tf_op jit(solution)/shard_map/reduce_scatter | solution.py:98
Sparse Core Ops, SparseCore 0:
  12.9 175.9 all-reduce.1
  194.4 184.5 reduce-scatter.2
  384.3 97.3 all-gather.7
Sparse Core Ops, SparseCore 1:
  15.4 38.0 all-gather.5
  189.0 139.3 all-gather.3
  485.2 37.1 reduce-scatter.4
where the time goes:
time: 533 us; the launch traced here: 531 us
  waiting for transfers between devices  493 us (92%)
  between operations  16.2 us (3%)
  matrix products  13.9 us (3%)
  other arithmetic  7.12 us (1%)
    psum x1, waiting for transfers between devices, shards(): lax.psum(partial_state.astype(jnp.bfloat16), 'col').astype(jnp.float32)  175 us
    all_gather x1, waiting for transfers between devices, shards(): lax.all_gather(summed_state.astype(jnp.bfloat16), 'req', axis=0, tiled=True)  134 us
    all_gather x1, waiting for transfers between devices, shards(): lax.all_gather(normed, 'col', axis=0, tiled=True)  97.4 us
    reduce_scatter x1, waiting for transfers between devices, shards(): lax.psum_scatter(partial_proj.astype(jnp.bfloat16), 'col', scatter_dimens...  48 us
    reduce_scatter x1, waiting for transfers between devices, shards(): lax.psum_scatter(out_terms.astype(jnp.bfloat16), 'row', scatter_dimension...  37.3 us
  transfers between devices with their start and end apart: 6, of which 5 were waited for; matrix products, arithmetic and copies ran while one was open for 1% of the time, Pallas kernels for 0%

commit v1 on v0

v1 whole, which is shorter than its diff:
```python
import jax
import jax.numpy as jnp
import numpy as np
from jax import lax
from jax.sharding import Mesh, PartitionSpec as P

FEAT = 16
SLOTS = 512
HD = 112

ROW = ("x", "c")
COL = ("y", "zh")

epsilon = 1e-05


def feature_map(values_in):
    feature_count = values_in.shape[-1]
    squares = (values_in[..., :, None] * values_in[..., None, :]).reshape(
        values_in.shape[:-1] + (feature_count * feature_count,)
    )
    constant = jnp.ones(values_in.shape[:-1] + (1,), jnp.float32)
    linear = values_in * feature_count ** (-0.25)
    quadratic = squares * (0.5**0.5 / feature_count**0.5)
    return jnp.concatenate([constant, linear, quadratic], axis=-1).astype(jnp.bfloat16)


def feature_columns(values_in):
    feature_count = values_in.shape[-2]
    length = values_in.shape[-1]
    squares = (values_in[..., :, None, :] * values_in[..., None, :, :]).reshape(
        values_in.shape[:-2] + (feature_count * feature_count, length)
    )
    constant = jnp.ones(values_in.shape[:-2] + (1, length), jnp.float32)
    linear = values_in * feature_count ** (-0.25)
    quadratic = squares * (0.5**0.5 / feature_count**0.5)
    return jnp.concatenate([constant, linear, quadratic], axis=-2).astype(jnp.bfloat16)


def shards(
    tokens, qkv_weight, out_weight, head_gain, prefix_keys, prefix_values, suffix_len, prefix_owner
):
    n_col = lax.psum(1, COL)
    heads_here = head_gain.shape[0] // HD
    partial_proj = lax.dot_general(
        lax.all_gather(tokens, ROW, axis=1, tiled=True),
        qkv_weight,
        (((0,), (0,)), ((), ())),
        preferred_element_type=jnp.float32,
    ).astype(jnp.bfloat16)
    projected = lax.psum_scatter(partial_proj, "y", scatter_dimension=0, tiled=True)
    projected = lax.psum_scatter(projected, "zh", scatter_dimension=0, tiled=True)
    projected = projected.reshape(SLOTS, heads_here, 2 * FEAT + HD)
    queries = projected[..., :FEAT]
    keys_now = projected[..., FEAT : 2 * FEAT]
    values_now = projected[..., 2 * FEAT :]

    pref_here = prefix_keys.shape[0]
    plen_here = prefix_keys.shape[2]
    feats_cached = feature_columns(
        prefix_keys.reshape(pref_here, heads_here, FEAT, plen_here).astype(jnp.float32)
    )
    values_cached = prefix_values.reshape(pref_here, heads_here, HD, plen_here)
    partial_state = jnp.einsum(
        "phet,phvt->phev", feats_cached, values_cached, preferred_element_type=jnp.float32
    )
    state_shape = partial_state.shape[1:]
    piece = partial_state[0].size // n_col
    pieces = partial_state.astype(jnp.bfloat16).reshape(pref_here, n_col, piece)
    pieces = jnp.swapaxes(pieces, 0, 1)
    pieces = lax.psum_scatter(pieces, "y", scatter_dimension=0, tiled=True)
    pieces = lax.psum_scatter(pieces, "zh", scatter_dimension=0, tiled=True)
    pieces = lax.all_gather(pieces[0], "req", axis=0, tiled=True)
    owners = lax.all_gather(prefix_owner, COL, axis=0, tiled=True)
    to_send = jnp.take(pieces, owners, axis=0)
    chosen = lax.all_to_all(to_send, COL, 0, 0, tiled=True)
    chosen = chosen.reshape(state_shape).astype(jnp.float32)

    feats_query = feature_map(queries.astype(jnp.float32)).astype(jnp.float32)
    carried = jnp.einsum("the,hev->thv", feats_query, chosen, precision=lax.Precision.HIGHEST)
    scores = jnp.einsum("thf,shf->hts", queries, keys_now, preferred_element_type=jnp.float32)
    weights = 1.0 + scores * FEAT ** (-0.5) + scores * scores * (0.5 / FEAT)
    positions = jnp.arange(SLOTS, dtype=jnp.int32)
    length = suffix_len[0]
    allowed = (positions[None, :] <= positions[:, None]) & (positions[None, :] < length)
    weights = jnp.where(allowed[None], weights, 0.0).astype(jnp.bfloat16)
    within = jnp.einsum("hts,shv->thv", weights, values_now, preferred_element_type=jnp.float32)
    active = (positions < length)[:, None, None]
    attended = jnp.where(active, carried + within, 0.0)
    inverse_rms = lax.rsqrt(jnp.mean(attended * attended, axis=-1, keepdims=True) + epsilon)
    gains = head_gain.reshape(heads_here, HD)
    normed = (attended * inverse_rms * gains).astype(jnp.bfloat16).reshape(SLOTS, heads_here * HD)
    gathered = lax.all_gather(normed, "zh", axis=0, tiled=True)
    gathered = lax.all_gather(gathered, "y", axis=0, tiled=True)
    out_terms = lax.dot_general(
        out_weight,
        gathered,
        (((0,), (1,)), ((), ())),
        preferred_element_type=jnp.float32,
    )
    mixed_sums = lax.psum_scatter(
        out_terms.astype(jnp.bfloat16), ROW, scatter_dimension=1, tiled=True
    ).astype(jnp.float32)
    return (tokens.astype(jnp.float32) + mixed_sums).astype(jnp.bfloat16)


def solution(mesh):
    n_req, n_row, n_col = (mesh.shape[a] for a in ("req", "row", "col"))
    fine = Mesh(
        np.asarray(mesh.devices).reshape(n_req, n_row // 2, 2, n_col // 2, 2),
        ("req", "x", "c", "y", "zh"),
    )
    in_specs = (
        P(COL, ("req",) + ROW),
        P(COL, ROW),
        P(ROW, COL),
        P(ROW),
        P("req", ROW, COL),
        P("req", ROW, COL),
        P(("req",) + COL),
        P(("req",) + COL),
    )
    out_specs = P(COL, ("req",) + ROW)
    return jax.shard_map(shards, mesh=fine, in_specs=in_specs, out_specs=out_specs, check_vma=False)
```

time: 533 us -> 353 us (0.66)
  waiting for transfers between devices: 493 us -> 210 us
  blocking collectives: 0 us -> 87.2 us
  local copies, waits for them, and re-layouts: 1.19 us -> 12.2 us
  starting transfers between devices: 0.21 us -> 7.21 us
    all_gather x3 -> x2, waiting for transfers between devices: 232 us -> 30.7 us  [the longest x1 30.7 us: shards(): gathered = lax.all_gather(gathered, 'y', axis=0, tiled=True)]
    psum x1 -> x0, waiting for transfers between devices: 175 us -> none  [shards(): lax.psum(partial_state.astype(jnp.bfloat16), 'col').astype(jnp.float32)]
    unnamed x6 -> x9, waiting for transfers between devices: 0.6 us -> 96 us
    all_gather x0 -> x2, blocking collectives: none -> 69.9 us  [the longest x1 42 us: shards(): pieces = lax.all_gather(pieces[0], 'req', axis=0, tiled=True)]
    unnamed x0 -> x1, blocking collectives: none -> 17.3 us
    reduce_scatter x2 -> x3, waiting for transfers between devices: 85.2 us -> 69.6 us  [the longest x1 39.6 us: shards(): lax.psum_scatter(out_terms.astype(jnp.bfloat16), ROW, scatter_dimension=1...]
    all_to_all x0 -> x1, waiting for transfers between devices: none -> 13.4 us  [shards(): chosen = lax.all_to_all(to_send, COL, 0, 0, tiled=True)]
    unnamed x10 -> x20, local copies, waits for them, and re-layouts: 0.03 us -> 8.69 us
  transfers between devices with their start and end apart: 6 -> 8, of which waited for: 5 -> 6; matrix products, arithmetic and copies ran while one was open for 1% -> 4% of each run, Pallas kernels for 0% -> 0%
where the time goes in v1:
time: 353 us; the launch traced here: 352 us
  waiting for transfers between devices  210 us (59%)
  blocking collectives  87.2 us (25%)
  between operations  16.7 us (5%)
  local copies, waits for them, and re-layouts  12.2 us (3%)
  matrix products  10.8 us (3%)
  other arithmetic  7.93 us (2%)
  starting transfers between devices  7.21 us (2%)
    unnamed x9, waiting for transfers between devices  96 us
    all_gather x1, blocking collectives, shards(): pieces = lax.all_gather(pieces[0], 'req', axis=0, tiled=True)  42 us
    reduce_scatter x1, waiting for transfers between devices, shards(): lax.psum_scatter(out_terms.astype(jnp.bfloat16), ROW, scatter_dimension=1...  39.6 us
    all_gather x1, waiting for transfers between devices, shards(): gathered = lax.all_gather(gathered, 'y', axis=0, tiled=True)  30.7 us
    reduce_scatter x1, waiting for transfers between devices, shards(): lax.psum_scatter(projected, 'zh', scatter_dimension=0, tiled=True)  29.9 us
    all_gather x1, blocking collectives, shards(): gathered = lax.all_gather(normed, 'zh', axis=0, tiled=True)  27.8 us
    unnamed x1, blocking collectives  17.3 us
    all_to_all x1, waiting for transfers between devices, shards(): chosen = lax.all_to_all(to_send, COL, 0, 0, tiled=True)  13.4 us
  transfers between devices with their start and end apart: 8, of which 6 were waited for; matrix products, arithmetic and copies ran while one was open for 4% of the time, Pallas kernels for 0%

profile of v1, /device:TPU:1, one launch (start us, length us, event | category | flops | bytes accessed | tf_op | source)
XLA Modules:
  0.0 351.7 jit_solution(18403591849002129596)
XLA Ops:
  7.4 1.1 convert.23
  8.4 1.0 multiply_convert_fusion.3
  9.4 0.9 multiply_convert_fusion
  10.3 1.3 fusion.8
  11.7 0.9 reshape.122
  12.6 1.1 copy.14
  13.7 0.0 all-gather.4.cloned.1.call-start
  13.7 0.5 all-gather.4.cloned.1.call-update
  14.2 0.0 all-reduce.8.cloned.1.call-start
  14.3 1.3 dynamic-slice.1
  16.2 59.1 %all-reduce.6.cloned.1.call-done = bf16[8,3,7644]{2,1,0:T(4,128)(2,1)} async-done(((bf16[8,3,7644]{2,1,0:T(4,128)(2,1)}), bf16[8,3,7644]{2,1,0:T(4,128)(2,1)}) %all-reduce.6.cloned.1.call-update) | async-done | bytes 366928
  75.3 1.6 constant_dynamic-slice_fusion.1
  77.0 0.0 reduce-scatter.4.cloned.1.call-start
  77.0 3.7 %convolution_convert_fusion = bf16[4096,288]{0,1:T(8,128)(2,1)} fusion(bf16[224,288]{0,1:T(8,128)(2,1)S(1)} %copy-done.2, bf16[224,4096]{1,0:T(8,128)(2,1)} %all-gather.4.cloned.1.call-done), kind=kOutput, calls=%fused_computation.2 | convolution fusion | flops 529661952 | bytes 4323328 | tf_op jit(solution)/shard_map/dot_general | solution.py:45
  80.8 0.0 reduce-scatter.6.cloned.1.call-start
  81.5 1.3 dynamic-slice
  82.7 0.7 dynamic-update-slice
  83.5 17.3 %all-reduce = s32[8]{0:T(128)S(1)} all-reduce(s32[8]{0:T(128)S(1)} %dynamic-update-slice), channel_id=1, replica_groups=mesh['req'=8,'x'=4,'c'=2,'y'=4,'zh'=2] {'y','zh'}, use_global_device_ids=true, to_apply=%add | all-reduce | flops 8 | bytes 64
  100.8 1.3 dynamic-slice.3
  102.1 36.2 %all-reduce.8.cloned.1.call-done = bf16[2,3,7644]{2,1,0:T(4,128)(2,1)} async-done(((bf16[2,3,7644]{2,1,0:T(4,128)(2,1)}), bf16[2,3,7644]{2,1,0:T(4,128)(2,1)}) %all-reduce.8.cloned.1.call-update) | async-done | bytes 91744
  138.3 1.5 constant_dynamic-slice_fusion
  139.8 0.1 copy.15
  139.9 42.0 %all-gather = bf16[1,24,7644]{2,0,1:T(2,128)(2,1)S(1)} all-gather(bf16[1,3,7644]{2,0,1:T(2,128)(2,1)S(1)} %copy.15), channel_id=2, replica_groups=mesh['req'=8,'x'=4,'c'=2,'y'=4,'zh'=2] {'req'}, dimensions={1}, use_global_device_ids=true | all-gather | bytes 412776 | tf_op jit(solution)/shard_map/all_gather | solution.py:73
  182.0 0.6 gather_fusion
  182.6 0.1 bitcast_select_fusion
  182.7 0.5 broadcast.109
  183.2 0.7 reduce.1
  183.9 0.8 reshape.147
  184.7 7.0 %all-to-all-start = ((bf16[8,2,3822]{2,1,0:T(2,128)(2,1)}), bf16[8,2,3822]{2,1,0:T(2,128)(2,1)S(1)}, u32[]{:S(2)}, u32[]{:S(2)}) async-start(bf16[8,2,3822]{2,1,0:T(2,128)(2,1)} %reshape.147), calls=%async_computation | async-start | bytes 245760 | tf_op jit(solution)/shard_map/all_to_all | solution.py:76
  192.4 0.1 mul.120
  192.5 0.1 fusion.17
  192.6 13.4 %all-to-all-done = bf16[8,2,3822]{2,1,0:T(2,128)(2,1)S(1)} async-done(((bf16[8,2,3822]{2,1,0:T(2,128)(2,1)}), bf16[8,2,3822]{2,1,0:T(2,128)(2,1)S(1)}, u32[]{:S(2)}, u32[]{:S(2)}) %all-to-all-start) | async-done | bytes 122336 | tf_op jit(solution)/shard_map/all_to_all | solution.py:76
  205.9 0.2 reshape.148
  206.1 0.7 reduce
  206.8 0.3 reshape.123
  207.1 29.9 %reduce-scatter.6.cloned.1.call-done = bf16[512,288]{0,1:T(8,128)(2,1)} async-done(((bf16[1024,288]{0,1:T(8,128)(2,1)}), bf16[512,288]{0,1:T(8,128)(2,1)}) %reduce-scatter.6.cloned.1.call-update) | async-done | bytes 294928 | tf_op jit(solution)/shard_map/reduce_scatter | solution.py:52
  237.0 0.8 slice_convert_fusion
  237.8 0.8 multiply_convert_fusion.4
  238.5 1.9 fusion.7
  240.5 0.1 multiply_convert_fusion.1
  240.6 0.5 multiply_reduce_fusion
  241.1 0.1 multiply_convert_fusion.2
  241.2 27.8 %all_gather.18 = bf16[1024,224]{0,1:T(8,128)(2,1)} all-gather(bf16[512,224]{0,1:T(8,128)(2,1)S(1)} %bitcast.34), channel_id=1, replica_groups=mesh['req'=8,'x'=4,'c'=2,'y'=4,'zh'=2] {'zh'}, dimensions={0}, use_global_device_ids=true | all-gather | bytes 688128 | tf_op jit(solution)/shard_map/all_gather | solution.py:93
  269.1 0.0 reduce-scatter.8.cloned.1.call-start
  269.1 30.7 %all-gather.6.cloned.1.call-done = bf16[4096,224]{0,1:T(8,128)(2,1)} async-done(((bf16[1024,224]{0,1:T(8,128)(2,1)}), bf16[4096,224]{0,1:T(8,128)(2,1)}) %all-gather.6.cloned.1.call-update) | async-done | bytes 1835024 | tf_op jit(solution)/shard_map/all_gather | solution.py:94
  299.8 3.4 fusion
  303.3 39.6 %reduce-scatter.8.cloned.1.call-done = bf16[224,512]{1,0:T(8,128)(2,1)} async-done(((bf16[224,4096]{1,0:T(8,128)(2,1)}), bf16[224,512]{1,0:T(8,128)(2,1)}) %reduce-scatter.8.cloned.1.call-update) | async-done | bytes 229392 | tf_op jit(solution)/shard_map/reduce_scatter | solution.py:101
  342.9 1.7 add_convert_fusion
  (28 shorter events, 0.3 us)
Async XLA Ops:
  7.4 3.0 copy-start
  7.4 68.0 %all-reduce.6.cloned.1.call-start = ((), (), s32[]{:S(2)}) async-start(), calls=%async_computation.9 | async-start | bytes 983040
  11.6 65.4 %copy-start.2 = (bf16[224,288]{0,1:T(8,128)(2,1)S(1)}, bf16[224,288]{0,1:T(8,128)(2,1)}, u32[]{:S(2)}) copy-start(bf16[224,288]{0,1:T(8,128)(2,1)} %param.9) | copy-start | bytes 387076
  13.7 63.4 %all-gather.4.cloned.1.call-start = ((), (), s32[]{:S(2)}) async-start(), calls=%async_computation.4 | async-start | bytes 2064384 | tf_op jit(solution)/shard_map/all_gather | solution.py:46
  14.2 124.1 %all-reduce.8.cloned.1.call-start = ((), (), s32[]{:S(2)}) async-start(), calls=%async_computation.10 | async-start | bytes 245760
  77.0 105.6 %reduce-scatter.4.cloned.1.call-start = ((), (), s32[]{:S(2)}) async-start(), calls=%async_computation.5 | async-start | bytes 2949120 | tf_op jit(solution)/shard_map/reduce_scatter | solution.py:51
  80.8 156.2 %reduce-scatter.6.cloned.1.call-start = ((), (), s32[]{:S(2)}) async-start(), calls=%async_computation.6 | async-start | bytes 884736 | tf_op jit(solution)/shard_map/reduce_scatter | solution.py:52
  181.9 10.5 %copy-start.4 = (f32[224]{0:T(256)S(1)}, f32[224]{0:T(256)}, u32[]{:S(2)}) copy-start(f32[224]{0:T(256)} %param.11) | copy-start | bytes 2692
  184.7 21.2 %all-to-all-start = ((bf16[8,2,3822]{2,1,0:T(2,128)(2,1)}), bf16[8,2,3822]{2,1,0:T(2,128)(2,1)S(1)}, u32[]{:S(2)}, u32[]{:S(2)}) async-start(bf16[8,2,3822]{2,1,0:T(2,128)(2,1)} %reshape.147), calls=%async_computation | async-start | bytes 245760 | tf_op jit(solution)/shard_map/all_to_all | solution.py:76
  191.7 108.1 %all-gather.6.cloned.1.call-start = ((), (), s32[]{:S(2)}) async-start(), calls=%async_computation.7 | async-start | bytes 2293760 | tf_op jit(solution)/shard_map/all_gather | solution.py:94
  240.5 59.4 %copy-start.3 = (bf16[224,224]{1,0:T(8,128)(2,1)S(1)}, bf16[224,224]{1,0:T(8,128)(2,1)}, u32[]{:S(2)}) copy-start(bf16[224,224]{1,0:T(8,128)(2,1)} %param.10) | copy-start | bytes 301060
  269.1 73.9 %copy-start.1 = (bf16[224,512]{1,0:T(8,128)(2,1)S(1)}, bf16[224,512]{1,0:T(8,128)(2,1)}, u32[]{:S(2)}) copy-start(bf16[224,512]{1,0:T(8,128)(2,1)} %param.8) | copy-start | bytes 688132
  269.1 73.9 %reduce-scatter.8.cloned.1.call-start = ((), (), s32[]{:S(2)}) async-start(), calls=%async_computation.8 | async-start | bytes 2064384 | tf_op jit(solution)/shard_map/reduce_scatter | solution.py:101
Sparse Core Ops, SparseCore 0:
  13.8 61.5 all-reduce.5
  78.2 60.0 all-reduce.7
  141.2 32.5 reduce-scatter.3
  182.8 54.2 reduce-scatter.5
  269.2 30.6 all-gather.5
Sparse Core Ops, SparseCore 1:
  16.3 38.0 all-gather.3
  303.4 39.5 reduce-scatter.7

commit v2 on v1

--- a/solution.py
+++ b/solution.py
@@ -40,20 +40,13 @@
 def shards(
     tokens, qkv_weight, out_weight, head_gain, prefix_keys, prefix_values, suffix_len, prefix_owner
 ):
+    n_row = lax.psum(1, ROW)
     n_col = lax.psum(1, COL)
     heads_here = head_gain.shape[0] // HD
-    partial_proj = lax.dot_general(
-        lax.all_gather(tokens, ROW, axis=1, tiled=True),
-        qkv_weight,
-        (((0,), (0,)), ((), ())),
-        preferred_element_type=jnp.float32,
-    ).astype(jnp.bfloat16)
-    projected = lax.psum_scatter(partial_proj, "y", scatter_dimension=0, tiled=True)
-    projected = lax.psum_scatter(projected, "zh", scatter_dimension=0, tiled=True)
-    projected = projected.reshape(SLOTS, heads_here, 2 * FEAT + HD)
-    queries = projected[..., :FEAT]
-    keys_now = projected[..., FEAT : 2 * FEAT]
-    values_now = projected[..., 2 * FEAT :]
+    row_here = lax.axis_index("x") * 2 + lax.axis_index("c")
+    col_here = lax.axis_index("y") * 2 + lax.axis_index("zh")
+    lens = lax.all_gather(suffix_len, COL, axis=0, tiled=True)
+    owners = lax.all_gather(prefix_owner, COL, axis=0, tiled=True)
 
     pref_here = prefix_keys.shape[0]
     plen_here = prefix_keys.shape[2]
@@ -67,40 +60,50 @@
     state_shape = partial_state.shape[1:]
     piece = partial_state[0].size // n_col
     pieces = partial_state.astype(jnp.bfloat16).reshape(pref_here, n_col, piece)
-    pieces = jnp.swapaxes(pieces, 0, 1)
-    pieces = lax.psum_scatter(pieces, "y", scatter_dimension=0, tiled=True)
-    pieces = lax.psum_scatter(pieces, "zh", scatter_dimension=0, tiled=True)
-    pieces = lax.all_gather(pieces[0], "req", axis=0, tiled=True)
-    owners = lax.all_gather(prefix_owner, COL, axis=0, tiled=True)
+    pieces = lax.all_to_all(jnp.swapaxes(pieces, 0, 1), COL, 0, 0, tiled=True)
+    pieces = jnp.sum(pieces.astype(jnp.float32), axis=0).astype(jnp.bfloat16)
+    pieces = lax.all_gather(pieces, "req", axis=0, tiled=True)
     to_send = jnp.take(pieces, owners, axis=0)
     chosen = lax.all_to_all(to_send, COL, 0, 0, tiled=True)
+    flat = ROW + COL
+    perm = [(i * n_col + j, j * n_col + i) for i in range(n_row) for j in range(n_col)]
+    chosen = lax.ppermute(chosen, flat, perm)
     chosen = chosen.reshape(state_shape).astype(jnp.float32)
+
+    weight_all = lax.all_gather(qkv_weight, ROW, axis=1, tiled=True)
+    partial_proj = lax.dot_general(
+        weight_all, tokens, (((0,), (0,)), ((), ())), preferred_element_type=jnp.float32
+    ).astype(jnp.bfloat16)
+    projected = lax.psum_scatter(partial_proj, "y", scatter_dimension=0, tiled=True)
+    projected = lax.psum_scatter(projected, "zh", scatter_dimension=0, tiled=True)
+    projected = projected.T.reshape(SLOTS, heads_here, 2 * FEAT + HD)
+    queries = projected[..., :FEAT]
+    keys_now = projected[..., FEAT : 2 * FEAT]
+    values_now = projected[..., 2 * FEAT :]
 
     feats_query = feature_map(queries.astype(jnp.float32)).astype(jnp.float32)
     carried = jnp.einsum("the,hev->thv", feats_query, chosen, precision=lax.Precision.HIGHEST)
     scores = jnp.einsum("thf,shf->hts", queries, keys_now, preferred_element_type=jnp.float32)
     weights = 1.0 + scores * FEAT ** (-0.5) + scores * scores * (0.5 / FEAT)
     positions = jnp.arange(SLOTS, dtype=jnp.int32)
-    length = suffix_len[0]
+    length = lens[row_here]
     allowed = (positions[None, :] <= positions[:, None]) & (positions[None, :] < length)
     weights = jnp.where(allowed[None], weights, 0.0).astype(jnp.bfloat16)
     within = jnp.einsum("hts,shv->thv", weights, values_now, preferred_element_type=jnp.float32)
     active = (positions < length)[:, None, None]
     attended = jnp.where(active, carried + within, 0.0)
     inverse_rms = lax.rsqrt(jnp.mean(attended * attended, axis=-1, keepdims=True) + epsilon)
-    gains = head_gain.reshape(heads_here, HD)
+    gains_all = lax.all_gather(head_gain, ROW, axis=0, tiled=True)
+    gains = lax.dynamic_slice_in_dim(gains_all, col_here * heads_here * HD, heads_here * HD)
+    gains = gains.reshape(heads_here, HD)
     normed = (attended * inverse_rms * gains).astype(jnp.bfloat16).reshape(SLOTS, heads_here * HD)
-    gathered = lax.all_gather(normed, "zh", axis=0, tiled=True)
-    gathered = lax.all_gather(gathered, "y", axis=0, tiled=True)
-    out_terms = lax.dot_general(
-        out_weight,
-        gathered,
-        (((0,), (1,)), ((), ())),
-        preferred_element_type=jnp.float32,
-    )
-    mixed_sums = lax.psum_scatter(
-        out_terms.astype(jnp.bfloat16), ROW, scatter_dimension=1, tiled=True
-    ).astype(jnp.float32)
+    hidden = lax.all_gather(normed, "zh", axis=0)
+    hidden = lax.all_gather(hidden, "y", axis=0)
+    hidden = hidden.reshape((n_col,) + normed.shape)
+    out_w = lax.all_gather(out_weight, ROW, axis=0, tiled=True)
+    out_w = out_w.reshape(n_col, heads_here * HD, out_w.shape[1])
+    blocks = jnp.einsum("ktd,kde->ket", hidden, out_w, preferred_element_type=jnp.float32)
+    mixed_sums = jnp.sum(blocks.astype(jnp.bfloat16).astype(jnp.float32), axis=0)
     return (tokens.astype(jnp.float32) + mixed_sums).astype(jnp.bfloat16)
 
 

time: 353 us -> 260 us (0.74)
  waiting for transfers between devices: 210 us -> 36 us
  blocking collectives: 87.2 us -> 154 us
  starting transfers between devices: 7.21 us -> 28.9 us
    unnamed x9 -> x3, waiting for transfers between devices: 96 us -> 0.05 us
    all_gather x2 -> x4, blocking collectives: 69.9 us -> 114 us  [the longest x1 53.6 us: shards(): pieces = lax.all_gather(pieces, 'req', axis=0, tiled=True)]
    reduce_scatter x1 -> x0, waiting for transfers between devices: 39.6 us -> none  [shards(): lax.psum_scatter(out_terms.astype(jnp.bfloat16), ROW, scatter_dimension=1...]
    reduce_scatter x1, waiting for transfers between devices: 29.9 us -> 0.02 us  [shards(): lax.psum_scatter(projected, 'zh', scatter_dimension=0, tiled=True)]
    unnamed x1 -> x2, blocking collectives: 17.3 us -> 39.6 us
    ppermute x0 -> x1, waiting for transfers between devices: none -> 15.2 us  [shards(): chosen = lax.ppermute(chosen, flat, perm)]
    all_to_all x1, waiting for transfers between devices: 13.4 us -> 0.01 us  [shards(): chosen = lax.all_to_all(to_send, COL, 0, 0, tiled=True)]
    ppermute x0 -> x1, starting transfers between devices: none -> 13.3 us  [shards(): chosen = lax.ppermute(chosen, flat, perm)]
  transfers between devices with their start and end apart: 8 -> 6, of which waited for: 6 -> 2; matrix products, arithmetic and copies ran while one was open for 4% -> 5% of each run, Pallas kernels for 0% -> 0%
where the time goes in v2:
time: 260 us; the launch traced here: 259 us
  blocking collectives  154 us (59%)
  waiting for transfers between devices  36 us (14%)
  starting transfers between devices  28.9 us (11%)
  between operations  15.2 us (6%)
  local copies, waits for them, and re-layouts  10.7 us (4%)
  matrix products  9.25 us (4%)
  other arithmetic  5.1 us (2%)
    all_gather x1, blocking collectives, shards(): pieces = lax.all_gather(pieces, 'req', axis=0, tiled=True)  53.6 us
    unnamed x2, blocking collectives  39.6 us
    all_gather x1, blocking collectives, shards(): hidden = lax.all_gather(normed, 'zh', axis=0)  23.9 us
    all_gather x1, blocking collectives, shards(): weight_all = lax.all_gather(qkv_weight, ROW, axis=1, tiled=True)  21.1 us
    all_gather x1, waiting for transfers between devices, shards(): hidden = lax.all_gather(hidden, 'y', axis=0)  20.8 us
    all_gather x1, blocking collectives, shards(): out_w = lax.all_gather(out_weight, ROW, axis=0, tiled=True)  15.9 us
    ppermute x1, waiting for transfers between devices, shards(): chosen = lax.ppermute(chosen, flat, perm)  15.2 us
    ppermute x1, starting transfers between devices, shards(): chosen = lax.ppermute(chosen, flat, perm)  13.3 us
  transfers between devices with their start and end apart: 6, of which 2 were waited for; matrix products, arithmetic and copies ran while one was open for 5% of the time, Pallas kernels for 0%

profile of v2, /device:TPU:1, one launch (start us, length us, event | category | flops | bytes accessed | tf_op | source)
XLA Modules:
  0.0 259.2 jit_solution(13862323276337971894)
XLA Ops:
  6.5 21.1 %all_gather.30 = bf16[224,2304]{0,1:T(8,128)(2,1)S(1)} all-gather(bf16[224,288]{0,1:T(8,128)(2,1)} %param.9), channel_id=1, replica_groups=mesh['req'=8,'x'=4,'c'=2,'y'=4,'zh'=2] {'x','c'}, dimensions={1}, use_global_device_ids=true | all-gather | bytes 1161216 | tf_op jit(solution)/shard_map/all_gather | solution.py:73
  27.6 3.1 %convolution_convert_fusion = bf16[2304,512]{1,0:T(8,128)(2,1)} fusion(bf16[224,2304]{0,1:T(8,128)(2,1)S(1)} %all_gather.30, bf16[224,512]{1,0:T(8,128)(2,1)} %param.8), kind=kOutput, calls=%fused_computation.2 | convolution fusion | flops 529661952 | bytes 3620864 | tf_op jit(solution)/shard_map/dot_general | solution.py:74
  30.8 0.9 copy-done.2
  31.8 0.9 multiply_convert_fusion
  32.7 1.4 fusion.7
  34.1 0.9 reshape.124
  35.0 1.0 copy.15
  36.1 12.1 %all-to-all-start = ((bf16[8,3,7644]{2,1,0:T(4,128)(2,1)}), bf16[8,3,7644]{2,1,0:T(4,128)(2,1)S(1)}, u32[]{:S(2)}, u32[]{:S(2)}) async-start(bf16[8,3,7644]{2,1,0:T(4,128)(2,1)} %copy.15), calls=%async_computation | async-start | bytes 983040 | tf_op jit(solution)/shard_map/all_to_all | solution.py:63
  48.2 0.0 reduce-scatter.5.cloned.1.call-start
  49.6 1.3 dynamic-slice
  50.8 0.8 dynamic-update-slice
  51.6 0.8 dynamic-update-slice.1
  52.3 18.7 %all-reduce.3 = (s32[8]{0:T(128)S(1)}, s32[8]{0:T(128)S(1)}) all-reduce(s32[8]{0:T(128)S(1)} %dynamic-update-slice, s32[8]{0:T(128)S(1)} %dynamic-update-slice.1), channel_id=1, replica_groups=mesh['req'=8,'x'=4,'c'=2,'y'=4,'zh'=2] {'y','zh'}, use_global_device_ids=true, to_apply=%add | all-reduce | flops 16 | bytes 128
  71.1 0.2 reduce_sum.32
  71.4 53.6 %all-gather.1 = bf16[8,3,7644]{2,1,0:T(4,128)(2,1)S(1)} all-gather(bf16[1,3,7644]{2,1,0:T(4,128)(2,1)S(1)} %bitcast.42), channel_id=1, replica_groups=mesh['req'=8,'x'=4,'c'=2,'y'=4,'zh'=2] {'req'}, dimensions={0}, use_global_device_ids=true | all-gather | bytes 412776 | tf_op jit(solution)/shard_map/all_gather | solution.py:65
  124.9 0.3 reshape.151
  125.3 0.6 gather_fusion
  125.9 0.0 reduce-scatter.3.cloned.1.call-done
  125.9 0.1 bitcast_select_fusion
  126.0 0.5 broadcast.110
  126.5 0.7 reduce.2
  127.2 0.8 reshape.160
  128.0 3.4 %all-to-all-start.1 = ((bf16[8,2,3822]{2,1,0:T(2,128)(2,1)}), bf16[8,2,3822]{2,1,0:T(2,128)(2,1)S(1)}, u32[]{:S(2)}, u32[]{:S(2)}) async-start(bf16[8,2,3822]{2,1,0:T(2,128)(2,1)} %reshape.160), calls=%async_computation.1 | async-start | bytes 245760 | tf_op jit(solution)/shard_map/all_to_all | solution.py:67
  131.4 0.0 all-gather.4.cloned.1.call-start
  131.5 1.2 dynamic-slice.2
  133.3 0.3 dynamic-update-slice.2
  133.6 20.8 %all-reduce.2 = f32[1792]{0:T(1024)S(1)} all-reduce(f32[1792]{0:T(1024)S(1)} %dynamic-update-slice.2), channel_id=1, replica_groups=mesh['req'=8,'x'=4,'c'=2,'y'=4,'zh'=2] {'x','c'}, use_global_device_ids=true, to_apply=%add.2 | all-reduce | flops 1792 | bytes 14336
  154.4 0.1 dynamic_slice.7
  154.5 0.1 mul.133
  154.5 0.6 dynamic_slice.6
  155.1 0.5 iota_compare_fusion.1
  155.7 0.2 reshape.161
  155.9 13.3 %collective-permute-start = (bf16[8,7644]{1,0:T(8,128)(2,1)S(1)}, bf16[8,7644]{1,0:T(8,128)(2,1)S(1)}, u32[]{:S(2)}, u32[]{:S(2)}) collective-permute-start(bf16[8,7644]{1,0:T(8,128)(2,1)S(1)} %bitcast.43), channel_id=1, source_target_pairs={{0,0},{1,8},{2,16},{3,24},{4,32},{5,40},{6,48},{7,56},{8,1},{9,9},... | collective-permute-start | bytes 366920 | tf_op jit(solution)/shard_map/ppermute | solution.py:70
  169.2 0.1 fusion.16
  169.3 15.2 %collective-permute-done = bf16[8,7644]{1,0:T(8,128)(2,1)S(1)} collective-permute-done((bf16[8,7644]{1,0:T(8,128)(2,1)S(1)}, bf16[8,7644]{1,0:T(8,128)(2,1)S(1)}, u32[]{:S(2)}, u32[]{:S(2)}) %collective-permute-start) | collective-permute-done | bytes 122336 | tf_op jit(solution)/shard_map/ppermute | solution.py:70
  184.4 0.3 reshape.125
  184.7 0.0 reduce-scatter.5.cloned.1.call-done
  184.7 0.8 slice_convert_fusion
  185.5 0.8 multiply_convert_fusion.4
  186.2 1.9 fusion.6
  188.2 0.1 multiply_convert_fusion.1
  188.3 0.5 multiply_reduce_fusion
  188.8 0.1 multiply_convert_fusion.2
  188.9 23.9 %all_gather.32 = bf16[2,512,224]{1,2,0:T(8,128)(2,1)} all-gather(bf16[1,512,224]{1,2,0:T(8,128)(2,1)S(1)} %bitcast.38), channel_id=1, replica_groups=mesh['req'=8,'x'=4,'c'=2,'y'=4,'zh'=2] {'zh'}, dimensions={0}, use_global_device_ids=true | all-gather | bytes 688128 | tf_op jit(solution)/shard_map/all_gather | solution.py:100
  212.8 15.9 %all_gather.35 = bf16[1792,224]{1,0:T(8,128)(2,1)S(1)} all-gather(bf16[224,224]{1,0:T(8,128)(2,1)S(1)} %copy-done.3), channel_id=1, replica_groups=mesh['req'=8,'x'=4,'c'=2,'y'=4,'zh'=2] {'x','c'}, dimensions={0}, use_global_device_ids=true | all-gather | bytes 903168 | tf_op jit(solution)/shard_map/all_gather | solution.py:103
  228.8 20.8 %all-gather.4.cloned.1.call-done = bf16[8,512,224]{1,2,0:T(8,128)(2,1)} async-done(((bf16[2,512,224]{1,2,0:T(8,128)(2,1)}), bf16[8,512,224]{1,2,0:T(8,128)(2,1)}) %all-gather.4.cloned.1.call-update) | async-done | bytes 1835024 | tf_op jit(solution)/shard_map/all_gather | solution.py:101
  249.6 2.3 convert_reduce_fusion
  251.9 0.8 fusion.22
  (26 shorter events, 0.2 us)
Async XLA Ops:
  6.5 26.2 %copy-start = (bf16[3,224,1024]{2,1,0:T(8,128)(2,1)S(1)}, bf16[3,224,1024]{2,1,0:T(8,128)(2,1)}, u32[]{:S(2)}) copy-start(bf16[3,224,1024]{2,1,0:T(8,128)(2,1)} %param.13) | copy-start | bytes 4128772
  6.5 119.4 %reduce-scatter.3.cloned.1.call-start = ((), (), s32[]{:S(2)}) async-start(), calls=%async_computation.4 | async-start | bytes 2949120 | tf_op jit(solution)/shard_map/reduce_scatter | solution.py:77
  30.8 0.9 copy-start.2
  36.1 35.0 %all-to-all-start = ((bf16[8,3,7644]{2,1,0:T(4,128)(2,1)}), bf16[8,3,7644]{2,1,0:T(4,128)(2,1)S(1)}, u32[]{:S(2)}, u32[]{:S(2)}) async-start(bf16[8,3,7644]{2,1,0:T(4,128)(2,1)} %copy.15), calls=%async_computation | async-start | bytes 983040 | tf_op jit(solution)/shard_map/all_to_all | solution.py:63
  48.2 136.5 %reduce-scatter.5.cloned.1.call-start = ((), (), s32[]{:S(2)}) async-start(), calls=%async_computation.5 | async-start | bytes 884736 | tf_op jit(solution)/shard_map/reduce_scatter | solution.py:78
  71.4 61.9 %copy-start.4 = (f32[224]{0:T(256)S(1)}, f32[224]{0:T(256)}, u32[]{:S(2)}) copy-start(f32[224]{0:T(256)} %param.11) | copy-start | bytes 2692
  128.0 27.6 %all-to-all-start.1 = ((bf16[8,2,3822]{2,1,0:T(2,128)(2,1)}), bf16[8,2,3822]{2,1,0:T(2,128)(2,1)S(1)}, u32[]{:S(2)}, u32[]{:S(2)}) async-start(bf16[8,2,3822]{2,1,0:T(2,128)(2,1)} %reshape.160), calls=%async_computation.1 | async-start | bytes 245760 | tf_op jit(solution)/shard_map/all_to_all | solution.py:67
  131.4 118.2 %all-gather.4.cloned.1.call-start = ((), (), s32[]{:S(2)}) async-start(), calls=%async_computation.6 | async-start | bytes 2293760 | tf_op jit(solution)/shard_map/all_gather | solution.py:101
  155.9 28.5 %collective-permute-start = (bf16[8,7644]{1,0:T(8,128)(2,1)S(1)}, bf16[8,7644]{1,0:T(8,128)(2,1)S(1)}, u32[]{:S(2)}, u32[]{:S(2)}) collective-permute-start(bf16[8,7644]{1,0:T(8,128)(2,1)S(1)} %bitcast.43), channel_id=1, source_target_pairs={{0,0},{1,8},{2,16},{3,24},{4,32},{5,40},{6,48},{7,56},{8,1},{9,9},... | collective-permute-start | bytes 366920 | tf_op jit(solution)/shard_map/ppermute | solution.py:70
  188.1 24.7 %copy-start.3 = (bf16[224,224]{1,0:T(8,128)(2,1)S(1)}, bf16[224,224]{1,0:T(8,128)(2,1)}, u32[]{:S(2)}) copy-start(bf16[224,224]{1,0:T(8,128)(2,1)} %param.10) | copy-start | bytes 301060
  212.8 39.1 %copy-start.1 = (bf16[224,512]{1,0:T(8,128)(2,1)S(1)}, bf16[224,512]{1,0:T(8,128)(2,1)}, u32[]{:S(2)}) copy-start(bf16[224,512]{1,0:T(8,128)(2,1)} %param.8) | copy-start | bytes 688132
Sparse Core Ops, SparseCore 0:
  30.9 43.1 reduce-scatter.2
  126.1 58.1 reduce-scatter.4
  212.9 36.5 all-gather.3

commit v3 on v2

--- a/solution.py
+++ b/solution.py
@@ -37,6 +37,25 @@
     return jnp.concatenate([constant, linear, quadratic], axis=-2).astype(jnp.bfloat16)
 
 
+def gather_by_shifts(x, axis, n):
+    me = lax.axis_index(axis)
+    got = [x] + [lax.ppermute(x, axis, [(i, (i + k) % n) for i in range(n)]) for k in range(1, n)]
+    stacked = jnp.stack(got)
+    return jnp.take(stacked, (me - jnp.arange(n)) % n, axis=0)
+
+
+def reduce_scatter_by_shifts(x, axis, n):
+    me = lax.axis_index(axis)
+    m = x.shape[0] // n
+    total = lax.dynamic_slice_in_dim(x, me * m, m).astype(jnp.float32)
+    for k in range(1, n):
+        part = lax.dynamic_slice_in_dim(x, ((me + k) % n) * m, m)
+        total = total + lax.ppermute(part, axis, [(i, (i + k) % n) for i in range(n)]).astype(
+            jnp.float32
+        )
+    return total
+
+
 def shards(
     tokens, qkv_weight, out_weight, head_gain, prefix_keys, prefix_values, suffix_len, prefix_owner
 ):
@@ -45,8 +64,13 @@
     heads_here = head_gain.shape[0] // HD
     row_here = lax.axis_index("x") * 2 + lax.axis_index("c")
     col_here = lax.axis_index("y") * 2 + lax.axis_index("zh")
-    lens = lax.all_gather(suffix_len, COL, axis=0, tiled=True)
-    owners = lax.all_gather(prefix_owner, COL, axis=0, tiled=True)
+    meta = jnp.concatenate([suffix_len, prefix_owner])
+    meta = gather_by_shifts(gather_by_shifts(meta, "zh", 2), "y", n_col // 2)
+    meta = meta.reshape(n_col, 2)
+    lens = meta[:, 0]
+    owners = meta[:, 1]
+    flat = ROW + COL
+    perm = [(i * n_col + j, j * n_col + i) for i in range(n_row) for j in range(n_col)]
 
     pref_here = prefix_keys.shape[0]
     plen_here = prefix_keys.shape[2]
@@ -62,20 +86,21 @@
     pieces = partial_state.astype(jnp.bfloat16).reshape(pref_here, n_col, piece)
     pieces = lax.all_to_all(jnp.swapaxes(pieces, 0, 1), COL, 0, 0, tiled=True)
     pieces = jnp.sum(pieces.astype(jnp.float32), axis=0).astype(jnp.bfloat16)
-    pieces = lax.all_gather(pieces, "req", axis=0, tiled=True)
+    pieces = gather_by_shifts(pieces, "req", lax.psum(1, "req"))
+    pieces = pieces.reshape((-1, piece))
     to_send = jnp.take(pieces, owners, axis=0)
     chosen = lax.all_to_all(to_send, COL, 0, 0, tiled=True)
-    flat = ROW + COL
-    perm = [(i * n_col + j, j * n_col + i) for i in range(n_row) for j in range(n_col)]
     chosen = lax.ppermute(chosen, flat, perm)
     chosen = chosen.reshape(state_shape).astype(jnp.float32)
 
-    weight_all = lax.all_gather(qkv_weight, ROW, axis=1, tiled=True)
-    partial_proj = lax.dot_general(
-        weight_all, tokens, (((0,), (0,)), ((), ())), preferred_element_type=jnp.float32
+    weight_all = gather_by_shifts(gather_by_shifts(qkv_weight, "c", 2), "x", n_row // 2)
+    weight_all = weight_all.reshape((n_row,) + qkv_weight.shape)
+    partial_proj = jnp.einsum(
+        "kdj,dt->kjt", weight_all, tokens, preferred_element_type=jnp.float32
     ).astype(jnp.bfloat16)
-    projected = lax.psum_scatter(partial_proj, "y", scatter_dimension=0, tiled=True)
-    projected = lax.psum_scatter(projected, "zh", scatter_dimension=0, tiled=True)
+    partial_proj = partial_proj.reshape(-1, tokens.shape[1])
+    projected = reduce_scatter_by_shifts(partial_proj, "y", n_col // 2).astype(jnp.bfloat16)
+    projected = reduce_scatter_by_shifts(projected, "zh", 2).astype(jnp.bfloat16)
     projected = projected.T.reshape(SLOTS, heads_here, 2 * FEAT + HD)
     queries = projected[..., :FEAT]
     keys_now = projected[..., FEAT : 2 * FEAT]
@@ -93,15 +118,12 @@
     active = (positions < length)[:, None, None]
     attended = jnp.where(active, carried + within, 0.0)
     inverse_rms = lax.rsqrt(jnp.mean(attended * attended, axis=-1, keepdims=True) + epsilon)
-    gains_all = lax.all_gather(head_gain, ROW, axis=0, tiled=True)
-    gains = lax.dynamic_slice_in_dim(gains_all, col_here * heads_here * HD, heads_here * HD)
-    gains = gains.reshape(heads_here, HD)
+    gains = lax.ppermute(head_gain, flat, perm).reshape(heads_here, HD)
     normed = (attended * inverse_rms * gains).astype(jnp.bfloat16).reshape(SLOTS, heads_here * HD)
-    hidden = lax.all_gather(normed, "zh", axis=0)
-    hidden = lax.all_gather(hidden, "y", axis=0)
+    hidden = gather_by_shifts(gather_by_shifts(normed, "zh", 2), "y", n_col // 2)
     hidden = hidden.reshape((n_col,) + normed.shape)
-    out_w = lax.all_gather(out_weight, ROW, axis=0, tiled=True)
-    out_w = out_w.reshape(n_col, heads_here * HD, out_w.shape[1])
+    out_w = gather_by_shifts(gather_by_shifts(out_weight, "c", 2), "x", n_row // 2)
+    out_w = out_w.reshape((n_row,) + out_weight.shape)
     blocks = jnp.einsum("ktd,kde->ket", hidden, out_w, preferred_element_type=jnp.float32)
     mixed_sums = jnp.sum(blocks.astype(jnp.bfloat16).astype(jnp.float32), axis=0)
     return (tokens.astype(jnp.float32) + mixed_sums).astype(jnp.bfloat16)

time: 260 us -> 303 us (1.17)
  the two profiles are of different devices: /device:TPU:1 before, /device:TPU:70 now
where the time goes in v3:
time: 303 us; the launch traced here: 302 us
  starting transfers between devices  146 us (48%)
  waiting for transfers between devices  105 us (35%)
  local copies, waits for them, and re-layouts  23.4 us (8%)
  other arithmetic  18.8 us (6%)
  matrix products  6.95 us (2%)
    ppermute x23, starting transfers between devices, gather_by_shifts(): lax.ppermute(x, axis, [(i, (i + k) % n) for i in range(n)])  117 us
    ppermute x4, waiting for transfers between devices, reduce_scatter_by_shifts(): lax.ppermute(part, axis, [(i, (i + k) % n) for i in range(n)])  44.3 us
    ppermute x23, waiting for transfers between devices, gather_by_shifts(): lax.ppermute(x, axis, [(i, (i + k) % n) for i in range(n)])  38.5 us
    gather x12, local copies, waits for them, and re-layouts, gather_by_shifts(): return jnp.take(stacked, (me - jnp.arange(n)) % n, axis=0)  13 us
    all_to_all x1, waiting for transfers between devices, shards(): chosen = lax.all_to_all(to_send, COL, 0, 0, tiled=True)  12.6 us
    ppermute x4, starting transfers between devices, reduce_scatter_by_shifts(): lax.ppermute(part, axis, [(i, (i + k) % n) for i in range(n)])  11.5 us
    ppermute x1, waiting for transfers between devices, shards(): chosen = lax.ppermute(chosen, flat, perm)  9.2 us
  transfers between devices with their start and end apart: 31, of which 13 were waited for; matrix products, arithmetic and copies ran while one was open for 11% of the time, Pallas kernels for 0%

profile of v3, /device:TPU:70, one launch (start us, length us, event | category | flops | bytes accessed | tf_op | source)
XLA Modules:
  0.0 301.7 jit_solution(10314378281284343348)
XLA Ops:
  1.5 13.9 %collective-permute-start.4 = (s32[2]{0:T(128)S(1)}, s32[2]{0:T(128)S(1)}, u32[]{:S(2)}, u32[]{:S(2)}) collective-permute-start(s32[2]{0:T(128)S(1)} %pad_add_fusion.2), channel_id=1, source_target_pairs={{0,1},{1,0},{2,3},{3,2},{4,5},{5,4},{6,7},{7,6},{8,9},{9,8},{10,11... | collective-permute-start | bytes 32 | tf_op jit(solution)/shard_map/ppermute | solution.py:42
  22.1 4.5 %all-to-all-start = ((bf16[8,3,7644]{2,1,0:T(4,128)(2,1)}), bf16[8,3,7644]{2,1,0:T(4,128)(2,1)S(1)}, u32[]{:S(2)}, u32[]{:S(2)}) async-start(bf16[8,3,7644]{2,1,0:T(4,128)(2,1)} %copy.19), calls=%async_computation | async-start | bytes 983040 | tf_op jit(solution)/shard_map/all_to_all | solution.py:87
  26.6 1.9 collective-permute-start.16
  28.5 5.0 %collective-permute-start.24 = (f32[224]{0:T(256)}, f32[224]{0:T(256)}, u32[]{:S(2)}, u32[]{:S(2)}) collective-permute-start(f32[224]{0:T(256)} %param.11), channel_id=1, source_target_pairs={{0,0},{1,8},{2,16},{3,24},{4,32},{5,40},{6,48},{7,56},{8,1},{9,9},... | collective-permute-start | bytes 2696 | tf_op jit(solution)/shard_map/ppermute | solution.py:121
  33.6 11.6 %collective-permute-start = (bf16[224,224]{1,0:T(8,128)(2,1)S(1)}, bf16[224,224]{1,0:T(8,128)(2,1)}, u32[]{:S(2)}, u32[]{:S(2)}) collective-permute-start(bf16[224,224]{1,0:T(8,128)(2,1)S(1)} %copy-done.7), channel_id=1, source_target_pairs={{0,8},{8,0},{1,9},{9,1},{2,10},{10,2},{3,11},{11,3},{4,12},{12,4},... | collective-permute-start | bytes 301064 | tf_op jit(solution)/shard_map/ppermute | solution.py:42
  48.9 3.7 %collective-permute-start.5 = (s32[2,2]{1,0:T(2,128)S(1)}, s32[2,2]{1,0:T(2,128)S(1)}, u32[]{:S(2)}, u32[]{:S(2)}) collective-permute-start(s32[2,2]{1,0:T(2,128)S(1)} %broadcast_select_fusion.4), channel_id=1, source_target_pairs={{0,2},{2,4},{4,6},{6,0},{1,3},{3,5},{5,7},{7,1},{8,10},{10,12},{12... | collective-permute-start | bytes 56 | tf_op jit(solution)/shard_map/ppermute | solution.py:42
  52.6 2.2 collective-permute-start.6
  54.9 4.3 %collective-permute-start.7 = (s32[2,2]{1,0:T(2,128)S(1)}, s32[2,2]{1,0:T(2,128)S(1)}, u32[]{:S(2)}, u32[]{:S(2)}) collective-permute-start(s32[2,2]{1,0:T(2,128)S(1)} %broadcast_select_fusion.4), channel_id=1, source_target_pairs={{0,6},{2,0},{4,2},{6,4},{1,7},{3,1},{5,3},{7,5},{8,14},{10,8},{12,... | collective-permute-start | bytes 56 | tf_op jit(solution)/shard_map/ppermute | solution.py:42
  60.6 3.9 %collective-permute-start.17 = (bf16[2,224,288]{1,2,0:T(8,128)(2,1)}, bf16[2,224,288]{1,2,0:T(8,128)(2,1)S(1)}, u32[]{:S(2)}, u32[]{:S(2)}) collective-permute-start(bf16[2,224,288]{1,2,0:T(8,128)(2,1)} %broadcast_select_fusion.2), channel_id=1, source_target_pairs={{0,16},{16,32},{32,48},{48,0},{1,17},{17,33},{33,49},{49,1},{2,18}... | collective-permute-start | bytes 774152 | tf_op jit(solution)/shard_map/ppermute | solution.py:42
  64.6 1.9 collective-permute-start.18
  66.5 2.8 collective-permute-start.19
  70.7 6.1 %collective-permute-done.17 = bf16[2,224,288]{1,2,0:T(8,128)(2,1)S(1)} collective-permute-done((bf16[2,224,288]{1,2,0:T(8,128)(2,1)}, bf16[2,224,288]{1,2,0:T(8,128)(2,1)S(1)}, u32[]{:S(2)}, u32[]{:S(2)}) %collective-permute-start.17) | collective-permute-done | bytes 258080 | tf_op jit(solution)/shard_map/ppermute | solution.py:42
  78.1 4.2 %collective-permute-done.19 = bf16[2,224,288]{1,2,0:T(8,128)(2,1)S(1)} collective-permute-done((bf16[2,224,288]{1,2,0:T(8,128)(2,1)}, bf16[2,224,288]{1,2,0:T(8,128)(2,1)S(1)}, u32[]{:S(2)}, u32[]{:S(2)}) %collective-permute-start.19) | collective-permute-done | bytes 258080 | tf_op jit(solution)/shard_map/ppermute | solution.py:42
  83.7 1.9 gather_fusion.7
  87.5 2.2 collective-permute-start.20
  89.7 3.4 %collective-permute-start.21 = (bf16[576,512]{1,0:T(8,128)(2,1)S(1)}, bf16[576,512]{1,0:T(8,128)(2,1)S(1)}, u32[]{:S(2)}, u32[]{:S(2)}) collective-permute-start(bf16[576,512]{1,0:T(8,128)(2,1)S(1)} %get-tuple-element.7), channel_id=1, source_target_pairs={{0,4},{2,6},{4,0},{6,2},{1,5},{3,7},{5,1},{7,3},{8,12},{10,14},{12... | collective-permute-start | bytes 1769480 | tf_op jit(solution)/shard_map/ppermute | solution.py:53
  93.1 3.4 %collective-permute-start.22 = (bf16[576,512]{1,0:T(8,128)(2,1)S(1)}, bf16[576,512]{1,0:T(8,128)(2,1)S(1)}, u32[]{:S(2)}, u32[]{:S(2)}) collective-permute-start(bf16[576,512]{1,0:T(8,128)(2,1)S(1)} %get-tuple-element.6), channel_id=1, source_target_pairs={{0,6},{2,0},{4,2},{6,4},{1,7},{3,1},{5,3},{7,5},{8,14},{10,8},{12,... | collective-permute-start | bytes 1769480 | tf_op jit(solution)/shard_map/ppermute | solution.py:53
  98.6 19.9 %collective-permute-done.20 = bf16[576,512]{1,0:T(8,128)(2,1)S(1)} collective-permute-done((bf16[576,512]{1,0:T(8,128)(2,1)S(1)}, bf16[576,512]{1,0:T(8,128)(2,1)S(1)}, u32[]{:S(2)}, u32[]{:S(2)}) %collective-permute-start.20) | collective-permute-done | bytes 589856 | tf_op jit(solution)/shard_map/ppermute | solution.py:53
  118.5 2.5 collective-permute-done.22
  122.1 2.6 collective-permute-start.23
  127.1 21.9 %collective-permute-done.23 = bf16[288,512]{1,0:T(8,128)(2,1)} collective-permute-done((bf16[288,512]{1,0:T(8,128)(2,1)}, bf16[288,512]{1,0:T(8,128)(2,1)}, u32[]{:S(2)}, u32[]{:S(2)}) %collective-permute-start.23) | collective-permute-done | bytes 294944 | tf_op jit(solution)/shard_map/ppermute | solution.py:53
  150.3 2.8 collective-permute-start.8
  153.2 12.7 %collective-permute-start.9 = (bf16[3,7644]{1,0:T(4,128)(2,1)S(1)}, bf16[3,7644]{1,0:T(4,128)(2,1)S(1)}, u32[]{:S(2)}, u32[]{:S(2)}) collective-permute-start(bf16[3,7644]{1,0:T(4,128)(2,1)S(1)} %reduce_sum.30), channel_id=1, source_target_pairs={{0,128},{64,192},{128,256},{192,320},{256,384},{320,448},{384,0},{... | collective-permute-start | bytes 137600 | tf_op jit(solution)/shard_map/ppermute | solution.py:42
  165.9 6.2 %collective-permute-start.10 = (bf16[3,7644]{1,0:T(4,128)(2,1)S(1)}, bf16[3,7644]{1,0:T(4,128)(2,1)S(1)}, u32[]{:S(2)}, u32[]{:S(2)}) collective-permute-start(bf16[3,7644]{1,0:T(4,128)(2,1)S(1)} %reduce_sum.30), channel_id=1, source_target_pairs={{0,192},{64,256},{128,320},{192,384},{256,448},{320,0},{384,64},{4... | collective-permute-start | bytes 137600 | tf_op jit(solution)/shard_map/ppermute | solution.py:42
  172.1 4.1 %collective-permute-start.11 = (bf16[3,7644]{1,0:T(4,128)(2,1)S(1)}, bf16[3,7644]{1,0:T(4,128)(2,1)S(1)}, u32[]{:S(2)}, u32[]{:S(2)}) collective-permute-start(bf16[3,7644]{1,0:T(4,128)(2,1)S(1)} %reduce_sum.30), channel_id=1, source_target_pairs={{0,256},{64,320},{128,384},{192,448},{256,0},{320,64},{384,128},{4... | collective-permute-start | bytes 137600 | tf_op jit(solution)/shard_map/ppermute | solution.py:42
  176.3 7.8 %collective-permute-start.12 = (bf16[3,7644]{1,0:T(4,128)(2,1)S(1)}, bf16[3,7644]{1,0:T(4,128)(2,1)S(1)}, u32[]{:S(2)}, u32[]{:S(2)}) collective-permute-start(bf16[3,7644]{1,0:T(4,128)(2,1)S(1)} %reduce_sum.30), channel_id=1, source_target_pairs={{0,320},{64,384},{128,448},{192,0},{256,64},{320,128},{384,192},{4... | collective-permute-start | bytes 137600 | tf_op jit(solution)/shard_map/ppermute | solution.py:42
  184.1 2.1 collective-permute-start.13
  186.2 4.8 %collective-permute-start.14 = (bf16[3,7644]{1,0:T(4,128)(2,1)S(1)}, bf16[3,7644]{1,0:T(4,128)(2,1)S(1)}, u32[]{:S(2)}, u32[]{:S(2)}) collective-permute-start(bf16[3,7644]{1,0:T(4,128)(2,1)S(1)} %reduce_sum.30), channel_id=1, source_target_pairs={{0,448},{64,0},{128,64},{192,128},{256,192},{320,256},{384,320},{4... | collective-permute-start | bytes 137600 | tf_op jit(solution)/shard_map/ppermute | solution.py:42
  197.3 5.1 %all-to-all-start.1 = ((bf16[8,2,3822]{2,1,0:T(2,128)(2,1)}), bf16[8,2,3822]{2,1,0:T(2,128)(2,1)S(1)}, u32[]{:S(2)}, u32[]{:S(2)}) async-start(bf16[8,2,3822]{2,1,0:T(2,128)(2,1)} %reshape.550), calls=%async_computation.1 | async-start | bytes 245760 | tf_op jit(solution)/shard_map/all_to_all | solution.py:92
  202.6 2.7 fusion.6
  205.3 12.6 %all-to-all-done.1 = bf16[8,2,3822]{2,1,0:T(2,128)(2,1)S(1)} async-done(((bf16[8,2,3822]{2,1,0:T(2,128)(2,1)}), bf16[8,2,3822]{2,1,0:T(2,128)(2,1)S(1)}, u32[]{:S(2)}, u32[]{:S(2)}) %all-to-all-start.1) | async-done | bytes 122336 | tf_op jit(solution)/shard_map/all_to_all | solution.py:92
  218.1 2.2 collective-permute-start.15
  220.4 9.2 %collective-permute-done.15 = bf16[8,7644]{1,0:T(8,128)(2,1)S(1)} collective-permute-done((bf16[8,7644]{1,0:T(8,128)(2,1)S(1)}, bf16[8,7644]{1,0:T(8,128)(2,1)S(1)}, u32[]{:S(2)}, u32[]{:S(2)}) %collective-permute-start.15) | collective-permute-done | bytes 122336 | tf_op jit(solution)/shard_map/ppermute | solution.py:93
  231.5 13.2 %collective-permute-start.25 = (bf16[512,224]{0,1:T(8,128)(2,1)S(1)}, bf16[512,224]{0,1:T(8,128)(2,1)S(1)}, u32[]{:S(2)}, u32[]{:S(2)}) collective-permute-start(bf16[512,224]{0,1:T(8,128)(2,1)S(1)} %bitcast.99), channel_id=1, source_target_pairs={{0,1},{1,0},{2,3},{3,2},{4,5},{5,4},{6,7},{7,6},{8,9},{9,8},{10,11... | collective-permute-start | bytes 688136 | tf_op jit(solution)/shard_map/ppermute | solution.py:42
  245.4 1.9 collective-permute-start.1
  247.4 1.9 collective-permute-start.2
  249.3 3.9 %collective-permute-start.3 = (bf16[2,224,224]{2,1,0:T(8,128)(2,1)}, bf16[2,224,224]{2,1,0:T(8,128)(2,1)}, u32[]{:S(2)}, u32[]{:S(2)}) collective-permute-start(bf16[2,224,224]{2,1,0:T(8,128)(2,1)} %broadcast_select_fusion.3), channel_id=1, source_target_pairs={{0,48},{16,0},{32,16},{48,32},{1,49},{17,1},{33,17},{49,33},{2,50}... | collective-permute-start | bytes 602120 | tf_op jit(solution)/shard_map/ppermute | solution.py:42
  253.2 11.8 %collective-permute-done.25 = bf16[512,224]{0,1:T(8,128)(2,1)S(1)} collective-permute-done((bf16[512,224]{0,1:T(8,128)(2,1)S(1)}, bf16[512,224]{0,1:T(8,128)(2,1)S(1)}, u32[]{:S(2)}, u32[]{:S(2)}) %collective-permute-start.25) | collective-permute-done | bytes 229408 | tf_op jit(solution)/shard_map/ppermute | solution.py:42
  266.7 2.9 collective-permute-start.26
  269.5 1.9 collective-permute-start.27
  271.5 4.6 %collective-permute-start.28 = (bf16[2,512,224]{1,2,0:T(8,128)(2,1)}, bf16[2,512,224]{1,2,0:T(8,128)(2,1)}, u32[]{:S(2)}, u32[]{:S(2)}) collective-permute-start(bf16[2,512,224]{1,2,0:T(8,128)(2,1)} %broadcast_select_fusion), channel_id=1, source_target_pairs={{0,6},{2,0},{4,2},{6,4},{1,7},{3,1},{5,3},{7,5},{8,14},{10,8},{12,... | collective-permute-start | bytes 1376264 | tf_op jit(solution)/shard_map/ppermute | solution.py:42
  277.6 1.7 gather_fusion.1
  279.2 2.2 copy.17
  281.6 10.8 %collective-permute-done.26 = bf16[2,512,224]{1,2,0:T(8,128)(2,1)} collective-permute-done((bf16[2,512,224]{1,2,0:T(8,128)(2,1)}, bf16[2,512,224]{1,2,0:T(8,128)(2,1)}, u32[]{:S(2)}, u32[]{:S(2)}) %collective-permute-start.26) | collective-permute-done | bytes 458784 | tf_op jit(solution)/shard_map/ppermute | solution.py:42
  292.3 2.5 collective-permute-done.28
  294.9 1.5 pad_maximum_fusion
  296.4 2.1 gather_fusion.9
  298.5 1.8 bitcast_select_fusion
  (159 shorter events, 38.2 us)
Async XLA Ops:
  0.0 18.3 %copy-start = (bf16[3,224,1024]{2,1,0:T(8,128)(2,1)S(1)}, bf16[3,224,1024]{2,1,0:T(8,128)(2,1)}, u32[]{:S(2)}) copy-start(bf16[3,224,1024]{2,1,0:T(8,128)(2,1)} %param.13) | copy-start | bytes 4128772
  1.5 46.8 %collective-permute-start.4 = (s32[2]{0:T(128)S(1)}, s32[2]{0:T(128)S(1)}, u32[]{:S(2)}, u32[]{:S(2)}) collective-permute-start(s32[2]{0:T(128)S(1)} %pad_add_fusion.2), channel_id=1, source_target_pairs={{0,1},{1,0},{2,3},{3,2},{4,5},{5,4},{6,7},{7,6},{8,9},{9,8},{10,11... | collective-permute-start | bytes 32 | tf_op jit(solution)/shard_map/ppermute | solution.py:42
  20.1 6.5 %copy-start.6 = (bf16[224,288]{0,1:T(8,128)(2,1)S(1)}, bf16[224,288]{0,1:T(8,128)(2,1)}, u32[]{:S(2)}) copy-start(bf16[224,288]{0,1:T(8,128)(2,1)} %param.9) | copy-start | bytes 387076
  20.1 13.4 %copy-start.7 = (bf16[224,224]{1,0:T(8,128)(2,1)S(1)}, bf16[224,224]{1,0:T(8,128)(2,1)}, u32[]{:S(2)}) copy-start(bf16[224,224]{1,0:T(8,128)(2,1)} %param.10) | copy-start | bytes 301060
  22.1 127.9 %all-to-all-start = ((bf16[8,3,7644]{2,1,0:T(4,128)(2,1)}), bf16[8,3,7644]{2,1,0:T(4,128)(2,1)S(1)}, u32[]{:S(2)}, u32[]{:S(2)}) async-start(bf16[8,3,7644]{2,1,0:T(4,128)(2,1)} %copy.19), calls=%async_computation | async-start | bytes 983040 | tf_op jit(solution)/shard_map/all_to_all | solution.py:87
  26.6 28.3 %collective-permute-start.16 = (bf16[224,288]{0,1:T(8,128)(2,1)S(1)}, bf16[224,288]{0,1:T(8,128)(2,1)S(1)}, u32[]{:S(2)}, u32[]{:S(2)}) collective-permute-start(bf16[224,288]{0,1:T(8,128)(2,1)S(1)} %copy-done.6), channel_id=1, source_target_pairs={{0,8},{8,0},{1,9},{9,1},{2,10},{10,2},{3,11},{11,3},{4,12},{12,4},... | collective-permute-start | bytes 387080 | tf_op jit(solution)/shard_map/ppermute | solution.py:42
  28.5 96.2 %collective-permute-start.24 = (f32[224]{0:T(256)}, f32[224]{0:T(256)}, u32[]{:S(2)}, u32[]{:S(2)}) collective-permute-start(f32[224]{0:T(256)} %param.11), channel_id=1, source_target_pairs={{0,0},{1,8},{2,16},{3,24},{4,32},{5,40},{6,48},{7,56},{8,1},{9,9},... | collective-permute-start | bytes 2696 | tf_op jit(solution)/shard_map/ppermute | solution.py:121
  33.6 91.9 %collective-permute-start = (bf16[224,224]{1,0:T(8,128)(2,1)S(1)}, bf16[224,224]{1,0:T(8,128)(2,1)}, u32[]{:S(2)}, u32[]{:S(2)}) collective-permute-start(bf16[224,224]{1,0:T(8,128)(2,1)S(1)} %copy-done.7), channel_id=1, source_target_pairs={{0,8},{8,0},{1,9},{9,1},{2,10},{10,2},{3,11},{11,3},{4,12},{12,4},... | collective-permute-start | bytes 301064 | tf_op jit(solution)/shard_map/ppermute | solution.py:42
  45.5 15.1 %copy-start.8 = (pred[2]{0:T(512)(128)(4,1)}, pred[2]{0:T(512)(128)(4,1)S(1)}, u32[]{:S(2)}) copy-start(pred[2]{0:T(512)(128)(4,1)S(1)} %get-tuple-element.12) | copy-start | bytes 10
  45.5 38.2 %copy-start.10 = (pred[2]{0:T(512)(128)(4,1)}, pred[2]{0:T(512)(128)(4,1)S(1)}, u32[]{:S(2)}) copy-start(pred[2]{0:T(512)(128)(4,1)S(1)} %get-tuple-element.13) | copy-start | bytes 10
  45.6 15.1 %copy-start.13 = (s32[1024]{0:T(1024)}, s32[1024]{0:T(1024)S(1)}, u32[]{:S(2)}) copy-start(s32[1024]{0:T(1024)S(1)} %pad_clamp_fusion.3) | copy-start | bytes 12292
  47.6 13.1 %copy-start.14 = (s32[1024]{0:T(1024)}, s32[1024]{0:T(1024)S(1)}, u32[]{:S(2)}) copy-start(s32[1024]{0:T(1024)S(1)} %pad_clamp_fusion.5) | copy-start | bytes 12292
  48.2 35.5 %copy-start.12 = (s32[1024]{0:T(1024)}, s32[1024]{0:T(1024)S(1)}, u32[]{:S(2)}) copy-start(s32[1024]{0:T(1024)S(1)} %get-tuple-element.16) | copy-start | bytes 12292
  48.2 35.5 %copy-start.15 = (s32[1024]{0:T(1024)}, s32[1024]{0:T(1024)S(1)}, u32[]{:S(2)}) copy-start(s32[1024]{0:T(1024)S(1)} %get-tuple-element.17) | copy-start | bytes 12292
  48.9 11.7 %collective-permute-start.5 = (s32[2,2]{1,0:T(2,128)S(1)}, s32[2,2]{1,0:T(2,128)S(1)}, u32[]{:S(2)}, u32[]{:S(2)}) collective-permute-start(s32[2,2]{1,0:T(2,128)S(1)} %broadcast_select_fusion.4), channel_id=1, source_target_pairs={{0,2},{2,4},{4,6},{6,0},{1,3},{3,5},{5,7},{7,1},{8,10},{10,12},{12... | collective-permute-start | bytes 56 | tf_op jit(solution)/shard_map/ppermute | solution.py:42
  52.6 12.0 %collective-permute-start.6 = (s32[2,2]{1,0:T(2,128)S(1)}, s32[2,2]{1,0:T(2,128)S(1)}, u32[]{:S(2)}, u32[]{:S(2)}) collective-permute-start(s32[2,2]{1,0:T(2,128)S(1)} %broadcast_select_fusion.4), channel_id=1, source_target_pairs={{0,4},{2,6},{4,0},{6,2},{1,5},{3,7},{5,1},{7,3},{8,12},{10,14},{12... | collective-permute-start | bytes 56 | tf_op jit(solution)/shard_map/ppermute | solution.py:42
  54.9 11.6 %collective-permute-start.7 = (s32[2,2]{1,0:T(2,128)S(1)}, s32[2,2]{1,0:T(2,128)S(1)}, u32[]{:S(2)}, u32[]{:S(2)}) collective-permute-start(s32[2,2]{1,0:T(2,128)S(1)} %broadcast_select_fusion.4), channel_id=1, source_target_pairs={{0,6},{2,0},{4,2},{6,4},{1,7},{3,1},{5,3},{7,5},{8,14},{10,8},{12,... | collective-permute-start | bytes 56 | tf_op jit(solution)/shard_map/ppermute | solution.py:42
  60.6 16.2 %collective-permute-start.17 = (bf16[2,224,288]{1,2,0:T(8,128)(2,1)}, bf16[2,224,288]{1,2,0:T(8,128)(2,1)S(1)}, u32[]{:S(2)}, u32[]{:S(2)}) collective-permute-start(bf16[2,224,288]{1,2,0:T(8,128)(2,1)} %broadcast_select_fusion.2), channel_id=1, source_target_pairs={{0,16},{16,32},{32,48},{48,0},{1,17},{17,33},{33,49},{49,1},{2,18}... | collective-permute-start | bytes 774152 | tf_op jit(solution)/shard_map/ppermute | solution.py:42
  64.6 13.5 %collective-permute-start.18 = (bf16[2,224,288]{1,2,0:T(8,128)(2,1)}, bf16[2,224,288]{1,2,0:T(8,128)(2,1)S(1)}, u32[]{:S(2)}, u32[]{:S(2)}) collective-permute-start(bf16[2,224,288]{1,2,0:T(8,128)(2,1)} %broadcast_select_fusion.2), channel_id=1, source_target_pairs={{0,32},{16,48},{32,0},{48,16},{1,33},{17,49},{33,1},{49,17},{2,34}... | collective-permute-start | bytes 774152 | tf_op jit(solution)/shard_map/ppermute | solution.py:42
  66.5 15.8 %collective-permute-start.19 = (bf16[2,224,288]{1,2,0:T(8,128)(2,1)}, bf16[2,224,288]{1,2,0:T(8,128)(2,1)S(1)}, u32[]{:S(2)}, u32[]{:S(2)}) collective-permute-start(bf16[2,224,288]{1,2,0:T(8,128)(2,1)} %broadcast_select_fusion.2), channel_id=1, source_target_pairs={{0,48},{16,0},{32,16},{48,32},{1,49},{17,1},{33,17},{49,33},{2,50}... | collective-permute-start | bytes 774152 | tf_op jit(solution)/shard_map/ppermute | solution.py:42
  87.3 9.2 %copy-start.16 = (s32[8,2]{0,1:T(2,128)S(1)}, s32[8,2]{0,1:T(2,128)}, u32[]{:S(2)}) copy-start(s32[8,2]{0,1:T(2,128)} %copy.21) | copy-start | bytes 196
  87.3 9.2 %copy-start.17 = (pred[8]{0:T(512)(128)(4,1)S(1)}, pred[8]{0:T(512)(128)(4,1)}, u32[]{:S(2)}) copy-start(pred[8]{0:T(512)(128)(4,1)} %broadcast_in_dim.167) | copy-start | bytes 28
  87.5 31.0 %collective-permute-start.20 = (bf16[576,512]{1,0:T(8,128)(2,1)S(1)}, bf16[576,512]{1,0:T(8,128)(2,1)S(1)}, u32[]{:S(2)}, u32[]{:S(2)}) collective-permute-start(bf16[576,512]{1,0:T(8,128)(2,1)S(1)} %get-tuple-element.5), channel_id=1, source_target_pairs={{0,2},{2,4},{4,6},{6,0},{1,3},{3,5},{5,7},{7,1},{8,10},{10,12},{12... | collective-permute-start | bytes 1769480 | tf_op jit(solution)/shard_map/ppermute | solution.py:53
  89.7 28.8 %collective-permute-start.21 = (bf16[576,512]{1,0:T(8,128)(2,1)S(1)}, bf16[576,512]{1,0:T(8,128)(2,1)S(1)}, u32[]{:S(2)}, u32[]{:S(2)}) collective-permute-start(bf16[576,512]{1,0:T(8,128)(2,1)S(1)} %get-tuple-element.7), channel_id=1, source_target_pairs={{0,4},{2,6},{4,0},{6,2},{1,5},{3,7},{5,1},{7,3},{8,12},{10,14},{12... | collective-permute-start | bytes 1769480 | tf_op jit(solution)/shard_map/ppermute | solution.py:53
  93.1 27.9 %collective-permute-start.22 = (bf16[576,512]{1,0:T(8,128)(2,1)S(1)}, bf16[576,512]{1,0:T(8,128)(2,1)S(1)}, u32[]{:S(2)}, u32[]{:S(2)}) collective-permute-start(bf16[576,512]{1,0:T(8,128)(2,1)S(1)} %get-tuple-element.6), channel_id=1, source_target_pairs={{0,6},{2,0},{4,2},{6,4},{1,7},{3,1},{5,3},{7,5},{8,14},{10,8},{12,... | collective-permute-start | bytes 1769480 | tf_op jit(solution)/shard_map/ppermute | solution.py:53
  122.1 26.9 %collective-permute-start.23 = (bf16[288,512]{1,0:T(8,128)(2,1)}, bf16[288,512]{1,0:T(8,128)(2,1)}, u32[]{:S(2)}, u32[]{:S(2)}) collective-permute-start(bf16[288,512]{1,0:T(8,128)(2,1)} %constant_dynamic-slice_fusion), channel_id=1, source_target_pairs={{0,1},{1,0},{2,3},{3,2},{4,5},{5,4},{6,7},{7,6},{8,9},{9,8},{10,11... | collective-permute-start | bytes 884744 | tf_op jit(solution)/shard_map/ppermute | solution.py:53
  150.0 43.0 %copy-start.4 = (bf16[288,512]{1,0:T(8,128)(2,1)}, bf16[288,512]{1,0:T(8,128)(2,1)S(1)}, u32[]{:S(2)}) copy-start(bf16[288,512]{1,0:T(8,128)(2,1)S(1)} %add_convert_fusion.1) | copy-start | bytes 884740
  150.0 44.4 %copy-start.23 = (pred[24]{0:T(512)(128)(4,1)S(1)}, pred[24]{0:T(512)(128)(4,1)}, u32[]{:S(2)}) copy-start(pred[24]{0:T(512)(128)(4,1)} %broadcast_in_dim.176) | copy-start | bytes 76
  150.3 33.8 %collective-permute-start.8 = (bf16[3,7644]{1,0:T(4,128)(2,1)S(1)}, bf16[3,7644]{1,0:T(4,128)(2,1)S(1)}, u32[]{:S(2)}, u32[]{:S(2)}) collective-permute-start(bf16[3,7644]{1,0:T(4,128)(2,1)S(1)} %reduce_sum.30), channel_id=1, source_target_pairs={{0,64},{64,128},{128,192},{192,256},{256,320},{320,384},{384,448},... | collective-permute-start | bytes 137600 | tf_op jit(solution)/shard_map/ppermute | solution.py:42
  153.2 33.1 %collective-permute-start.9 = (bf16[3,7644]{1,0:T(4,128)(2,1)S(1)}, bf16[3,7644]{1,0:T(4,128)(2,1)S(1)}, u32[]{:S(2)}, u32[]{:S(2)}) collective-permute-start(bf16[3,7644]{1,0:T(4,128)(2,1)S(1)} %reduce_sum.30), channel_id=1, source_target_pairs={{0,128},{64,192},{128,256},{192,320},{256,384},{320,448},{384,0},{... | collective-permute-start | bytes 137600 | tf_op jit(solution)/shard_map/ppermute | solution.py:42
  165.9 25.2 %collective-permute-start.10 = (bf16[3,7644]{1,0:T(4,128)(2,1)S(1)}, bf16[3,7644]{1,0:T(4,128)(2,1)S(1)}, u32[]{:S(2)}, u32[]{:S(2)}) collective-permute-start(bf16[3,7644]{1,0:T(4,128)(2,1)S(1)} %reduce_sum.30), channel_id=1, source_target_pairs={{0,192},{64,256},{128,320},{192,384},{256,448},{320,0},{384,64},{4... | collective-permute-start | bytes 137600 | tf_op jit(solution)/shard_map/ppermute | solution.py:42
  172.1 19.0 %collective-permute-start.11 = (bf16[3,7644]{1,0:T(4,128)(2,1)S(1)}, bf16[3,7644]{1,0:T(4,128)(2,1)S(1)}, u32[]{:S(2)}, u32[]{:S(2)}) collective-permute-start(bf16[3,7644]{1,0:T(4,128)(2,1)S(1)} %reduce_sum.30), channel_id=1, source_target_pairs={{0,256},{64,320},{128,384},{192,448},{256,0},{320,64},{384,128},{4... | collective-permute-start | bytes 137600 | tf_op jit(solution)/shard_map/ppermute | solution.py:42
  176.3 15.0 %collective-permute-start.12 = (bf16[3,7644]{1,0:T(4,128)(2,1)S(1)}, bf16[3,7644]{1,0:T(4,128)(2,1)S(1)}, u32[]{:S(2)}, u32[]{:S(2)}) collective-permute-start(bf16[3,7644]{1,0:T(4,128)(2,1)S(1)} %reduce_sum.30), channel_id=1, source_target_pairs={{0,320},{64,384},{128,448},{192,0},{256,64},{320,128},{384,192},{4... | collective-permute-start | bytes 137600 | tf_op jit(solution)/shard_map/ppermute | solution.py:42
  184.1 8.3 %collective-permute-start.13 = (bf16[3,7644]{1,0:T(4,128)(2,1)S(1)}, bf16[3,7644]{1,0:T(4,128)(2,1)S(1)}, u32[]{:S(2)}, u32[]{:S(2)}) collective-permute-start(bf16[3,7644]{1,0:T(4,128)(2,1)S(1)} %reduce_sum.30), channel_id=1, source_target_pairs={{0,384},{64,448},{128,0},{192,64},{256,128},{320,192},{384,256},{4... | collective-permute-start | bytes 137600 | tf_op jit(solution)/shard_map/ppermute | solution.py:42
  186.2 6.7 %collective-permute-start.14 = (bf16[3,7644]{1,0:T(4,128)(2,1)S(1)}, bf16[3,7644]{1,0:T(4,128)(2,1)S(1)}, u32[]{:S(2)}, u32[]{:S(2)}) collective-permute-start(bf16[3,7644]{1,0:T(4,128)(2,1)S(1)} %reduce_sum.30), channel_id=1, source_target_pairs={{0,448},{64,0},{128,64},{192,128},{256,192},{320,256},{384,320},{4... | collective-permute-start | bytes 137600 | tf_op jit(solution)/shard_map/ppermute | solution.py:42
  194.6 8.0 %copy-start.5 = (bf16[288,512]{1,0:T(8,128)(2,1)S(1)}, bf16[288,512]{1,0:T(8,128)(2,1)}, u32[]{:S(2)}) copy-start(bf16[288,512]{1,0:T(8,128)(2,1)} %copy-done.4) | copy-start | bytes 884740
  197.3 20.6 %all-to-all-start.1 = ((bf16[8,2,3822]{2,1,0:T(2,128)(2,1)}), bf16[8,2,3822]{2,1,0:T(2,128)(2,1)S(1)}, u32[]{:S(2)}, u32[]{:S(2)}) async-start(bf16[8,2,3822]{2,1,0:T(2,128)(2,1)} %reshape.550), calls=%async_computation.1 | async-start | bytes 245760 | tf_op jit(solution)/shard_map/all_to_all | solution.py:92
  202.6 27.3 %copy-start.20 = (bf16[273]{0:T(512)(128)(2,1)S(1)}, bf16[273]{0:T(512)(128)(2,1)}, u32[]{:S(2)}) copy-start(bf16[273]{0:T(512)(128)(2,1)} %copy-done.19) | copy-start | bytes 1642
  205.3 39.4 %copy-start.11 = (pred[2]{0:T(512)(128)(4,1)S(1)}, pred[2]{0:T(512)(128)(4,1)}, u32[]{:S(2)}) copy-start(pred[2]{0:T(512)(128)(4,1)} %copy-done.10) | copy-start | bytes 10
  218.1 11.4 %collective-permute-start.15 = (bf16[8,7644]{1,0:T(8,128)(2,1)S(1)}, bf16[8,7644]{1,0:T(8,128)(2,1)S(1)}, u32[]{:S(2)}, u32[]{:S(2)}) collective-permute-start(bf16[8,7644]{1,0:T(8,128)(2,1)S(1)} %bitcast.114), channel_id=1, source_target_pairs={{0,0},{1,8},{2,16},{3,24},{4,32},{5,40},{6,48},{7,56},{8,1},{9,9},... | collective-permute-start | bytes 366920 | tf_op jit(solution)/shard_map/ppermute | solution.py:93
  231.3 34.4 %copy-start.9 = (pred[2]{0:T(512)(128)(4,1)S(1)}, pred[2]{0:T(512)(128)(4,1)}, u32[]{:S(2)}) copy-start(pred[2]{0:T(512)(128)(4,1)} %copy-done.8) | copy-start | bytes 10
  231.5 33.5 %collective-permute-start.25 = (bf16[512,224]{0,1:T(8,128)(2,1)S(1)}, bf16[512,224]{0,1:T(8,128)(2,1)S(1)}, u32[]{:S(2)}, u32[]{:S(2)}) collective-permute-start(bf16[512,224]{0,1:T(8,128)(2,1)S(1)} %bitcast.99), channel_id=1, source_target_pairs={{0,1},{1,0},{2,3},{3,2},{4,5},{5,4},{6,7},{7,6},{8,9},{9,8},{10,11... | collective-permute-start | bytes 688136 | tf_op jit(solution)/shard_map/ppermute | solution.py:42
  245.4 26.0 %collective-permute-start.1 = (bf16[2,224,224]{2,1,0:T(8,128)(2,1)}, bf16[2,224,224]{2,1,0:T(8,128)(2,1)}, u32[]{:S(2)}, u32[]{:S(2)}) collective-permute-start(bf16[2,224,224]{2,1,0:T(8,128)(2,1)} %broadcast_select_fusion.3), channel_id=1, source_target_pairs={{0,16},{16,32},{32,48},{48,0},{1,17},{17,33},{33,49},{49,1},{2,18}... | collective-permute-start | bytes 602120 | tf_op jit(solution)/shard_map/ppermute | solution.py:42
  247.4 28.8 %collective-permute-start.2 = (bf16[2,224,224]{2,1,0:T(8,128)(2,1)}, bf16[2,224,224]{2,1,0:T(8,128)(2,1)}, u32[]{:S(2)}, u32[]{:S(2)}) collective-permute-start(bf16[2,224,224]{2,1,0:T(8,128)(2,1)} %broadcast_select_fusion.3), channel_id=1, source_target_pairs={{0,32},{16,48},{32,0},{48,16},{1,33},{17,49},{33,1},{49,17},{2,34}... | collective-permute-start | bytes 602120 | tf_op jit(solution)/shard_map/ppermute | solution.py:42
  249.3 26.9 %collective-permute-start.3 = (bf16[2,224,224]{2,1,0:T(8,128)(2,1)}, bf16[2,224,224]{2,1,0:T(8,128)(2,1)}, u32[]{:S(2)}, u32[]{:S(2)}) collective-permute-start(bf16[2,224,224]{2,1,0:T(8,128)(2,1)} %broadcast_select_fusion.3), channel_id=1, source_target_pairs={{0,48},{16,0},{32,16},{48,32},{1,49},{17,1},{33,17},{49,33},{2,50}... | collective-permute-start | bytes 602120 | tf_op jit(solution)/shard_map/ppermute | solution.py:42
  266.7 25.7 %collective-permute-start.26 = (bf16[2,512,224]{1,2,0:T(8,128)(2,1)}, bf16[2,512,224]{1,2,0:T(8,128)(2,1)}, u32[]{:S(2)}, u32[]{:S(2)}) collective-permute-start(bf16[2,512,224]{1,2,0:T(8,128)(2,1)} %broadcast_select_fusion), channel_id=1, source_target_pairs={{0,2},{2,4},{4,6},{6,0},{1,3},{3,5},{5,7},{7,1},{8,10},{10,12},{12... | collective-permute-start | bytes 1376264 | tf_op jit(solution)/shard_map/ppermute | solution.py:42
  269.5 22.8 %collective-permute-start.27 = (bf16[2,512,224]{1,2,0:T(8,128)(2,1)}, bf16[2,512,224]{1,2,0:T(8,128)(2,1)S(1)}, u32[]{:S(2)}, u32[]{:S(2)}) collective-permute-start(bf16[2,512,224]{1,2,0:T(8,128)(2,1)} %broadcast_select_fusion), channel_id=1, source_target_pairs={{0,4},{2,6},{4,0},{6,2},{1,5},{3,7},{5,1},{7,3},{8,12},{10,14},{12... | collective-permute-start | bytes 1376264 | tf_op jit(solution)/shard_map/ppermute | solution.py:42
  271.5 23.4 %collective-permute-start.28 = (bf16[2,512,224]{1,2,0:T(8,128)(2,1)}, bf16[2,512,224]{1,2,0:T(8,128)(2,1)}, u32[]{:S(2)}, u32[]{:S(2)}) collective-permute-start(bf16[2,512,224]{1,2,0:T(8,128)(2,1)} %broadcast_select_fusion), channel_id=1, source_target_pairs={{0,6},{2,0},{4,2},{6,4},{1,7},{3,1},{5,3},{7,5},{8,14},{10,8},{12,... | collective-permute-start | bytes 1376264 | tf_op jit(solution)/shard_map/ppermute | solution.py:42
  (7 other events, 11.7 us)

commit v4 on v3

--- a/solution.py
+++ b/solution.py
@@ -64,11 +64,6 @@
     heads_here = head_gain.shape[0] // HD
     row_here = lax.axis_index("x") * 2 + lax.axis_index("c")
     col_here = lax.axis_index("y") * 2 + lax.axis_index("zh")
-    meta = jnp.concatenate([suffix_len, prefix_owner])
-    meta = gather_by_shifts(gather_by_shifts(meta, "zh", 2), "y", n_col // 2)
-    meta = meta.reshape(n_col, 2)
-    lens = meta[:, 0]
-    owners = meta[:, 1]
     flat = ROW + COL
     perm = [(i * n_col + j, j * n_col + i) for i in range(n_row) for j in range(n_col)]
 
@@ -84,9 +79,18 @@
     state_shape = partial_state.shape[1:]
     piece = partial_state[0].size // n_col
     pieces = partial_state.astype(jnp.bfloat16).reshape(pref_here, n_col, piece)
-    pieces = lax.all_to_all(jnp.swapaxes(pieces, 0, 1), COL, 0, 0, tiled=True)
+    pieces = jnp.swapaxes(pieces, 0, 1).reshape(n_col, pref_here * piece)
+    meta = jnp.stack([prefix_owner[0], suffix_len[0] // 16, suffix_len[0] % 16])
+    meta = jnp.broadcast_to(meta.astype(jnp.bfloat16)[None], (n_col, 3))
+    got = lax.all_to_all(jnp.concatenate([pieces, meta], axis=1), COL, 0, 0, tiled=True)
+    meta = got[:, pref_here * piece :].astype(jnp.int32)
+    owners = meta[:, 0]
+    lens = meta[:, 1] * 16 + meta[:, 2]
+    pieces = got[:, : pref_here * piece].reshape(n_col, pref_here, piece)
     pieces = jnp.sum(pieces.astype(jnp.float32), axis=0).astype(jnp.bfloat16)
-    pieces = gather_by_shifts(pieces, "req", lax.psum(1, "req"))
+    n_req = lax.psum(1, "req")
+    pieces = jnp.broadcast_to(pieces[None], (n_req,) + pieces.shape)
+    pieces = lax.all_to_all(pieces, "req", 0, 0, tiled=True)
     pieces = pieces.reshape((-1, piece))
     to_send = jnp.take(pieces, owners, axis=0)
     chosen = lax.all_to_all(to_send, COL, 0, 0, tiled=True)
@@ -99,7 +103,9 @@
         "kdj,dt->kjt", weight_all, tokens, preferred_element_type=jnp.float32
     ).astype(jnp.bfloat16)
     partial_proj = partial_proj.reshape(-1, tokens.shape[1])
+    partial_proj, to_send = lax.optimization_barrier((partial_proj, to_send))
     projected = reduce_scatter_by_shifts(partial_proj, "y", n_col // 2).astype(jnp.bfloat16)
+    projected, chosen = lax.optimization_barrier((projected, chosen))
     projected = reduce_scatter_by_shifts(projected, "zh", 2).astype(jnp.bfloat16)
     projected = projected.T.reshape(SLOTS, heads_here, 2 * FEAT + HD)
     queries = projected[..., :FEAT]

time: 303 us -> 245 us (0.81)
  the two profiles are of different devices: /device:TPU:70 before, /device:TPU:15 now
where the time goes in v4:
time: 245 us; the launch traced here: 244 us
  starting transfers between devices  95.8 us (39%)
  waiting for transfers between devices  91.8 us (37%)
  local copies, waits for them, and re-layouts  24 us (10%)
  other arithmetic  23.2 us (9%)
  matrix products  7.28 us (3%)
    ppermute x12, waiting for transfers between devices, gather_by_shifts(): lax.ppermute(x, axis, [(i, (i + k) % n) for i in range(n)])  40.7 us
    ppermute x4, waiting for transfers between devices, reduce_scatter_by_shifts(): lax.ppermute(part, axis, [(i, (i + k) % n) for i in range(n)])  32.2 us
    ppermute x12, starting transfers between devices, gather_by_shifts(): lax.ppermute(x, axis, [(i, (i + k) % n) for i in range(n)])  28.6 us
    all_to_all x1, starting transfers between devices, shards(): lax.all_to_all(jnp.concatenate([pieces, meta], axis=1), COL, 0, 0, tiled=...  17.6 us
    ppermute x1, starting transfers between devices, shards(): gains = lax.ppermute(head_gain, flat, perm).reshape(heads_here, HD)  14.1 us
    ppermute x1, starting transfers between devices, shards(): chosen = lax.ppermute(chosen, flat, perm)  13.8 us
    ppermute x4, starting transfers between devices, reduce_scatter_by_shifts(): lax.ppermute(part, axis, [(i, (i + k) % n) for i in range(n)])  12.4 us
    gather x7, local copies, waits for them, and re-layouts, gather_by_shifts(): return jnp.take(stacked, (me - jnp.arange(n)) % n, axis=0)  9.65 us
  transfers between devices with their start and end apart: 21, of which 11 were waited for; matrix products, arithmetic and copies ran while one was open for 13% of the time, Pallas kernels for 0%

profile of v4, /device:TPU:15, one launch (start us, length us, event | category | flops | bytes accessed | tf_op | source)
XLA Modules:
  0.0 244.2 jit_solution(6870549289731942952)
XLA Ops:
  1.7 1.0 multiply_convert_fusion.3
  4.9 1.3 fusion.7
  8.0 1.5 copy.21
  9.5 17.6 %all-to-all-start = ((bf16[8,1,22935]{2,1,0:T(2,128)(2,1)}), bf16[8,1,22935]{2,1,0:T(2,128)(2,1)S(1)}, u32[]{:S(2)}, u32[]{:S(2)}) async-start(bf16[8,1,22935]{2,1,0:T(2,128)(2,1)} %copy.21), calls=%async_computation | async-start | bytes 1474560 | tf_op jit(solution)/shard_map/all_to_all | solution.py:85
  27.1 3.1 %collective-permute-start.4 = (bf16[224,288]{0,1:T(8,128)(2,1)S(1)}, bf16[224,288]{0,1:T(8,128)(2,1)S(1)}, u32[]{:S(2)}, u32[]{:S(2)}) collective-permute-start(bf16[224,288]{0,1:T(8,128)(2,1)S(1)} %copy-done.7), channel_id=1, source_target_pairs={{0,8},{8,0},{1,9},{9,1},{2,10},{10,2},{3,11},{11,3},{4,12},{12,4},... | collective-permute-start | bytes 387080 | tf_op jit(solution)/shard_map/ppermute | solution.py:42
  30.2 14.1 %collective-permute-start.13 = (f32[224]{0:T(256)}, f32[224]{0:T(256)}, u32[]{:S(2)}, u32[]{:S(2)}) collective-permute-start(f32[224]{0:T(256)} %param.11), channel_id=1, source_target_pairs={{0,0},{1,8},{2,16},{3,24},{4,32},{5,40},{6,48},{7,56},{8,1},{9,9},... | collective-permute-start | bytes 2696 | tf_op jit(solution)/shard_map/ppermute | solution.py:127
  44.3 1.9 collective-permute-start
  48.9 1.9 collective-permute-start.5
  50.8 2.8 %collective-permute-start.6 = (bf16[2,224,288]{1,2,0:T(8,128)(2,1)}, bf16[2,224,288]{1,2,0:T(8,128)(2,1)S(1)}, u32[]{:S(2)}, u32[]{:S(2)}) collective-permute-start(bf16[2,224,288]{1,2,0:T(8,128)(2,1)} %broadcast_select_fusion.1), channel_id=1, source_target_pairs={{0,32},{16,48},{32,0},{48,16},{1,33},{17,49},{33,1},{49,17},{2,34}... | collective-permute-start | bytes 774152 | tf_op jit(solution)/shard_map/ppermute | solution.py:42
  53.5 2.5 %collective-permute-start.7 = (bf16[2,224,288]{1,2,0:T(8,128)(2,1)}, bf16[2,224,288]{1,2,0:T(8,128)(2,1)}, u32[]{:S(2)}, u32[]{:S(2)}) collective-permute-start(bf16[2,224,288]{1,2,0:T(8,128)(2,1)} %broadcast_select_fusion.1), channel_id=1, source_target_pairs={{0,48},{16,0},{32,16},{48,32},{1,49},{17,1},{33,17},{49,33},{2,50}... | collective-permute-start | bytes 774152 | tf_op jit(solution)/shard_map/ppermute | solution.py:42
  57.4 1.6 collective-permute-done.5
  59.0 3.5 %collective-permute-done.6 = bf16[2,224,288]{1,2,0:T(8,128)(2,1)S(1)} collective-permute-done((bf16[2,224,288]{1,2,0:T(8,128)(2,1)}, bf16[2,224,288]{1,2,0:T(8,128)(2,1)S(1)}, u32[]{:S(2)}, u32[]{:S(2)}) %collective-permute-start.6) | collective-permute-done | bytes 258080 | tf_op jit(solution)/shard_map/ppermute | solution.py:42
  62.5 7.2 %collective-permute-done.7 = bf16[2,224,288]{1,2,0:T(8,128)(2,1)} collective-permute-done((bf16[2,224,288]{1,2,0:T(8,128)(2,1)}, bf16[2,224,288]{1,2,0:T(8,128)(2,1)}, u32[]{:S(2)}, u32[]{:S(2)}) %collective-permute-start.7) | collective-permute-done | bytes 258080 | tf_op jit(solution)/shard_map/ppermute | solution.py:42
  69.7 2.3 pad_maximum_fusion.1
  72.0 1.9 gather_fusion.3
  76.0 4.7 %all-to-all-start.1 = ((bf16[8,3,7644]{2,1,0:T(4,128)(2,1)}), bf16[8,3,7644]{2,1,0:T(4,128)(2,1)S(1)}, u32[]{:S(2)}, u32[]{:S(2)}) async-start(bf16[8,3,7644]{2,1,0:T(4,128)(2,1)} %broadcast_in_dim.167), calls=%async_computation.1 | async-start | bytes 983040 | tf_op jit(solution)/shard_map/all_to_all | solution.py:93
  82.4 1.4 copy-done.1
  83.8 1.3 constant_dynamic-slice_fusion.3
  85.1 2.0 collective-permute-start.10
  87.1 3.4 %collective-permute-start.8 = (bf16[576,512]{1,0:T(8,128)(2,1)}, bf16[576,512]{1,0:T(8,128)(2,1)}, u32[]{:S(2)}, u32[]{:S(2)}) collective-permute-start(bf16[576,512]{1,0:T(8,128)(2,1)} %get-tuple-element.9), channel_id=1, source_target_pairs={{0,2},{2,4},{4,6},{6,0},{1,3},{3,5},{5,7},{7,1},{8,10},{10,12},{12... | collective-permute-start | bytes 1769480 | tf_op jit(solution)/shard_map/ppermute | solution.py:53
  90.5 4.9 %collective-permute-start.9 = (bf16[576,512]{1,0:T(8,128)(2,1)}, bf16[576,512]{1,0:T(8,128)(2,1)}, u32[]{:S(2)}, u32[]{:S(2)}) collective-permute-start(bf16[576,512]{1,0:T(8,128)(2,1)} %get-tuple-element.11), channel_id=1, source_target_pairs={{0,4},{2,6},{4,0},{6,2},{1,5},{3,7},{5,1},{7,3},{8,12},{10,14},{12... | collective-permute-start | bytes 1769480 | tf_op jit(solution)/shard_map/ppermute | solution.py:53
  96.4 4.6 %all-to-all-done.1 = bf16[8,3,7644]{2,1,0:T(4,128)(2,1)S(1)} async-done(((bf16[8,3,7644]{2,1,0:T(4,128)(2,1)}), bf16[8,3,7644]{2,1,0:T(4,128)(2,1)S(1)}, u32[]{:S(2)}, u32[]{:S(2)}) %all-to-all-start.1) | async-done | bytes 366944 | tf_op jit(solution)/shard_map/all_to_all | solution.py:93
  104.1 4.6 %all-to-all-start.2 = ((bf16[8,2,3822]{2,1,0:T(2,128)(2,1)}), bf16[8,2,3822]{2,1,0:T(2,128)(2,1)S(1)}, u32[]{:S(2)}, u32[]{:S(2)}) async-start(bf16[8,2,3822]{2,1,0:T(2,128)(2,1)} %reshape.489), calls=%async_computation.2 | async-start | bytes 245760 | tf_op jit(solution)/shard_map/all_to_all | solution.py:96
  112.4 9.3 %all-to-all-done.2 = bf16[8,2,3822]{2,1,0:T(2,128)(2,1)S(1)} async-done(((bf16[8,2,3822]{2,1,0:T(2,128)(2,1)}), bf16[8,2,3822]{2,1,0:T(2,128)(2,1)S(1)}, u32[]{:S(2)}, u32[]{:S(2)}) %all-to-all-start.2) | async-done | bytes 122336 | tf_op jit(solution)/shard_map/all_to_all | solution.py:96
  121.9 13.8 %collective-permute-start.11 = (bf16[8,7644]{1,0:T(8,128)(2,1)S(1)}, bf16[8,7644]{1,0:T(8,128)(2,1)S(1)}, u32[]{:S(2)}, u32[]{:S(2)}) collective-permute-start(bf16[8,7644]{1,0:T(8,128)(2,1)S(1)} %bitcast.96), channel_id=1, source_target_pairs={{0,0},{1,8},{2,16},{3,24},{4,32},{5,40},{6,48},{7,56},{8,1},{9,9},... | collective-permute-start | bytes 366920 | tf_op jit(solution)/shard_map/ppermute | solution.py:97
  135.7 1.9 add_convert_fusion
  138.2 5.0 %collective-permute-done.11 = bf16[8,7644]{1,0:T(8,128)(2,1)S(1)} collective-permute-done((bf16[8,7644]{1,0:T(8,128)(2,1)S(1)}, bf16[8,7644]{1,0:T(8,128)(2,1)S(1)}, u32[]{:S(2)}, u32[]{:S(2)}) %collective-permute-start.11) | collective-permute-done | bytes 122336 | tf_op jit(solution)/shard_map/ppermute | solution.py:97
  144.1 2.1 collective-permute-start.12
  147.7 32.2 %collective-permute-done.12 = bf16[288,512]{1,0:T(8,128)(2,1)S(1)} collective-permute-done((bf16[288,512]{1,0:T(8,128)(2,1)S(1)}, bf16[288,512]{1,0:T(8,128)(2,1)S(1)}, u32[]{:S(2)}, u32[]{:S(2)}) %collective-permute-start.12) | collective-permute-done | bytes 294944 | tf_op jit(solution)/shard_map/ppermute | solution.py:53
  180.1 2.7 %fusion.6 = f32[2,112,512]{2,1,0:T(8,128)} fusion(pred[512,512]{1,0:T(8,128)(4,1)} %fusion.16, bf16[512,2,144]{0,2,1:T(8,128)(2,1)S(1)} %bitcast.90), kind=kOutput, calls=%fused_computation.19 | convolution fusion | flops 137887744 | bytes 1015808 | tf_op jit(solution)/shard_map/hts,shv->thv/dot_general | solution.py:123
  182.9 1.8 multiply_reduce_fusion
  184.8 1.9 collective-permute-start.14
  187.5 1.9 collective-permute-start.1
  189.4 1.9 collective-permute-start.2
  191.4 3.4 %collective-permute-start.3 = (bf16[2,224,224]{2,1,0:T(8,128)(2,1)}, bf16[2,224,224]{2,1,0:T(8,128)(2,1)}, u32[]{:S(2)}, u32[]{:S(2)}) collective-permute-start(bf16[2,224,224]{2,1,0:T(8,128)(2,1)} %broadcast_select_fusion.2), channel_id=1, source_target_pairs={{0,48},{16,0},{32,16},{48,32},{1,49},{17,1},{33,17},{49,33},{2,50}... | collective-permute-start | bytes 602120 | tf_op jit(solution)/shard_map/ppermute | solution.py:42
  194.7 13.2 %collective-permute-done.14 = bf16[512,224]{0,1:T(8,128)(2,1)S(1)} collective-permute-done((bf16[512,224]{0,1:T(8,128)(2,1)S(1)}, bf16[512,224]{0,1:T(8,128)(2,1)S(1)}, u32[]{:S(2)}, u32[]{:S(2)}) %collective-permute-start.14) | collective-permute-done | bytes 229408 | tf_op jit(solution)/shard_map/ppermute | solution.py:42
  209.5 1.9 collective-permute-start.15
  211.4 1.9 collective-permute-start.16
  213.3 3.4 %collective-permute-start.17 = (bf16[2,512,224]{1,2,0:T(8,128)(2,1)}, bf16[2,512,224]{1,2,0:T(8,128)(2,1)}, u32[]{:S(2)}, u32[]{:S(2)}) collective-permute-start(bf16[2,512,224]{1,2,0:T(8,128)(2,1)} %broadcast_select_fusion), channel_id=1, source_target_pairs={{0,6},{2,0},{4,2},{6,4},{1,7},{3,1},{5,3},{7,5},{8,14},{10,8},{12,... | collective-permute-start | bytes 1376264 | tf_op jit(solution)/shard_map/ppermute | solution.py:42
  216.8 1.4 pad_maximum_fusion.2
  218.2 1.7 gather_fusion.1
  219.9 2.2 copy.19
  222.2 1.1 collective-permute-done.15
  223.3 3.5 %collective-permute-done.16 = bf16[2,512,224]{1,2,0:T(8,128)(2,1)} collective-permute-done((bf16[2,512,224]{1,2,0:T(8,128)(2,1)}, bf16[2,512,224]{1,2,0:T(8,128)(2,1)}, u32[]{:S(2)}, u32[]{:S(2)}) %collective-permute-start.16) | collective-permute-done | bytes 458784 | tf_op jit(solution)/shard_map/ppermute | solution.py:42
  226.7 10.6 %collective-permute-done.17 = bf16[2,512,224]{1,2,0:T(8,128)(2,1)} collective-permute-done((bf16[2,512,224]{1,2,0:T(8,128)(2,1)}, bf16[2,512,224]{1,2,0:T(8,128)(2,1)}, u32[]{:S(2)}, u32[]{:S(2)}) %collective-permute-start.17) | collective-permute-done | bytes 458784 | tf_op jit(solution)/shard_map/ppermute | solution.py:42
  237.4 1.5 pad_maximum_fusion
  238.9 2.0 gather_fusion.6
  241.0 1.8 bitcast_select_fusion
  (115 shorter events, 26.8 us)
Async XLA Ops:
  0.0 4.3 %copy-start = (bf16[3,224,1024]{2,1,0:T(8,128)(2,1)S(1)}, bf16[3,224,1024]{2,1,0:T(8,128)(2,1)}, u32[]{:S(2)}) copy-start(bf16[3,224,1024]{2,1,0:T(8,128)(2,1)} %param.13) | copy-start | bytes 4128772
  4.3 0.6 copy-start.14
  7.8 19.3 %copy-start.7 = (bf16[224,288]{0,1:T(8,128)(2,1)S(1)}, bf16[224,288]{0,1:T(8,128)(2,1)}, u32[]{:S(2)}) copy-start(bf16[224,288]{0,1:T(8,128)(2,1)} %param.9) | copy-start | bytes 387076
  7.8 36.5 %copy-start.8 = (bf16[224,224]{1,0:T(8,128)(2,1)S(1)}, bf16[224,224]{1,0:T(8,128)(2,1)}, u32[]{:S(2)}) copy-start(bf16[224,224]{1,0:T(8,128)(2,1)} %param.10) | copy-start | bytes 301060
  9.5 64.4 %all-to-all-start = ((bf16[8,1,22935]{2,1,0:T(2,128)(2,1)}), bf16[8,1,22935]{2,1,0:T(2,128)(2,1)S(1)}, u32[]{:S(2)}, u32[]{:S(2)}) async-start(bf16[8,1,22935]{2,1,0:T(2,128)(2,1)} %copy.21), calls=%async_computation | async-start | bytes 1474560 | tf_op jit(solution)/shard_map/all_to_all | solution.py:85
  27.1 20.3 %collective-permute-start.4 = (bf16[224,288]{0,1:T(8,128)(2,1)S(1)}, bf16[224,288]{0,1:T(8,128)(2,1)S(1)}, u32[]{:S(2)}, u32[]{:S(2)}) collective-permute-start(bf16[224,288]{0,1:T(8,128)(2,1)S(1)} %copy-done.7), channel_id=1, source_target_pairs={{0,8},{8,0},{1,9},{9,1},{2,10},{10,2},{3,11},{11,3},{4,12},{12,4},... | collective-permute-start | bytes 387080 | tf_op jit(solution)/shard_map/ppermute | solution.py:42
  30.2 79.8 %collective-permute-start.13 = (f32[224]{0:T(256)}, f32[224]{0:T(256)}, u32[]{:S(2)}, u32[]{:S(2)}) collective-permute-start(f32[224]{0:T(256)} %param.11), channel_id=1, source_target_pairs={{0,0},{1,8},{2,16},{3,24},{4,32},{5,40},{6,48},{7,56},{8,1},{9,9},... | collective-permute-start | bytes 2696 | tf_op jit(solution)/shard_map/ppermute | solution.py:127
  44.3 66.4 %collective-permute-start = (bf16[224,224]{1,0:T(8,128)(2,1)S(1)}, bf16[224,224]{1,0:T(8,128)(2,1)}, u32[]{:S(2)}, u32[]{:S(2)}) collective-permute-start(bf16[224,224]{1,0:T(8,128)(2,1)S(1)} %copy-done.8), channel_id=1, source_target_pairs={{0,8},{8,0},{1,9},{9,1},{2,10},{10,2},{3,11},{11,3},{4,12},{12,4},... | collective-permute-start | bytes 301064 | tf_op jit(solution)/shard_map/ppermute | solution.py:42
  46.8 25.2 %copy-start.9 = (pred[2]{0:T(512)(128)(4,1)}, pred[2]{0:T(512)(128)(4,1)S(1)}, u32[]{:S(2)}) copy-start(pred[2]{0:T(512)(128)(4,1)S(1)} %get-tuple-element.17) | copy-start | bytes 10
  47.4 24.7 %copy-start.11 = (s32[1024]{0:T(1024)}, s32[1024]{0:T(1024)S(1)}, u32[]{:S(2)}) copy-start(s32[1024]{0:T(1024)S(1)} %pad_clamp_fusion.4) | copy-start | bytes 12292
  47.4 24.6 %copy-start.12 = (s32[1024]{0:T(1024)}, s32[1024]{0:T(1024)S(1)}, u32[]{:S(2)}) copy-start(s32[1024]{0:T(1024)S(1)} %pad_clamp_fusion.3) | copy-start | bytes 12292
  48.9 10.2 %collective-permute-start.5 = (bf16[2,224,288]{1,2,0:T(8,128)(2,1)}, bf16[2,224,288]{1,2,0:T(8,128)(2,1)S(1)}, u32[]{:S(2)}, u32[]{:S(2)}) collective-permute-start(bf16[2,224,288]{1,2,0:T(8,128)(2,1)} %broadcast_select_fusion.1), channel_id=1, source_target_pairs={{0,16},{16,32},{32,48},{48,0},{1,17},{17,33},{33,49},{49,1},{2,18}... | collective-permute-start | bytes 774152 | tf_op jit(solution)/shard_map/ppermute | solution.py:42
  50.8 11.7 %collective-permute-start.6 = (bf16[2,224,288]{1,2,0:T(8,128)(2,1)}, bf16[2,224,288]{1,2,0:T(8,128)(2,1)S(1)}, u32[]{:S(2)}, u32[]{:S(2)}) collective-permute-start(bf16[2,224,288]{1,2,0:T(8,128)(2,1)} %broadcast_select_fusion.1), channel_id=1, source_target_pairs={{0,32},{16,48},{32,0},{48,16},{1,33},{17,49},{33,1},{49,17},{2,34}... | collective-permute-start | bytes 774152 | tf_op jit(solution)/shard_map/ppermute | solution.py:42
  53.5 16.2 %collective-permute-start.7 = (bf16[2,224,288]{1,2,0:T(8,128)(2,1)}, bf16[2,224,288]{1,2,0:T(8,128)(2,1)}, u32[]{:S(2)}, u32[]{:S(2)}) collective-permute-start(bf16[2,224,288]{1,2,0:T(8,128)(2,1)} %broadcast_select_fusion.1), channel_id=1, source_target_pairs={{0,48},{16,0},{32,16},{48,32},{1,49},{17,1},{33,17},{49,33},{2,50}... | collective-permute-start | bytes 774152 | tf_op jit(solution)/shard_map/ppermute | solution.py:42
  74.0 0.7 copy-start.2
  75.1 6.5 %copy-start.4 = (bf16[224,512]{1,0:T(8,128)(2,1)S(1)}, bf16[224,512]{1,0:T(8,128)(2,1)}, u32[]{:S(2)}) copy-start(bf16[224,512]{1,0:T(8,128)(2,1)} %param.8) | copy-start | bytes 688132
  76.0 25.0 %all-to-all-start.1 = ((bf16[8,3,7644]{2,1,0:T(4,128)(2,1)}), bf16[8,3,7644]{2,1,0:T(4,128)(2,1)S(1)}, u32[]{:S(2)}, u32[]{:S(2)}) async-start(bf16[8,3,7644]{2,1,0:T(4,128)(2,1)} %broadcast_in_dim.167), calls=%async_computation.1 | async-start | bytes 983040 | tf_op jit(solution)/shard_map/all_to_all | solution.py:93
  82.4 1.4 copy-start.1
  85.1 23.6 %copy-start.17 = (s32[2]{0:T(128)S(1)}, s32[2]{0:T(128)}, u32[]{:S(2)}) copy-start(s32[2]{0:T(128)} %fusion.43) | copy-start | bytes 28
  85.1 24.2 %copy-start.18 = (pred[4]{0:T(512)(128)(4,1)S(1)}, pred[4]{0:T(512)(128)(4,1)}, u32[]{:S(2)}) copy-start(pred[4]{0:T(512)(128)(4,1)} %get-tuple-element.18) | copy-start | bytes 16
  85.1 50.6 %collective-permute-start.10 = (bf16[576,512]{1,0:T(8,128)(2,1)}, bf16[576,512]{1,0:T(8,128)(2,1)}, u32[]{:S(2)}, u32[]{:S(2)}) collective-permute-start(bf16[576,512]{1,0:T(8,128)(2,1)} %get-tuple-element.10), channel_id=1, source_target_pairs={{0,6},{2,0},{4,2},{6,4},{1,7},{3,1},{5,3},{7,5},{8,14},{10,8},{12,... | collective-permute-start | bytes 1769480 | tf_op jit(solution)/shard_map/ppermute | solution.py:53
  87.1 48.6 %collective-permute-start.8 = (bf16[576,512]{1,0:T(8,128)(2,1)}, bf16[576,512]{1,0:T(8,128)(2,1)}, u32[]{:S(2)}, u32[]{:S(2)}) collective-permute-start(bf16[576,512]{1,0:T(8,128)(2,1)} %get-tuple-element.9), channel_id=1, source_target_pairs={{0,2},{2,4},{4,6},{6,0},{1,3},{3,5},{5,7},{7,1},{8,10},{10,12},{12... | collective-permute-start | bytes 1769480 | tf_op jit(solution)/shard_map/ppermute | solution.py:53
  90.5 45.2 %collective-permute-start.9 = (bf16[576,512]{1,0:T(8,128)(2,1)}, bf16[576,512]{1,0:T(8,128)(2,1)}, u32[]{:S(2)}, u32[]{:S(2)}) collective-permute-start(bf16[576,512]{1,0:T(8,128)(2,1)} %get-tuple-element.11), channel_id=1, source_target_pairs={{0,4},{2,6},{4,0},{6,2},{1,5},{3,7},{5,1},{7,3},{8,12},{10,14},{12... | collective-permute-start | bytes 1769480 | tf_op jit(solution)/shard_map/ppermute | solution.py:53
  104.1 17.6 %all-to-all-start.2 = ((bf16[8,2,3822]{2,1,0:T(2,128)(2,1)}), bf16[8,2,3822]{2,1,0:T(2,128)(2,1)S(1)}, u32[]{:S(2)}, u32[]{:S(2)}) async-start(bf16[8,2,3822]{2,1,0:T(2,128)(2,1)} %reshape.489), calls=%async_computation.2 | async-start | bytes 245760 | tf_op jit(solution)/shard_map/all_to_all | solution.py:96
  121.9 21.2 %collective-permute-start.11 = (bf16[8,7644]{1,0:T(8,128)(2,1)S(1)}, bf16[8,7644]{1,0:T(8,128)(2,1)S(1)}, u32[]{:S(2)}, u32[]{:S(2)}) collective-permute-start(bf16[8,7644]{1,0:T(8,128)(2,1)S(1)} %bitcast.96), channel_id=1, source_target_pairs={{0,0},{1,8},{2,16},{3,24},{4,32},{5,40},{6,48},{7,56},{8,1},{9,9},... | collective-permute-start | bytes 366920 | tf_op jit(solution)/shard_map/ppermute | solution.py:97
  144.1 35.7 %collective-permute-start.12 = (bf16[288,512]{1,0:T(8,128)(2,1)S(1)}, bf16[288,512]{1,0:T(8,128)(2,1)S(1)}, u32[]{:S(2)}, u32[]{:S(2)}) collective-permute-start(bf16[288,512]{1,0:T(8,128)(2,1)S(1)} %constant_dynamic-slice_fusion), channel_id=1, source_target_pairs={{0,1},{1,0},{2,3},{3,2},{4,5},{5,4},{6,7},{7,6},{8,9},{9,8},{10,11... | collective-permute-start | bytes 884744 | tf_op jit(solution)/shard_map/ppermute | solution.py:53
  180.1 2.8 %copy-start.6 = (f32[2,273,112]{2,1,0:T(8,128)S(1)}, f32[2,273,112]{2,1,0:T(8,128)}, u32[]{:S(2)}) copy-start(f32[2,273,112]{2,1,0:T(8,128)} %reshape.426) | copy-start | bytes 733828
  180.1 2.8 %copy-start.15 = (bf16[273]{0:T(512)(128)(2,1)S(1)}, bf16[273]{0:T(512)(128)(2,1)}, u32[]{:S(2)}) copy-start(bf16[273]{0:T(512)(128)(2,1)} %copy-done.14) | copy-start | bytes 1642
  182.8 3.9 %copy-start.10 = (pred[2]{0:T(512)(128)(4,1)S(1)}, pred[2]{0:T(512)(128)(4,1)}, u32[]{:S(2)}) copy-start(pred[2]{0:T(512)(128)(4,1)} %copy-done.9) | copy-start | bytes 10
  184.7 23.9 %copy-start.13 = (pred[2]{0:T(512)(128)(4,1)S(1)}, pred[2]{0:T(512)(128)(4,1)}, u32[]{:S(2)}) copy-start(pred[2]{0:T(512)(128)(4,1)} %get-tuple-element.16) | copy-start | bytes 10
  184.8 23.2 %collective-permute-start.14 = (bf16[512,224]{0,1:T(8,128)(2,1)S(1)}, bf16[512,224]{0,1:T(8,128)(2,1)S(1)}, u32[]{:S(2)}, u32[]{:S(2)}) collective-permute-start(bf16[512,224]{0,1:T(8,128)(2,1)S(1)} %bitcast.82), channel_id=1, source_target_pairs={{0,1},{1,0},{2,3},{3,2},{4,5},{5,4},{6,7},{7,6},{8,9},{9,8},{10,11... | collective-permute-start | bytes 688136 | tf_op jit(solution)/shard_map/ppermute | solution.py:42
  187.5 25.8 %collective-permute-start.1 = (bf16[2,224,224]{2,1,0:T(8,128)(2,1)}, bf16[2,224,224]{2,1,0:T(8,128)(2,1)}, u32[]{:S(2)}, u32[]{:S(2)}) collective-permute-start(bf16[2,224,224]{2,1,0:T(8,128)(2,1)} %broadcast_select_fusion.2), channel_id=1, source_target_pairs={{0,16},{16,32},{32,48},{48,0},{1,17},{17,33},{33,49},{49,1},{2,18}... | collective-permute-start | bytes 602120 | tf_op jit(solution)/shard_map/ppermute | solution.py:42
  189.4 27.4 %collective-permute-start.2 = (bf16[2,224,224]{2,1,0:T(8,128)(2,1)}, bf16[2,224,224]{2,1,0:T(8,128)(2,1)}, u32[]{:S(2)}, u32[]{:S(2)}) collective-permute-start(bf16[2,224,224]{2,1,0:T(8,128)(2,1)} %broadcast_select_fusion.2), channel_id=1, source_target_pairs={{0,32},{16,48},{32,0},{48,16},{1,33},{17,49},{33,1},{49,17},{2,34}... | collective-permute-start | bytes 602120 | tf_op jit(solution)/shard_map/ppermute | solution.py:42
  191.4 25.5 %collective-permute-start.3 = (bf16[2,224,224]{2,1,0:T(8,128)(2,1)}, bf16[2,224,224]{2,1,0:T(8,128)(2,1)}, u32[]{:S(2)}, u32[]{:S(2)}) collective-permute-start(bf16[2,224,224]{2,1,0:T(8,128)(2,1)} %broadcast_select_fusion.2), channel_id=1, source_target_pairs={{0,48},{16,0},{32,16},{48,32},{1,49},{17,1},{33,17},{49,33},{2,50}... | collective-permute-start | bytes 602120 | tf_op jit(solution)/shard_map/ppermute | solution.py:42
  209.5 13.8 %collective-permute-start.15 = (bf16[2,512,224]{1,2,0:T(8,128)(2,1)}, bf16[2,512,224]{1,2,0:T(8,128)(2,1)S(1)}, u32[]{:S(2)}, u32[]{:S(2)}) collective-permute-start(bf16[2,512,224]{1,2,0:T(8,128)(2,1)} %broadcast_select_fusion), channel_id=1, source_target_pairs={{0,2},{2,4},{4,6},{6,0},{1,3},{3,5},{5,7},{7,1},{8,10},{10,12},{12... | collective-permute-start | bytes 1376264 | tf_op jit(solution)/shard_map/ppermute | solution.py:42
  211.4 15.3 %collective-permute-start.16 = (bf16[2,512,224]{1,2,0:T(8,128)(2,1)}, bf16[2,512,224]{1,2,0:T(8,128)(2,1)}, u32[]{:S(2)}, u32[]{:S(2)}) collective-permute-start(bf16[2,512,224]{1,2,0:T(8,128)(2,1)} %broadcast_select_fusion), channel_id=1, source_target_pairs={{0,4},{2,6},{4,0},{6,2},{1,5},{3,7},{5,1},{7,3},{8,12},{10,14},{12... | collective-permute-start | bytes 1376264 | tf_op jit(solution)/shard_map/ppermute | solution.py:42
  213.3 24.0 %collective-permute-start.17 = (bf16[2,512,224]{1,2,0:T(8,128)(2,1)}, bf16[2,512,224]{1,2,0:T(8,128)(2,1)}, u32[]{:S(2)}, u32[]{:S(2)}) collective-permute-start(bf16[2,512,224]{1,2,0:T(8,128)(2,1)} %broadcast_select_fusion), channel_id=1, source_target_pairs={{0,6},{2,0},{4,2},{6,4},{1,7},{3,1},{5,3},{7,5},{8,14},{10,8},{12,... | collective-permute-start | bytes 1376264 | tf_op jit(solution)/shard_map/ppermute | solution.py:42
  223.3 14.1 %copy-start.5 = (bf16[2,512,224]{1,2,0:T(8,128)(2,1)}, bf16[2,512,224]{1,2,0:T(8,128)(2,1)S(1)}, u32[]{:S(2)}) copy-start(bf16[2,512,224]{1,2,0:T(8,128)(2,1)S(1)} %collective-permute-done.15) | copy-start | bytes 1376260
  238.9 2.1 copy-start.19
  241.0 1.8 copy-start.3
  241.0 1.8 copy-start.16

commit v5 on v4

--- a/solution.py
+++ b/solution.py
@@ -56,6 +56,15 @@
     return total
 
 
+def gather_by_all_to_all(x, axis, n):
+    return lax.all_to_all(jnp.broadcast_to(x[None], (n,) + x.shape), axis, 0, 0, tiled=True)
+
+
+def reduce_scatter_by_all_to_all(x, axis, n):
+    got = lax.all_to_all(x.reshape((n, x.shape[0] // n) + x.shape[1:]), axis, 0, 0, tiled=True)
+    return jnp.sum(got.astype(jnp.float32), axis=0)
+
+
 def shards(
     tokens, qkv_weight, out_weight, head_gain, prefix_keys, prefix_values, suffix_len, prefix_owner
 ):
@@ -97,15 +106,17 @@
     chosen = lax.ppermute(chosen, flat, perm)
     chosen = chosen.reshape(state_shape).astype(jnp.float32)
 
-    weight_all = gather_by_shifts(gather_by_shifts(qkv_weight, "c", 2), "x", n_row // 2)
-    weight_all = weight_all.reshape((n_row,) + qkv_weight.shape)
+    weight_all = gather_by_all_to_all(qkv_weight, ROW, n_row)
+    out_w = gather_by_all_to_all(out_weight, ROW, n_row)
+    gains = lax.ppermute(head_gain, flat, perm)
     partial_proj = jnp.einsum(
         "kdj,dt->kjt", weight_all, tokens, preferred_element_type=jnp.float32
     ).astype(jnp.bfloat16)
     partial_proj = partial_proj.reshape(-1, tokens.shape[1])
-    partial_proj, to_send = lax.optimization_barrier((partial_proj, to_send))
-    projected = reduce_scatter_by_shifts(partial_proj, "y", n_col // 2).astype(jnp.bfloat16)
-    projected, chosen = lax.optimization_barrier((projected, chosen))
+    partial_proj, chosen, out_w, gains = lax.optimization_barrier(
+        (partial_proj, chosen, out_w, gains)
+    )
+    projected = reduce_scatter_by_all_to_all(partial_proj, "y", n_col // 2).astype(jnp.bfloat16)
     projected = reduce_scatter_by_shifts(projected, "zh", 2).astype(jnp.bfloat16)
     projected = projected.T.reshape(SLOTS, heads_here, 2 * FEAT + HD)
     queries = projected[..., :FEAT]
@@ -124,12 +135,10 @@
     active = (positions < length)[:, None, None]
     attended = jnp.where(active, carried + within, 0.0)
     inverse_rms = lax.rsqrt(jnp.mean(attended * attended, axis=-1, keepdims=True) + epsilon)
-    gains = lax.ppermute(head_gain, flat, perm).reshape(heads_here, HD)
+    gains = gains.reshape(heads_here, HD)
     normed = (attended * inverse_rms * gains).astype(jnp.bfloat16).reshape(SLOTS, heads_here * HD)
-    hidden = gather_by_shifts(gather_by_shifts(normed, "zh", 2), "y", n_col // 2)
+    hidden = gather_by_all_to_all(gather_by_shifts(normed, "zh", 2), "y", n_col // 2)
     hidden = hidden.reshape((n_col,) + normed.shape)
-    out_w = gather_by_shifts(gather_by_shifts(out_weight, "c", 2), "x", n_row // 2)
-    out_w = out_w.reshape((n_row,) + out_weight.shape)
     blocks = jnp.einsum("ktd,kde->ket", hidden, out_w, preferred_element_type=jnp.float32)
     mixed_sums = jnp.sum(blocks.astype(jnp.bfloat16).astype(jnp.float32), axis=0)
     return (tokens.astype(jnp.float32) + mixed_sums).astype(jnp.bfloat16)

time: 245 us -> 295 us (1.20)
  the two profiles are of different devices: /device:TPU:15 before, /device:TPU:1 now
where the time goes in v5:
time: 295 us; the launch traced here: 292 us
  waiting for transfers between devices  106 us (36%)
  starting transfers between devices  81.7 us (28%)
  blocking collectives  73 us (25%)
  matrix products  9.81 us (3%)
  local copies, waits for them, and re-layouts  9.5 us (3%)
  other arithmetic  9.35 us (3%)
    all_to_all x1, blocking collectives, shards(): lax.all_to_all(jnp.concatenate([pieces, meta], axis=1), COL, 0, 0, tiled=...  43.6 us
    all_to_all x1, blocking collectives, gather_by_all_to_all(): lax.all_to_all(jnp.broadcast_to(x[None], (n,) + x.shape), axis, 0, 0, til...  29.4 us
    ppermute x1, waiting for transfers between devices, reduce_scatter_by_shifts(): lax.ppermute(part, axis, [(i, (i + k) % n) for i in range(n)])  28.5 us
    all_to_all x1, starting transfers between devices, shards(): pieces = lax.all_to_all(pieces, 'req', 0, 0, tiled=True)  23 us
    all_to_all x1, waiting for transfers between devices, reduce_scatter_by_all_to_all(): lax.all_to_all(x.reshape((n, x.shape[0] // n) + x.shape[1:]), axis, 0, 0,...  20.9 us
    all_to_all x1, waiting for transfers between devices, shards(): pieces = lax.all_to_all(pieces, 'req', 0, 0, tiled=True)  19.6 us
    all_to_all x2, starting transfers between devices, gather_by_all_to_all(): lax.all_to_all(jnp.broadcast_to(x[None], (n,) + x.shape), axis, 0, 0, til...  19 us
    all_to_all x1, waiting for transfers between devices, shards(): chosen = lax.all_to_all(to_send, COL, 0, 0, tiled=True)  14 us
  transfers between devices with their start and end apart: 9, of which 7 were waited for; matrix products, arithmetic and copies ran while one was open for 3% of the time, Pallas kernels for 0%

profile of v5, /device:TPU:1, one launch (start us, length us, event | category | flops | bytes accessed | tf_op | source)
XLA Modules:
  0.0 291.6 jit_solution(3371493067798773655)
XLA Ops:
  0.8 1.0 convert.40
  1.7 1.0 multiply_convert_fusion.3
  3.4 0.9 multiply_convert_fusion
  4.3 1.3 fusion.7
  5.6 0.9 reshape.239
  6.6 0.3 copy.19
  6.8 0.4 reshape.240
  7.5 0.6 copy.20
  8.0 43.6 %all_to_all.46 = bf16[8,1,22935]{2,1,0:T(2,128)(2,1)S(1)} all-to-all(bf16[8,1,22935]{2,1,0:T(2,128)(2,1)S(1)} %copy.20), channel_id=1, replica_groups=mesh['req'=8,'x'=4,'c'=2,'y'=4,'zh'=2] {'y','zh'}, dimensions={0} | all-to-all | bytes 733920 | tf_op jit(solution)/shard_map/all_to_all | solution.py:94
  51.7 0.2 slice_reduce_fusion
  52.1 0.9 broadcast_in_dim.97
  53.0 23.0 %all-to-all-start.2 = ((bf16[8,3,7644]{2,1,0:T(4,128)(2,1)}), bf16[8,3,7644]{2,1,0:T(4,128)(2,1)S(1)}, u32[]{:S(2)}, u32[]{:S(2)}) async-start(bf16[8,3,7644]{2,1,0:T(4,128)(2,1)} %broadcast_in_dim.97), calls=%async_computation.2 | async-start | bytes 983040 | tf_op jit(solution)/shard_map/all_to_all | solution.py:102
  76.3 19.6 %all-to-all-done.2 = bf16[8,3,7644]{2,1,0:T(4,128)(2,1)S(1)} async-done(((bf16[8,3,7644]{2,1,0:T(4,128)(2,1)}), bf16[8,3,7644]{2,1,0:T(4,128)(2,1)S(1)}, u32[]{:S(2)}, u32[]{:S(2)}) %all-to-all-start.2) | async-done | bytes 366944 | tf_op jit(solution)/shard_map/all_to_all | solution.py:102
  95.9 1.1 broadcast_in_dim.92
  97.0 12.8 %all-to-all-start = ((bf16[8,224,288]{1,2,0:T(8,128)(2,1)}), bf16[8,224,288]{1,2,0:T(8,128)(2,1)S(1)}, u32[]{:S(2)}, u32[]{:S(2)}) async-start(bf16[8,224,288]{1,2,0:T(8,128)(2,1)} %broadcast_in_dim.92), calls=%async_computation | async-start | bytes 2359296 | tf_op jit(solution)/shard_map/all_to_all | solution.py:60
  109.7 0.3 reshape.241
  110.1 0.6 gather_fusion
  110.8 0.5 broadcast.238
  111.3 0.7 reduce.7
  112.0 0.8 reshape.270
  112.8 13.3 %all-to-all-done = bf16[8,224,288]{1,2,0:T(8,128)(2,1)S(1)} async-done(((bf16[8,224,288]{1,2,0:T(8,128)(2,1)}), bf16[8,224,288]{1,2,0:T(8,128)(2,1)S(1)}, u32[]{:S(2)}, u32[]{:S(2)}) %all-to-all-start) | async-done | bytes 1032224 | tf_op jit(solution)/shard_map/all_to_all | solution.py:60
  126.1 3.4 %all-to-all-start.3 = ((bf16[8,2,3822]{2,1,0:T(2,128)(2,1)}), bf16[8,2,3822]{2,1,0:T(2,128)(2,1)S(1)}, u32[]{:S(2)}, u32[]{:S(2)}) async-start(bf16[8,2,3822]{2,1,0:T(2,128)(2,1)} %reshape.270), calls=%async_computation.3 | async-start | bytes 245760 | tf_op jit(solution)/shard_map/all_to_all | solution.py:105
  129.6 14.0 %all-to-all-done.3 = bf16[8,2,3822]{2,1,0:T(2,128)(2,1)S(1)} async-done(((bf16[8,2,3822]{2,1,0:T(2,128)(2,1)}), bf16[8,2,3822]{2,1,0:T(2,128)(2,1)S(1)}, u32[]{:S(2)}, u32[]{:S(2)}) %all-to-all-start.3) | async-done | bytes 122336 | tf_op jit(solution)/shard_map/all_to_all | solution.py:105
  143.6 1.0 broadcast_in_dim.99
  144.6 6.2 %all-to-all-start.4 = ((bf16[8,224,224]{1,2,0:T(8,128)(2,1)}), bf16[8,224,224]{1,2,0:T(8,128)(2,1)}, u32[]{:S(2)}, u32[]{:S(2)}) async-start(bf16[8,224,224]{1,2,0:T(8,128)(2,1)} %broadcast_in_dim.99), calls=%async_computation.4 | async-start | bytes 1835008 | tf_op jit(solution)/shard_map/all_to_all | solution.py:60
  150.9 2.4 collective-permute-start.1
  153.3 0.2 reshape.271
  153.5 11.9 %collective-permute-start = (bf16[8,7644]{1,0:T(8,128)(2,1)S(1)}, bf16[8,7644]{1,0:T(8,128)(2,1)S(1)}, u32[]{:S(2)}, u32[]{:S(2)}) collective-permute-start(bf16[8,7644]{1,0:T(8,128)(2,1)S(1)} %bitcast.63), channel_id=1, source_target_pairs={{0,0},{1,8},{2,16},{3,24},{4,32},{5,40},{6,48},{7,56},{8,1},{9,9},... | collective-permute-start | bytes 366920 | tf_op jit(solution)/shard_map/ppermute | solution.py:106
  165.4 2.2 convolution_convert_fusion
  167.6 0.8 collective-permute-done
  168.4 0.2 reshape.247
  168.7 12.2 %all-to-all-start.5 = ((bf16[4,576,512]{2,1,0:T(8,128)(2,1)}), bf16[4,576,512]{2,1,0:T(8,128)(2,1)}, u32[]{:S(2)}, u32[]{:S(2)}) async-start(bf16[4,576,512]{2,1,0:T(8,128)(2,1)} %bitcast.48), calls=%async_computation.5 | async-start | bytes 4718592 | tf_op jit(solution)/shard_map/all_to_all | solution.py:64
  180.8 0.5 constant_dynamic-slice_fusion.1
  181.3 20.9 %all-to-all-done.5 = bf16[4,576,512]{2,1,0:T(8,128)(2,1)} async-done(((bf16[4,576,512]{2,1,0:T(8,128)(2,1)}), bf16[4,576,512]{2,1,0:T(8,128)(2,1)}, u32[]{:S(2)}, u32[]{:S(2)}) %all-to-all-start.5) | async-done | bytes 2359328 | tf_op jit(solution)/shard_map/all_to_all | solution.py:64
  202.3 2.3 reduce_sum.43
  204.6 1.9 collective-permute-start.2
  206.6 0.7 iota_compare_fusion.1
  207.2 0.8 fusion.16
  208.1 28.5 %collective-permute-done.2 = bf16[288,512]{1,0:T(8,128)(2,1)S(1)} collective-permute-done((bf16[288,512]{1,0:T(8,128)(2,1)S(1)}, bf16[288,512]{1,0:T(8,128)(2,1)S(1)}, u32[]{:S(2)}, u32[]{:S(2)}) %collective-permute-start.2) | collective-permute-done | bytes 294944 | tf_op jit(solution)/shard_map/ppermute | solution.py:53
  236.8 2.7 fusion.6
  239.5 1.8 multiply_reduce_fusion
  241.4 8.1 %collective-permute-start.3 = (bf16[512,224]{0,1:T(8,128)(2,1)S(1)}, bf16[512,224]{0,1:T(8,128)(2,1)S(1)}, u32[]{:S(2)}, u32[]{:S(2)}) collective-permute-start(bf16[512,224]{0,1:T(8,128)(2,1)S(1)} %bitcast.54), channel_id=1, source_target_pairs={{0,1},{1,0},{2,3},{3,2},{4,5},{5,4},{6,7},{7,6},{8,9},{9,8},{10,11... | collective-permute-start | bytes 688136 | tf_op jit(solution)/shard_map/ppermute | solution.py:42
  249.5 9.2 %collective-permute-done.3 = bf16[512,224]{0,1:T(8,128)(2,1)S(1)} collective-permute-done((bf16[512,224]{0,1:T(8,128)(2,1)S(1)}, bf16[512,224]{0,1:T(8,128)(2,1)S(1)}, u32[]{:S(2)}, u32[]{:S(2)}) %collective-permute-start.3) | collective-permute-done | bytes 229408 | tf_op jit(solution)/shard_map/ppermute | solution.py:42
  258.8 0.6 gather_fusion.1
  259.5 0.2 broadcast_in_dim.107
  259.7 29.4 %all_to_all.47 = bf16[4,2,512,224]{2,3,1,0:T(8,128)(2,1)S(1)} all-to-all(bf16[4,2,512,224]{2,3,1,0:T(8,128)(2,1)S(1)} %broadcast_in_dim.107), channel_id=1, replica_groups=mesh['req'=8,'x'=4,'c'=2,'y'=4,'zh'=2] {'y'}, dimensions={0} | all-to-all | bytes 3670016 | tf_op jit(solution)/shard_map/all_to_all | solution.py:60
  289.0 1.8 convert_reduce_fusion
  290.9 0.8 add_convert_fusion.1
  (37 shorter events, 1.5 us)
Async XLA Ops:
  0.0 4.3 %copy-start = (bf16[3,224,1024]{2,1,0:T(8,128)(2,1)S(1)}, bf16[3,224,1024]{2,1,0:T(8,128)(2,1)}, u32[]{:S(2)}) copy-start(bf16[3,224,1024]{2,1,0:T(8,128)(2,1)} %param.13) | copy-start | bytes 4128772
  8.0 87.8 %copy-start.2 = (bf16[224,288]{0,1:T(8,128)(2,1)S(1)}, bf16[224,288]{0,1:T(8,128)(2,1)}, u32[]{:S(2)}) copy-start(bf16[224,288]{0,1:T(8,128)(2,1)} %param.9) | copy-start | bytes 387076
  53.0 42.9 %all-to-all-start.2 = ((bf16[8,3,7644]{2,1,0:T(4,128)(2,1)}), bf16[8,3,7644]{2,1,0:T(4,128)(2,1)S(1)}, u32[]{:S(2)}, u32[]{:S(2)}) async-start(bf16[8,3,7644]{2,1,0:T(4,128)(2,1)} %broadcast_in_dim.97), calls=%async_computation.2 | async-start | bytes 983040 | tf_op jit(solution)/shard_map/all_to_all | solution.py:102
  97.0 32.5 %copy-start.3 = (bf16[224,224]{1,0:T(8,128)(2,1)S(1)}, bf16[224,224]{1,0:T(8,128)(2,1)}, u32[]{:S(2)}) copy-start(bf16[224,224]{1,0:T(8,128)(2,1)} %param.10) | copy-start | bytes 301060
  97.0 29.2 %all-to-all-start = ((bf16[8,224,288]{1,2,0:T(8,128)(2,1)}), bf16[8,224,288]{1,2,0:T(8,128)(2,1)S(1)}, u32[]{:S(2)}, u32[]{:S(2)}) async-start(bf16[8,224,288]{1,2,0:T(8,128)(2,1)} %broadcast_in_dim.92), calls=%async_computation | async-start | bytes 2359296 | tf_op jit(solution)/shard_map/all_to_all | solution.py:60
  110.7 40.2 %copy-start.4 = (f32[224]{0:T(256)S(1)}, f32[224]{0:T(256)}, u32[]{:S(2)}) copy-start(f32[224]{0:T(256)} %param.11) | copy-start | bytes 2692
  112.8 52.6 %copy-start.1 = (bf16[224,512]{1,0:T(8,128)(2,1)S(1)}, bf16[224,512]{1,0:T(8,128)(2,1)}, u32[]{:S(2)}) copy-start(bf16[224,512]{1,0:T(8,128)(2,1)} %param.8) | copy-start | bytes 688132
  126.1 17.5 %all-to-all-start.3 = ((bf16[8,2,3822]{2,1,0:T(2,128)(2,1)}), bf16[8,2,3822]{2,1,0:T(2,128)(2,1)S(1)}, u32[]{:S(2)}, u32[]{:S(2)}) async-start(bf16[8,2,3822]{2,1,0:T(2,128)(2,1)} %reshape.270), calls=%async_computation.3 | async-start | bytes 245760 | tf_op jit(solution)/shard_map/all_to_all | solution.py:105
  144.6 24.0 %all-to-all-start.4 = ((bf16[8,224,224]{1,2,0:T(8,128)(2,1)}), bf16[8,224,224]{1,2,0:T(8,128)(2,1)}, u32[]{:S(2)}, u32[]{:S(2)}) async-start(bf16[8,224,224]{1,2,0:T(8,128)(2,1)} %broadcast_in_dim.99), calls=%async_computation.4 | async-start | bytes 1835008 | tf_op jit(solution)/shard_map/all_to_all | solution.py:60
  150.9 17.8 %collective-permute-start.1 = (f32[224]{0:T(256)S(1)}, f32[224]{0:T(256)S(1)}, u32[]{:S(2)}, u32[]{:S(2)}) collective-permute-start(f32[224]{0:T(256)S(1)} %copy-done.4), channel_id=1, source_target_pairs={{0,0},{1,8},{2,16},{3,24},{4,32},{5,40},{6,48},{7,56},{8,1},{9,9},... | collective-permute-start | bytes 2696 | tf_op jit(solution)/shard_map/ppermute | solution.py:111
  153.5 14.9 %collective-permute-start = (bf16[8,7644]{1,0:T(8,128)(2,1)S(1)}, bf16[8,7644]{1,0:T(8,128)(2,1)S(1)}, u32[]{:S(2)}, u32[]{:S(2)}) collective-permute-start(bf16[8,7644]{1,0:T(8,128)(2,1)S(1)} %bitcast.63), channel_id=1, source_target_pairs={{0,0},{1,8},{2,16},{3,24},{4,32},{5,40},{6,48},{7,56},{8,1},{9,9},... | collective-permute-start | bytes 366920 | tf_op jit(solution)/shard_map/ppermute | solution.py:106
  168.7 33.6 %all-to-all-start.5 = ((bf16[4,576,512]{2,1,0:T(8,128)(2,1)}), bf16[4,576,512]{2,1,0:T(8,128)(2,1)}, u32[]{:S(2)}, u32[]{:S(2)}) async-start(bf16[4,576,512]{2,1,0:T(8,128)(2,1)} %bitcast.48), calls=%async_computation.5 | async-start | bytes 4718592 | tf_op jit(solution)/shard_map/all_to_all | solution.py:64
  204.6 31.9 %collective-permute-start.2 = (bf16[288,512]{1,0:T(8,128)(2,1)S(1)}, bf16[288,512]{1,0:T(8,128)(2,1)S(1)}, u32[]{:S(2)}, u32[]{:S(2)}) collective-permute-start(bf16[288,512]{1,0:T(8,128)(2,1)S(1)} %constant_dynamic-slice_fusion), channel_id=1, source_target_pairs={{0,1},{1,0},{2,3},{3,2},{4,5},{5,4},{6,7},{7,6},{8,9},{9,8},{10,11... | collective-permute-start | bytes 884744 | tf_op jit(solution)/shard_map/ppermute | solution.py:53
  241.4 17.3 %collective-permute-start.3 = (bf16[512,224]{0,1:T(8,128)(2,1)S(1)}, bf16[512,224]{0,1:T(8,128)(2,1)S(1)}, u32[]{:S(2)}, u32[]{:S(2)}) collective-permute-start(bf16[512,224]{0,1:T(8,128)(2,1)S(1)} %bitcast.54), channel_id=1, source_target_pairs={{0,1},{1,0},{2,3},{3,2},{4,5},{5,4},{6,7},{7,6},{8,9},{9,8},{10,11... | collective-permute-start | bytes 688136 | tf_op jit(solution)/shard_map/ppermute | solution.py:42

commit v6 on v4

--- a/solution.py
+++ b/solution.py
@@ -97,8 +97,11 @@
     chosen = lax.ppermute(chosen, flat, perm)
     chosen = chosen.reshape(state_shape).astype(jnp.float32)
 
-    weight_all = gather_by_shifts(gather_by_shifts(qkv_weight, "c", 2), "x", n_row // 2)
-    weight_all = weight_all.reshape((n_row,) + qkv_weight.shape)
+    both = jnp.concatenate([qkv_weight, out_weight], axis=1)
+    both = gather_by_shifts(gather_by_shifts(both, "c", 2), "x", n_row // 2)
+    both = both.reshape((n_row,) + both.shape[2:])
+    weight_all = both[:, :, : qkv_weight.shape[1]]
+    out_w = both[:, :, qkv_weight.shape[1] :]
     partial_proj = jnp.einsum(
         "kdj,dt->kjt", weight_all, tokens, preferred_element_type=jnp.float32
     ).astype(jnp.bfloat16)
@@ -128,8 +131,6 @@
     normed = (attended * inverse_rms * gains).astype(jnp.bfloat16).reshape(SLOTS, heads_here * HD)
     hidden = gather_by_shifts(gather_by_shifts(normed, "zh", 2), "y", n_col // 2)
     hidden = hidden.reshape((n_col,) + normed.shape)
-    out_w = gather_by_shifts(gather_by_shifts(out_weight, "c", 2), "x", n_row // 2)
-    out_w = out_w.reshape((n_row,) + out_weight.shape)
     blocks = jnp.einsum("ktd,kde->ket", hidden, out_w, preferred_element_type=jnp.float32)
     mixed_sums = jnp.sum(blocks.astype(jnp.bfloat16).astype(jnp.float32), axis=0)
     return (tokens.astype(jnp.float32) + mixed_sums).astype(jnp.bfloat16)

time: 245 us -> 258 us (1.053)
  the two profiles are of different devices: /device:TPU:15 before, /device:TPU:1 now
where the time goes in v6:
time: 258 us; the launch traced here: 253 us
  starting transfers between devices  111 us (43%)
  waiting for transfers between devices  95.6 us (37%)
  local copies, waits for them, and re-layouts  22.4 us (9%)
  other arithmetic  15.9 us (6%)
  matrix products  5.75 us (2%)
    ppermute x8, waiting for transfers between devices, gather_by_shifts(): lax.ppermute(x, axis, [(i, (i + k) % n) for i in range(n)])  56.6 us
    ppermute x8, starting transfers between devices, gather_by_shifts(): lax.ppermute(x, axis, [(i, (i + k) % n) for i in range(n)])  36.9 us
    ppermute x4, waiting for transfers between devices, reduce_scatter_by_shifts(): lax.ppermute(part, axis, [(i, (i + k) % n) for i in range(n)])  30.4 us
    ppermute x1, starting transfers between devices, shards(): gains = lax.ppermute(head_gain, flat, perm).reshape(heads_here, HD)  20.9 us
    all_to_all x1, starting transfers between devices, shards(): pieces = lax.all_to_all(pieces, 'req', 0, 0, tiled=True)  13.9 us
    all_to_all x1, starting transfers between devices, shards(): lax.all_to_all(jnp.concatenate([pieces, meta], axis=1), COL, 0, 0, tiled=...  12.1 us
    ppermute x1, starting transfers between devices, shards(): chosen = lax.ppermute(chosen, flat, perm)  12.1 us
    ppermute x4, starting transfers between devices, reduce_scatter_by_shifts(): lax.ppermute(part, axis, [(i, (i + k) % n) for i in range(n)])  10.6 us
  transfers between devices with their start and end apart: 17, of which 10 were waited for; matrix products, arithmetic and copies ran while one was open for 10% of the time, Pallas kernels for 0%

profile of v6, /device:TPU:1, one launch (start us, length us, event | category | flops | bytes accessed | tf_op | source)
XLA Modules:
  0.0 252.6 jit_solution(4929258568520199199)
XLA Ops:
  0.0 1.1 copy.19
  1.1 1.0 fusion.50
  2.1 8.7 %collective-permute-start = (bf16[224,512]{0,1:T(8,128)(2,1)S(1)}, bf16[224,512]{0,1:T(8,128)(2,1)S(1)}, u32[]{:S(2)}, u32[]{:S(2)}) collective-permute-start(bf16[224,512]{0,1:T(8,128)(2,1)S(1)} %get-tuple-element.13), channel_id=1, source_target_pairs={{0,8},{8,0},{1,9},{9,1},{2,10},{10,2},{3,11},{11,3},{4,12},{12,4},... | collective-permute-start | bytes 688136 | tf_op jit(solution)/shard_map/ppermute | solution.py:42
  11.5 1.0 convert.39
  12.5 1.0 multiply_convert_fusion.3
  15.0 1.3 fusion.7
  16.4 0.9 reshape.409
  18.2 1.5 copy.21
  19.6 12.1 %all-to-all-start = ((bf16[8,1,22935]{2,1,0:T(2,128)(2,1)}), bf16[8,1,22935]{2,1,0:T(2,128)(2,1)}, u32[]{:S(2)}, u32[]{:S(2)}) async-start(bf16[8,1,22935]{2,1,0:T(2,128)(2,1)} %copy.21), calls=%async_computation | async-start | bytes 1474560 | tf_op jit(solution)/shard_map/all_to_all | solution.py:85
  32.8 3.1 %collective-permute-start.1 = (bf16[2,224,512]{1,2,0:T(8,128)(2,1)S(1)}, bf16[2,224,512]{1,2,0:T(8,128)(2,1)S(1)}, u32[]{:S(2)}, u32[]{:S(2)}) collective-permute-start(bf16[2,224,512]{1,2,0:T(8,128)(2,1)S(1)} %broadcast_select_fusion), channel_id=1, source_target_pairs={{0,16},{16,32},{32,48},{48,0},{1,17},{17,33},{33,49},{49,1},{2,18}... | collective-permute-start | bytes 1376264 | tf_op jit(solution)/shard_map/ppermute | solution.py:42
  35.9 4.4 %collective-permute-start.2 = (bf16[2,224,512]{1,2,0:T(8,128)(2,1)S(1)}, bf16[2,224,512]{1,2,0:T(8,128)(2,1)S(1)}, u32[]{:S(2)}, u32[]{:S(2)}) collective-permute-start(bf16[2,224,512]{1,2,0:T(8,128)(2,1)S(1)} %broadcast_select_fusion), channel_id=1, source_target_pairs={{0,32},{16,48},{32,0},{48,16},{1,33},{17,49},{33,1},{49,17},{2,34}... | collective-permute-start | bytes 1376264 | tf_op jit(solution)/shard_map/ppermute | solution.py:42
  40.3 3.1 %collective-permute-start.3 = (bf16[2,224,512]{1,2,0:T(8,128)(2,1)S(1)}, bf16[2,224,512]{1,2,0:T(8,128)(2,1)S(1)}, u32[]{:S(2)}, u32[]{:S(2)}) collective-permute-start(bf16[2,224,512]{1,2,0:T(8,128)(2,1)S(1)} %broadcast_select_fusion), channel_id=1, source_target_pairs={{0,48},{16,0},{32,16},{48,32},{1,49},{17,1},{33,17},{49,33},{2,50}... | collective-permute-start | bytes 1376264 | tf_op jit(solution)/shard_map/ppermute | solution.py:42
  43.5 5.7 %collective-permute-done.1 = bf16[2,224,512]{1,2,0:T(8,128)(2,1)S(1)} collective-permute-done((bf16[2,224,512]{1,2,0:T(8,128)(2,1)S(1)}, bf16[2,224,512]{1,2,0:T(8,128)(2,1)S(1)}, u32[]{:S(2)}, u32[]{:S(2)}) %collective-permute-start.1) | collective-permute-done | bytes 458784 | tf_op jit(solution)/shard_map/ppermute | solution.py:42
  49.2 12.1 %collective-permute-done.2 = bf16[2,224,512]{1,2,0:T(8,128)(2,1)S(1)} collective-permute-done((bf16[2,224,512]{1,2,0:T(8,128)(2,1)S(1)}, bf16[2,224,512]{1,2,0:T(8,128)(2,1)S(1)}, u32[]{:S(2)}, u32[]{:S(2)}) %collective-permute-start.2) | collective-permute-done | bytes 458784 | tf_op jit(solution)/shard_map/ppermute | solution.py:42
  61.3 1.3 collective-permute-done.3
  62.6 1.9 pad_maximum_fusion
  64.5 2.3 gather_fusion.1
  66.8 1.2 copy.27
  70.4 0.9 broadcast_in_dim.137
  71.3 13.9 %all-to-all-start.1 = ((bf16[8,3,7644]{2,1,0:T(4,128)(2,1)}), bf16[8,3,7644]{2,1,0:T(4,128)(2,1)}, u32[]{:S(2)}, u32[]{:S(2)}) async-start(bf16[8,3,7644]{2,1,0:T(4,128)(2,1)} %broadcast_in_dim.137), calls=%async_computation.1 | async-start | bytes 983040 | tf_op jit(solution)/shard_map/all_to_all | solution.py:93
  87.0 1.4 copy-done.1
  88.4 0.9 constant_dynamic-slice_fusion.3
  89.3 2.0 collective-permute-start.4
  91.4 3.7 %collective-permute-start.5 = (bf16[576,512]{1,0:T(8,128)(2,1)S(1)}, bf16[576,512]{1,0:T(8,128)(2,1)}, u32[]{:S(2)}, u32[]{:S(2)}) collective-permute-start(bf16[576,512]{1,0:T(8,128)(2,1)S(1)} %get-tuple-element.11), channel_id=1, source_target_pairs={{0,4},{2,6},{4,0},{6,2},{1,5},{3,7},{5,1},{7,3},{8,12},{10,14},{12... | collective-permute-start | bytes 1769480 | tf_op jit(solution)/shard_map/ppermute | solution.py:53
  95.1 2.8 %collective-permute-start.6 = (bf16[576,512]{1,0:T(8,128)(2,1)S(1)}, bf16[576,512]{1,0:T(8,128)(2,1)}, u32[]{:S(2)}, u32[]{:S(2)}) collective-permute-start(bf16[576,512]{1,0:T(8,128)(2,1)S(1)} %get-tuple-element.10), channel_id=1, source_target_pairs={{0,6},{2,0},{4,2},{6,4},{1,7},{3,1},{5,3},{7,5},{8,14},{10,8},{12,... | collective-permute-start | bytes 1769480 | tf_op jit(solution)/shard_map/ppermute | solution.py:53
  98.9 6.4 %all-to-all-done.1 = bf16[8,3,7644]{2,1,0:T(4,128)(2,1)} async-done(((bf16[8,3,7644]{2,1,0:T(4,128)(2,1)}), bf16[8,3,7644]{2,1,0:T(4,128)(2,1)}, u32[]{:S(2)}, u32[]{:S(2)}) %all-to-all-start.1) | async-done | bytes 366944 | tf_op jit(solution)/shard_map/all_to_all | solution.py:93
  105.3 1.3 reshape.412
  106.6 1.3 gather_fusion.2
  107.9 1.0 bitcast_select_fusion.4
  110.9 4.5 %all-to-all-start.2 = ((bf16[8,2,3822]{2,1,0:T(2,128)(2,1)}), bf16[8,2,3822]{2,1,0:T(2,128)(2,1)S(1)}, u32[]{:S(2)}, u32[]{:S(2)}) async-start(bf16[8,2,3822]{2,1,0:T(2,128)(2,1)} %reshape.463), calls=%async_computation.2 | async-start | bytes 245760 | tf_op jit(solution)/shard_map/all_to_all | solution.py:96
  115.4 20.9 %collective-permute-start.9 = (f32[224]{0:T(256)S(1)}, f32[224]{0:T(256)S(1)}, u32[]{:S(2)}, u32[]{:S(2)}) collective-permute-start(f32[224]{0:T(256)S(1)} %copy-done.6), channel_id=1, source_target_pairs={{0,0},{1,8},{2,16},{3,24},{4,32},{5,40},{6,48},{7,56},{8,1},{9,9},... | collective-permute-start | bytes 2696 | tf_op jit(solution)/shard_map/ppermute | solution.py:130
  136.3 1.5 collective-permute-done.9
  138.2 12.1 %collective-permute-start.7 = (bf16[8,7644]{1,0:T(8,128)(2,1)S(1)}, bf16[8,7644]{1,0:T(8,128)(2,1)}, u32[]{:S(2)}, u32[]{:S(2)}) collective-permute-start(bf16[8,7644]{1,0:T(8,128)(2,1)S(1)} %bitcast.89), channel_id=1, source_target_pairs={{0,0},{1,8},{2,16},{3,24},{4,32},{5,40},{6,48},{7,56},{8,1},{9,9},... | collective-permute-start | bytes 366920 | tf_op jit(solution)/shard_map/ppermute | solution.py:97
  150.3 1.7 add_convert_fusion
  153.2 1.1 reshape.416
  154.4 2.1 collective-permute-start.8
  157.2 30.4 %collective-permute-done.8 = bf16[288,512]{1,0:T(8,128)(2,1)S(1)} collective-permute-done((bf16[288,512]{1,0:T(8,128)(2,1)S(1)}, bf16[288,512]{1,0:T(8,128)(2,1)S(1)}, u32[]{:S(2)}, u32[]{:S(2)}) %collective-permute-start.8) | collective-permute-done | bytes 294944 | tf_op jit(solution)/shard_map/ppermute | solution.py:53
  187.9 1.0 fusion.6
  189.8 1.9 collective-permute-start.10
  191.9 23.2 %collective-permute-done.10 = bf16[512,224]{0,1:T(8,128)(2,1)S(1)} collective-permute-done((bf16[512,224]{0,1:T(8,128)(2,1)S(1)}, bf16[512,224]{0,1:T(8,128)(2,1)S(1)}, u32[]{:S(2)}, u32[]{:S(2)}) %collective-permute-start.10) | collective-permute-done | bytes 229408 | tf_op jit(solution)/shard_map/ppermute | solution.py:42
  215.8 1.9 collective-permute-start.11
  217.7 9.8 %collective-permute-start.12 = (bf16[2,512,224]{1,2,0:T(8,128)(2,1)S(1)}, bf16[2,512,224]{1,2,0:T(8,128)(2,1)S(1)}, u32[]{:S(2)}, u32[]{:S(2)}) collective-permute-start(bf16[2,512,224]{1,2,0:T(8,128)(2,1)S(1)} %broadcast_select_fusion.1), channel_id=1, source_target_pairs={{0,4},{2,6},{4,0},{6,2},{1,5},{3,7},{5,1},{7,3},{8,12},{10,14},{12... | collective-permute-start | bytes 1376264 | tf_op jit(solution)/shard_map/ppermute | solution.py:42
  227.6 4.0 %collective-permute-start.13 = (bf16[2,512,224]{1,2,0:T(8,128)(2,1)S(1)}, bf16[2,512,224]{1,2,0:T(8,128)(2,1)S(1)}, u32[]{:S(2)}, u32[]{:S(2)}) collective-permute-start(bf16[2,512,224]{1,2,0:T(8,128)(2,1)S(1)} %broadcast_select_fusion.1), channel_id=1, source_target_pairs={{0,6},{2,0},{4,2},{6,4},{1,7},{3,1},{5,3},{7,5},{8,14},{10,8},{12,... | collective-permute-start | bytes 1376264 | tf_op jit(solution)/shard_map/ppermute | solution.py:42
  231.7 11.7 %collective-permute-done.12 = bf16[2,512,224]{1,2,0:T(8,128)(2,1)S(1)} collective-permute-done((bf16[2,512,224]{1,2,0:T(8,128)(2,1)S(1)}, bf16[2,512,224]{1,2,0:T(8,128)(2,1)S(1)}, u32[]{:S(2)}, u32[]{:S(2)}) %collective-permute-start.12) | collective-permute-done | bytes 458784 | tf_op jit(solution)/shard_map/ppermute | solution.py:42
  243.4 2.7 %collective-permute-done.13 = bf16[2,512,224]{1,2,0:T(8,128)(2,1)S(1)} collective-permute-done((bf16[2,512,224]{1,2,0:T(8,128)(2,1)S(1)}, bf16[2,512,224]{1,2,0:T(8,128)(2,1)S(1)}, u32[]{:S(2)}, u32[]{:S(2)}) %collective-permute-start.13) | collective-permute-done | bytes 458784 | tf_op jit(solution)/shard_map/ppermute | solution.py:42
  246.3 1.9 gather_fusion.4
  248.2 1.7 bitcast_select_fusion.1
  250.0 1.9 convert_reduce_fusion
  (76 shorter events, 15.5 us)
Async XLA Ops:
  0.0 15.0 %copy-start = (bf16[3,224,1024]{2,1,0:T(8,128)(2,1)S(1)}, bf16[3,224,1024]{2,1,0:T(8,128)(2,1)}, u32[]{:S(2)}) copy-start(bf16[3,224,1024]{2,1,0:T(8,128)(2,1)} %param.13) | copy-start | bytes 4128772
  2.1 29.9 %collective-permute-start = (bf16[224,512]{0,1:T(8,128)(2,1)S(1)}, bf16[224,512]{0,1:T(8,128)(2,1)S(1)}, u32[]{:S(2)}, u32[]{:S(2)}) collective-permute-start(bf16[224,512]{0,1:T(8,128)(2,1)S(1)} %get-tuple-element.13), channel_id=1, source_target_pairs={{0,8},{8,0},{1,9},{9,1},{2,10},{10,2},{3,11},{11,3},{4,12},{12,4},... | collective-permute-start | bytes 688136 | tf_op jit(solution)/shard_map/ppermute | solution.py:42
  19.6 47.1 %all-to-all-start = ((bf16[8,1,22935]{2,1,0:T(2,128)(2,1)}), bf16[8,1,22935]{2,1,0:T(2,128)(2,1)}, u32[]{:S(2)}, u32[]{:S(2)}) async-start(bf16[8,1,22935]{2,1,0:T(2,128)(2,1)} %copy.21), calls=%async_computation | async-start | bytes 1474560 | tf_op jit(solution)/shard_map/all_to_all | solution.py:85
  32.8 16.4 %collective-permute-start.1 = (bf16[2,224,512]{1,2,0:T(8,128)(2,1)S(1)}, bf16[2,224,512]{1,2,0:T(8,128)(2,1)S(1)}, u32[]{:S(2)}, u32[]{:S(2)}) collective-permute-start(bf16[2,224,512]{1,2,0:T(8,128)(2,1)S(1)} %broadcast_select_fusion), channel_id=1, source_target_pairs={{0,16},{16,32},{32,48},{48,0},{1,17},{17,33},{33,49},{49,1},{2,18}... | collective-permute-start | bytes 1376264 | tf_op jit(solution)/shard_map/ppermute | solution.py:42
  35.9 25.4 %collective-permute-start.2 = (bf16[2,224,512]{1,2,0:T(8,128)(2,1)S(1)}, bf16[2,224,512]{1,2,0:T(8,128)(2,1)S(1)}, u32[]{:S(2)}, u32[]{:S(2)}) collective-permute-start(bf16[2,224,512]{1,2,0:T(8,128)(2,1)S(1)} %broadcast_select_fusion), channel_id=1, source_target_pairs={{0,32},{16,48},{32,0},{48,16},{1,33},{17,49},{33,1},{49,17},{2,34}... | collective-permute-start | bytes 1376264 | tf_op jit(solution)/shard_map/ppermute | solution.py:42
  40.3 22.3 %collective-permute-start.3 = (bf16[2,224,512]{1,2,0:T(8,128)(2,1)S(1)}, bf16[2,224,512]{1,2,0:T(8,128)(2,1)S(1)}, u32[]{:S(2)}, u32[]{:S(2)}) collective-permute-start(bf16[2,224,512]{1,2,0:T(8,128)(2,1)S(1)} %broadcast_select_fusion), channel_id=1, source_target_pairs={{0,48},{16,0},{32,16},{48,32},{1,49},{17,1},{33,17},{49,33},{2,50}... | collective-permute-start | bytes 1376264 | tf_op jit(solution)/shard_map/ppermute | solution.py:42
  67.9 0.7 copy-start.3
  71.3 33.9 %all-to-all-start.1 = ((bf16[8,3,7644]{2,1,0:T(4,128)(2,1)}), bf16[8,3,7644]{2,1,0:T(4,128)(2,1)}, u32[]{:S(2)}, u32[]{:S(2)}) async-start(bf16[8,3,7644]{2,1,0:T(4,128)(2,1)} %broadcast_in_dim.137), calls=%async_computation.1 | async-start | bytes 983040 | tf_op jit(solution)/shard_map/all_to_all | solution.py:93
  85.3 0.9 copy-start.4
  86.2 3.1 %copy-start.2 = (bf16[8,224,512]{1,2,0:T(8,128)(2,1)}, bf16[8,224,512]{1,2,0:T(8,128)(2,1)S(1)}, u32[]{:S(2)}) copy-start(bf16[8,224,512]{1,2,0:T(8,128)(2,1)S(1)} %bitcast_select_fusion) | copy-start | bytes 5505028
  87.0 1.4 copy-start.1
  89.3 26.1 %copy-start.6 = (f32[224]{0:T(256)S(1)}, f32[224]{0:T(256)}, u32[]{:S(2)}) copy-start(f32[224]{0:T(256)} %param.11) | copy-start | bytes 2692
  89.3 60.9 %collective-permute-start.4 = (bf16[576,512]{1,0:T(8,128)(2,1)}, bf16[576,512]{1,0:T(8,128)(2,1)S(1)}, u32[]{:S(2)}, u32[]{:S(2)}) collective-permute-start(bf16[576,512]{1,0:T(8,128)(2,1)} %get-tuple-element.9), channel_id=1, source_target_pairs={{0,2},{2,4},{4,6},{6,0},{1,3},{3,5},{5,7},{7,1},{8,10},{10,12},{12... | collective-permute-start | bytes 1769480 | tf_op jit(solution)/shard_map/ppermute | solution.py:53
  91.4 58.9 %collective-permute-start.5 = (bf16[576,512]{1,0:T(8,128)(2,1)S(1)}, bf16[576,512]{1,0:T(8,128)(2,1)}, u32[]{:S(2)}, u32[]{:S(2)}) collective-permute-start(bf16[576,512]{1,0:T(8,128)(2,1)S(1)} %get-tuple-element.11), channel_id=1, source_target_pairs={{0,4},{2,6},{4,0},{6,2},{1,5},{3,7},{5,1},{7,3},{8,12},{10,14},{12... | collective-permute-start | bytes 1769480 | tf_op jit(solution)/shard_map/ppermute | solution.py:53
  95.1 55.2 %collective-permute-start.6 = (bf16[576,512]{1,0:T(8,128)(2,1)S(1)}, bf16[576,512]{1,0:T(8,128)(2,1)}, u32[]{:S(2)}, u32[]{:S(2)}) collective-permute-start(bf16[576,512]{1,0:T(8,128)(2,1)S(1)} %get-tuple-element.10), channel_id=1, source_target_pairs={{0,6},{2,0},{4,2},{6,4},{1,7},{3,1},{5,3},{7,5},{8,14},{10,8},{12,... | collective-permute-start | bytes 1769480 | tf_op jit(solution)/shard_map/ppermute | solution.py:53
  110.9 27.1 %all-to-all-start.2 = ((bf16[8,2,3822]{2,1,0:T(2,128)(2,1)}), bf16[8,2,3822]{2,1,0:T(2,128)(2,1)S(1)}, u32[]{:S(2)}, u32[]{:S(2)}) async-start(bf16[8,2,3822]{2,1,0:T(2,128)(2,1)} %reshape.463), calls=%async_computation.2 | async-start | bytes 245760 | tf_op jit(solution)/shard_map/all_to_all | solution.py:96
  115.4 22.4 %collective-permute-start.9 = (f32[224]{0:T(256)S(1)}, f32[224]{0:T(256)S(1)}, u32[]{:S(2)}, u32[]{:S(2)}) collective-permute-start(f32[224]{0:T(256)S(1)} %copy-done.6), channel_id=1, source_target_pairs={{0,0},{1,8},{2,16},{3,24},{4,32},{5,40},{6,48},{7,56},{8,1},{9,9},... | collective-permute-start | bytes 2696 | tf_op jit(solution)/shard_map/ppermute | solution.py:130
  138.2 15.0 %collective-permute-start.7 = (bf16[8,7644]{1,0:T(8,128)(2,1)S(1)}, bf16[8,7644]{1,0:T(8,128)(2,1)}, u32[]{:S(2)}, u32[]{:S(2)}) collective-permute-start(bf16[8,7644]{1,0:T(8,128)(2,1)S(1)} %bitcast.89), channel_id=1, source_target_pairs={{0,0},{1,8},{2,16},{3,24},{4,32},{5,40},{6,48},{7,56},{8,1},{9,9},... | collective-permute-start | bytes 366920 | tf_op jit(solution)/shard_map/ppermute | solution.py:97
  154.4 33.3 %collective-permute-start.8 = (bf16[288,512]{1,0:T(8,128)(2,1)S(1)}, bf16[288,512]{1,0:T(8,128)(2,1)S(1)}, u32[]{:S(2)}, u32[]{:S(2)}) collective-permute-start(bf16[288,512]{1,0:T(8,128)(2,1)S(1)} %constant_dynamic-slice_fusion), channel_id=1, source_target_pairs={{0,1},{1,0},{2,3},{3,2},{4,5},{5,4},{6,7},{7,6},{8,9},{9,8},{10,11... | collective-permute-start | bytes 884744 | tf_op jit(solution)/shard_map/ppermute | solution.py:53
  189.8 25.3 %collective-permute-start.10 = (bf16[512,224]{0,1:T(8,128)(2,1)S(1)}, bf16[512,224]{0,1:T(8,128)(2,1)S(1)}, u32[]{:S(2)}, u32[]{:S(2)}) collective-permute-start(bf16[512,224]{0,1:T(8,128)(2,1)S(1)} %bitcast.73), channel_id=1, source_target_pairs={{0,1},{1,0},{2,3},{3,2},{4,5},{5,4},{6,7},{7,6},{8,9},{9,8},{10,11... | collective-permute-start | bytes 688136 | tf_op jit(solution)/shard_map/ppermute | solution.py:42
  215.8 15.9 %collective-permute-start.11 = (bf16[2,512,224]{1,2,0:T(8,128)(2,1)S(1)}, bf16[2,512,224]{1,2,0:T(8,128)(2,1)S(1)}, u32[]{:S(2)}, u32[]{:S(2)}) collective-permute-start(bf16[2,512,224]{1,2,0:T(8,128)(2,1)S(1)} %broadcast_select_fusion.1), channel_id=1, source_target_pairs={{0,2},{2,4},{4,6},{6,0},{1,3},{3,5},{5,7},{7,1},{8,10},{10,12},{12... | collective-permute-start | bytes 1376264 | tf_op jit(solution)/shard_map/ppermute | solution.py:42
  217.7 25.6 %collective-permute-start.12 = (bf16[2,512,224]{1,2,0:T(8,128)(2,1)S(1)}, bf16[2,512,224]{1,2,0:T(8,128)(2,1)S(1)}, u32[]{:S(2)}, u32[]{:S(2)}) collective-permute-start(bf16[2,512,224]{1,2,0:T(8,128)(2,1)S(1)} %broadcast_select_fusion.1), channel_id=1, source_target_pairs={{0,4},{2,6},{4,0},{6,2},{1,5},{3,7},{5,1},{7,3},{8,12},{10,14},{12... | collective-permute-start | bytes 1376264 | tf_op jit(solution)/shard_map/ppermute | solution.py:42
  227.6 18.5 %collective-permute-start.13 = (bf16[2,512,224]{1,2,0:T(8,128)(2,1)S(1)}, bf16[2,512,224]{1,2,0:T(8,128)(2,1)S(1)}, u32[]{:S(2)}, u32[]{:S(2)}) collective-permute-start(bf16[2,512,224]{1,2,0:T(8,128)(2,1)S(1)} %broadcast_select_fusion.1), channel_id=1, source_target_pairs={{0,6},{2,0},{4,2},{6,4},{1,7},{3,1},{5,3},{7,5},{8,14},{10,8},{12,... | collective-permute-start | bytes 1376264 | tf_op jit(solution)/shard_map/ppermute | solution.py:42
  250.0 1.9 copy-start.5

commit v7 on v6

--- a/solution.py
+++ b/solution.py
@@ -98,8 +98,8 @@
     chosen = chosen.reshape(state_shape).astype(jnp.float32)
 
     both = jnp.concatenate([qkv_weight, out_weight], axis=1)
-    both = gather_by_shifts(gather_by_shifts(both, "c", 2), "x", n_row // 2)
-    both = both.reshape((n_row,) + both.shape[2:])
+    both = lax.all_gather(both, ROW, axis=1, tiled=True)
+    both = jnp.swapaxes(both.reshape(both.shape[0], n_row, -1), 0, 1)
     weight_all = both[:, :, : qkv_weight.shape[1]]
     out_w = both[:, :, qkv_weight.shape[1] :]
     partial_proj = jnp.einsum(

time: 258 us -> 285 us (1.10)
  the two profiles are of different devices: /device:TPU:1 before, /device:TPU:47 now
where the time goes in v7:
time: 285 us; the launch traced here: 284 us
  waiting for transfers between devices  109 us (38%)
  blocking collectives  83.1 us (29%)
  starting transfers between devices  44.8 us (16%)
  between operations  15.2 us (5%)
  local copies, waits for them, and re-layouts  12.3 us (4%)
  other arithmetic  11.8 us (4%)
  matrix products  8.73 us (3%)
    all_to_all x1, blocking collectives, shards(): lax.all_to_all(jnp.concatenate([pieces, meta], axis=1), COL, 0, 0, tiled=...  58.6 us
    ppermute x4, waiting for transfers between devices, gather_by_shifts(): lax.ppermute(x, axis, [(i, (i + k) % n) for i in range(n)])  45.1 us
    ppermute x4, waiting for transfers between devices, reduce_scatter_by_shifts(): lax.ppermute(part, axis, [(i, (i + k) % n) for i in range(n)])  34.2 us
    all_to_all x1, blocking collectives, shards(): chosen = lax.all_to_all(to_send, COL, 0, 0, tiled=True)  24.4 us
    all_to_all x1, waiting for transfers between devices, shards(): pieces = lax.all_to_all(pieces, 'req', 0, 0, tiled=True)  24.1 us
    ppermute x1, starting transfers between devices, shards(): gains = lax.ppermute(head_gain, flat, perm).reshape(heads_here, HD)  13.2 us
    ppermute x4, starting transfers between devices, reduce_scatter_by_shifts(): lax.ppermute(part, axis, [(i, (i + k) % n) for i in range(n)])  11.6 us
    ppermute x4, starting transfers between devices, gather_by_shifts(): lax.ppermute(x, axis, [(i, (i + k) % n) for i in range(n)])  9.12 us
  transfers between devices with their start and end apart: 12, of which 7 were waited for; matrix products, arithmetic and copies ran while one was open for 4% of the time, Pallas kernels for 0%

profile of v7, /device:TPU:47, one launch (start us, length us, event | category | flops | bytes accessed | tf_op | source)
XLA Modules:
  0.0 284.4 jit_solution(17925211674236004062)
XLA Ops:
  6.5 1.1 copy.19
  7.6 1.6 pad_maximum_fusion.2
  10.0 1.0 convert.39
  10.9 1.0 multiply_convert_fusion.3
  12.6 0.9 multiply_convert_fusion
  13.5 1.3 fusion.7
  14.8 0.9 reshape.295
  15.8 0.3 copy.20
  16.0 0.4 reshape.296
  16.6 0.6 copy.21
  17.2 58.6 %all_to_all.26 = bf16[8,1,22935]{2,1,0:T(2,128)(2,1)S(1)} all-to-all(bf16[8,1,22935]{2,1,0:T(2,128)(2,1)S(1)} %copy.21), channel_id=1, replica_groups=mesh['req'=8,'x'=4,'c'=2,'y'=4,'zh'=2] {'y','zh'}, dimensions={0} | all-to-all | bytes 733920 | tf_op jit(solution)/shard_map/all_to_all | solution.py:85
  76.3 0.9 broadcast_in_dim.101
  77.2 5.0 %all-to-all-start.1 = ((bf16[8,3,7644]{2,1,0:T(4,128)(2,1)}), bf16[8,3,7644]{2,1,0:T(4,128)(2,1)S(1)}, u32[]{:S(2)}, u32[]{:S(2)}) async-start(bf16[8,3,7644]{2,1,0:T(4,128)(2,1)} %broadcast_in_dim.101), calls=%async_computation.1 | async-start | bytes 983040 | tf_op jit(solution)/shard_map/all_to_all | solution.py:93
  82.5 24.1 %all-to-all-done.1 = bf16[8,3,7644]{2,1,0:T(4,128)(2,1)S(1)} async-done(((bf16[8,3,7644]{2,1,0:T(4,128)(2,1)}), bf16[8,3,7644]{2,1,0:T(4,128)(2,1)S(1)}, u32[]{:S(2)}, u32[]{:S(2)}) %all-to-all-start.1) | async-done | bytes 366944 | tf_op jit(solution)/shard_map/all_to_all | solution.py:93
  106.6 0.3 reshape.298
  106.9 0.6 gather_fusion
  107.6 2.0 convolution_convert_fusion
  109.6 1.4 copy-done.1
  111.0 1.2 constant_dynamic-slice_fusion.3
  112.2 2.9 %collective-permute-start = (bf16[576,512]{1,0:T(8,128)(2,1)}, bf16[576,512]{1,0:T(8,128)(2,1)S(1)}, u32[]{:S(2)}, u32[]{:S(2)}) collective-permute-start(bf16[576,512]{1,0:T(8,128)(2,1)} %get-tuple-element.9), channel_id=1, source_target_pairs={{0,2},{2,4},{4,6},{6,0},{1,3},{3,5},{5,7},{7,1},{8,10},{10,12},{12... | collective-permute-start | bytes 1769480 | tf_op jit(solution)/shard_map/ppermute | solution.py:53
  115.2 4.6 %collective-permute-start.1 = (bf16[576,512]{1,0:T(8,128)(2,1)}, bf16[576,512]{1,0:T(8,128)(2,1)}, u32[]{:S(2)}, u32[]{:S(2)}) collective-permute-start(bf16[576,512]{1,0:T(8,128)(2,1)} %get-tuple-element.11), channel_id=1, source_target_pairs={{0,4},{2,6},{4,0},{6,2},{1,5},{3,7},{5,1},{7,3},{8,12},{10,14},{12... | collective-permute-start | bytes 1769480 | tf_op jit(solution)/shard_map/ppermute | solution.py:53
  119.8 2.1 collective-permute-start.2
  122.0 0.5 broadcast.349
  122.5 0.7 reduce.6
  123.4 24.4 %all_to_all.27 = bf16[8,2,3822]{2,1,0:T(2,128)(2,1)S(1)} all-to-all(bf16[8,2,3822]{2,1,0:T(2,128)(2,1)S(1)} %reshape.333), channel_id=1, replica_groups=mesh['req'=8,'x'=4,'c'=2,'y'=4,'zh'=2] {'y','zh'}, dimensions={0} | all-to-all | bytes 244608 | tf_op jit(solution)/shard_map/all_to_all | solution.py:96
  148.0 5.9 %collective-permute-start.3 = (bf16[8,7644]{1,0:T(8,128)(2,1)S(1)}, bf16[8,7644]{1,0:T(8,128)(2,1)S(1)}, u32[]{:S(2)}, u32[]{:S(2)}) collective-permute-start(bf16[8,7644]{1,0:T(8,128)(2,1)S(1)} %bitcast.76), channel_id=1, source_target_pairs={{0,0},{1,8},{2,16},{3,24},{4,32},{5,40},{6,48},{7,56},{8,1},{9,9},... | collective-permute-start | bytes 366920 | tf_op jit(solution)/shard_map/ppermute | solution.py:97
  153.9 13.2 %collective-permute-start.5 = (f32[224]{0:T(256)S(1)}, f32[224]{0:T(256)S(1)}, u32[]{:S(2)}, u32[]{:S(2)}) collective-permute-start(f32[224]{0:T(256)S(1)} %copy-done.3), channel_id=1, source_target_pairs={{0,0},{1,8},{2,16},{3,24},{4,32},{5,40},{6,48},{7,56},{8,1},{9,9},... | collective-permute-start | bytes 2696 | tf_op jit(solution)/shard_map/ppermute | solution.py:130
  167.2 5.1 %collective-permute-done.5 = f32[224]{0:T(256)S(1)} collective-permute-done((f32[224]{0:T(256)S(1)}, f32[224]{0:T(256)S(1)}, u32[]{:S(2)}, u32[]{:S(2)}) %collective-permute-start.5) | collective-permute-done | bytes 928 | tf_op jit(solution)/shard_map/ppermute | solution.py:130
  172.4 0.5 constant_dynamic-slice_fusion.4
  173.2 1.7 add_convert_fusion
  175.0 1.9 collective-permute-start.4
  176.9 0.7 iota_compare_fusion.1
  177.6 34.2 %collective-permute-done.4 = bf16[288,512]{1,0:T(8,128)(2,1)S(1)} collective-permute-done((bf16[288,512]{1,0:T(8,128)(2,1)S(1)}, bf16[288,512]{1,0:T(8,128)(2,1)S(1)}, u32[]{:S(2)}, u32[]{:S(2)}) %collective-permute-start.4) | collective-permute-done | bytes 294944 | tf_op jit(solution)/shard_map/ppermute | solution.py:53
  212.1 1.7 fusion.6
  213.8 1.8 multiply_reduce_fusion
  215.7 1.9 collective-permute-start.6
  217.9 24.9 %collective-permute-done.6 = bf16[512,224]{0,1:T(8,128)(2,1)S(1)} collective-permute-done((bf16[512,224]{0,1:T(8,128)(2,1)S(1)}, bf16[512,224]{0,1:T(8,128)(2,1)S(1)}, u32[]{:S(2)}, u32[]{:S(2)}) %collective-permute-start.6) | collective-permute-done | bytes 229408 | tf_op jit(solution)/shard_map/ppermute | solution.py:42
  242.8 0.6 gather_fusion.1
  243.5 1.9 collective-permute-start.7
  245.4 1.9 collective-permute-start.8
  247.4 3.4 %collective-permute-start.9 = (bf16[2,512,224]{1,2,0:T(8,128)(2,1)S(1)}, bf16[2,512,224]{1,2,0:T(8,128)(2,1)S(1)}, u32[]{:S(2)}, u32[]{:S(2)}) collective-permute-start(bf16[2,512,224]{1,2,0:T(8,128)(2,1)S(1)} %broadcast_select_fusion), channel_id=1, source_target_pairs={{0,6},{2,0},{4,2},{6,4},{1,7},{3,1},{5,3},{7,5},{8,14},{10,8},{12,... | collective-permute-start | bytes 1376264 | tf_op jit(solution)/shard_map/ppermute | solution.py:42
  250.9 6.1 %collective-permute-done.7 = bf16[2,512,224]{1,2,0:T(8,128)(2,1)S(1)} collective-permute-done((bf16[2,512,224]{1,2,0:T(8,128)(2,1)S(1)}, bf16[2,512,224]{1,2,0:T(8,128)(2,1)S(1)}, u32[]{:S(2)}, u32[]{:S(2)}) %collective-permute-start.7) | collective-permute-done | bytes 458784 | tf_op jit(solution)/shard_map/ppermute | solution.py:42
  257.0 3.5 %collective-permute-done.8 = bf16[2,512,224]{1,2,0:T(8,128)(2,1)S(1)} collective-permute-done((bf16[2,512,224]{1,2,0:T(8,128)(2,1)S(1)}, bf16[2,512,224]{1,2,0:T(8,128)(2,1)S(1)}, u32[]{:S(2)}, u32[]{:S(2)}) %collective-permute-start.8) | collective-permute-done | bytes 458784 | tf_op jit(solution)/shard_map/ppermute | solution.py:42
  260.5 10.6 %collective-permute-done.9 = bf16[2,512,224]{1,2,0:T(8,128)(2,1)S(1)} collective-permute-done((bf16[2,512,224]{1,2,0:T(8,128)(2,1)S(1)}, bf16[2,512,224]{1,2,0:T(8,128)(2,1)S(1)}, u32[]{:S(2)}, u32[]{:S(2)}) %collective-permute-start.9) | collective-permute-done | bytes 458784 | tf_op jit(solution)/shard_map/ppermute | solution.py:42
  271.3 1.9 gather_fusion.2
  273.3 1.7 bitcast_select_fusion
  275.0 1.8 convert_reduce_fusion
  276.8 0.8 add_convert_fusion.2
  (50 shorter events, 2.9 us)
Async XLA Ops:
  6.5 7.0 %copy-start = (bf16[3,224,1024]{2,1,0:T(8,128)(2,1)S(1)}, bf16[3,224,1024]{2,1,0:T(8,128)(2,1)}, u32[]{:S(2)}) copy-start(bf16[3,224,1024]{2,1,0:T(8,128)(2,1)} %param.13) | copy-start | bytes 4128772
  6.5 101.0 %all-gather.2.cloned.1.call-start = ((), (), s32[]{:S(2)}) async-start(), calls=%async_computation.3 | async-start | bytes 2359296 | tf_op jit(solution)/shard_map/all_gather | solution.py:101
  75.9 31.6 %copy-start.2 = (bf16[224,512]{1,0:T(8,128)(2,1)S(1)}, bf16[224,512]{1,0:T(8,128)(2,1)}, u32[]{:S(2)}) copy-start(bf16[224,512]{1,0:T(8,128)(2,1)} %param.8) | copy-start | bytes 688132
  77.2 29.4 %all-to-all-start.1 = ((bf16[8,3,7644]{2,1,0:T(4,128)(2,1)}), bf16[8,3,7644]{2,1,0:T(4,128)(2,1)S(1)}, u32[]{:S(2)}, u32[]{:S(2)}) async-start(bf16[8,3,7644]{2,1,0:T(4,128)(2,1)} %broadcast_in_dim.101), calls=%async_computation.1 | async-start | bytes 983040 | tf_op jit(solution)/shard_map/all_to_all | solution.py:93
  109.6 1.4 copy-start.1
  111.0 42.9 %copy-start.3 = (f32[224]{0:T(256)S(1)}, f32[224]{0:T(256)}, u32[]{:S(2)}) copy-start(f32[224]{0:T(256)} %param.11) | copy-start | bytes 2692
  112.2 61.0 %collective-permute-start = (bf16[576,512]{1,0:T(8,128)(2,1)}, bf16[576,512]{1,0:T(8,128)(2,1)S(1)}, u32[]{:S(2)}, u32[]{:S(2)}) collective-permute-start(bf16[576,512]{1,0:T(8,128)(2,1)} %get-tuple-element.9), channel_id=1, source_target_pairs={{0,2},{2,4},{4,6},{6,0},{1,3},{3,5},{5,7},{7,1},{8,10},{10,12},{12... | collective-permute-start | bytes 1769480 | tf_op jit(solution)/shard_map/ppermute | solution.py:53
  115.2 58.0 %collective-permute-start.1 = (bf16[576,512]{1,0:T(8,128)(2,1)}, bf16[576,512]{1,0:T(8,128)(2,1)}, u32[]{:S(2)}, u32[]{:S(2)}) collective-permute-start(bf16[576,512]{1,0:T(8,128)(2,1)} %get-tuple-element.11), channel_id=1, source_target_pairs={{0,4},{2,6},{4,0},{6,2},{1,5},{3,7},{5,1},{7,3},{8,12},{10,14},{12... | collective-permute-start | bytes 1769480 | tf_op jit(solution)/shard_map/ppermute | solution.py:53
  119.8 53.4 %collective-permute-start.2 = (bf16[576,512]{1,0:T(8,128)(2,1)S(1)}, bf16[576,512]{1,0:T(8,128)(2,1)}, u32[]{:S(2)}, u32[]{:S(2)}) collective-permute-start(bf16[576,512]{1,0:T(8,128)(2,1)S(1)} %get-tuple-element.10), channel_id=1, source_target_pairs={{0,6},{2,0},{4,2},{6,4},{1,7},{3,1},{5,3},{7,5},{8,14},{10,8},{12,... | collective-permute-start | bytes 1769480 | tf_op jit(solution)/shard_map/ppermute | solution.py:53
  148.0 24.9 %collective-permute-start.3 = (bf16[8,7644]{1,0:T(8,128)(2,1)S(1)}, bf16[8,7644]{1,0:T(8,128)(2,1)S(1)}, u32[]{:S(2)}, u32[]{:S(2)}) collective-permute-start(bf16[8,7644]{1,0:T(8,128)(2,1)S(1)} %bitcast.76), channel_id=1, source_target_pairs={{0,0},{1,8},{2,16},{3,24},{4,32},{5,40},{6,48},{7,56},{8,1},{9,9},... | collective-permute-start | bytes 366920 | tf_op jit(solution)/shard_map/ppermute | solution.py:97
  153.9 18.4 %collective-permute-start.5 = (f32[224]{0:T(256)S(1)}, f32[224]{0:T(256)S(1)}, u32[]{:S(2)}, u32[]{:S(2)}) collective-permute-start(f32[224]{0:T(256)S(1)} %copy-done.3), channel_id=1, source_target_pairs={{0,0},{1,8},{2,16},{3,24},{4,32},{5,40},{6,48},{7,56},{8,1},{9,9},... | collective-permute-start | bytes 2696 | tf_op jit(solution)/shard_map/ppermute | solution.py:130
  175.0 36.8 %collective-permute-start.4 = (bf16[288,512]{1,0:T(8,128)(2,1)S(1)}, bf16[288,512]{1,0:T(8,128)(2,1)S(1)}, u32[]{:S(2)}, u32[]{:S(2)}) collective-permute-start(bf16[288,512]{1,0:T(8,128)(2,1)S(1)} %constant_dynamic-slice_fusion), channel_id=1, source_target_pairs={{0,1},{1,0},{2,3},{3,2},{4,5},{5,4},{6,7},{7,6},{8,9},{9,8},{10,11... | collective-permute-start | bytes 884744 | tf_op jit(solution)/shard_map/ppermute | solution.py:53
  215.7 27.0 %collective-permute-start.6 = (bf16[512,224]{0,1:T(8,128)(2,1)S(1)}, bf16[512,224]{0,1:T(8,128)(2,1)S(1)}, u32[]{:S(2)}, u32[]{:S(2)}) collective-permute-start(bf16[512,224]{0,1:T(8,128)(2,1)S(1)} %bitcast.62), channel_id=1, source_target_pairs={{0,1},{1,0},{2,3},{3,2},{4,5},{5,4},{6,7},{7,6},{8,9},{9,8},{10,11... | collective-permute-start | bytes 688136 | tf_op jit(solution)/shard_map/ppermute | solution.py:42
  243.5 13.5 %collective-permute-start.7 = (bf16[2,512,224]{1,2,0:T(8,128)(2,1)S(1)}, bf16[2,512,224]{1,2,0:T(8,128)(2,1)S(1)}, u32[]{:S(2)}, u32[]{:S(2)}) collective-permute-start(bf16[2,512,224]{1,2,0:T(8,128)(2,1)S(1)} %broadcast_select_fusion), channel_id=1, source_target_pairs={{0,2},{2,4},{4,6},{6,0},{1,3},{3,5},{5,7},{7,1},{8,10},{10,12},{12... | collective-permute-start | bytes 1376264 | tf_op jit(solution)/shard_map/ppermute | solution.py:42
  245.4 15.0 %collective-permute-start.8 = (bf16[2,512,224]{1,2,0:T(8,128)(2,1)S(1)}, bf16[2,512,224]{1,2,0:T(8,128)(2,1)S(1)}, u32[]{:S(2)}, u32[]{:S(2)}) collective-permute-start(bf16[2,512,224]{1,2,0:T(8,128)(2,1)S(1)} %broadcast_select_fusion), channel_id=1, source_target_pairs={{0,4},{2,6},{4,0},{6,2},{1,5},{3,7},{5,1},{7,3},{8,12},{10,14},{12... | collective-permute-start | bytes 1376264 | tf_op jit(solution)/shard_map/ppermute | solution.py:42
  247.4 23.7 %collective-permute-start.9 = (bf16[2,512,224]{1,2,0:T(8,128)(2,1)S(1)}, bf16[2,512,224]{1,2,0:T(8,128)(2,1)S(1)}, u32[]{:S(2)}, u32[]{:S(2)}) collective-permute-start(bf16[2,512,224]{1,2,0:T(8,128)(2,1)S(1)} %broadcast_select_fusion), channel_id=1, source_target_pairs={{0,6},{2,0},{4,2},{6,4},{1,7},{3,1},{5,3},{7,5},{8,14},{10,8},{12,... | collective-permute-start | bytes 1376264 | tf_op jit(solution)/shard_map/ppermute | solution.py:42
Sparse Core Ops, SparseCore 0:
  9.5 36.0 all-gather.1

commit v8 on v4

--- a/solution.py
+++ b/solution.py
@@ -128,6 +128,7 @@
     normed = (attended * inverse_rms * gains).astype(jnp.bfloat16).reshape(SLOTS, heads_here * HD)
     hidden = gather_by_shifts(gather_by_shifts(normed, "zh", 2), "y", n_col // 2)
     hidden = hidden.reshape((n_col,) + normed.shape)
+    out_weight, normed = lax.optimization_barrier((out_weight, normed))
     out_w = gather_by_shifts(gather_by_shifts(out_weight, "c", 2), "x", n_row // 2)
     out_w = out_w.reshape((n_row,) + out_weight.shape)
     blocks = jnp.einsum("ktd,kde->ket", hidden, out_w, preferred_element_type=jnp.float32)

time: 245 us -> 260 us (1.061)
  the two profiles are of different devices: /device:TPU:15 before, /device:TPU:41 now
where the time goes in v8:
time: 260 us; the launch traced here: 259 us
  starting transfers between devices  130 us (50%)
  waiting for transfers between devices  83 us (32%)
  other arithmetic  18.8 us (7%)
  local copies, waits for them, and re-layouts  18.5 us (7%)
  matrix products  6.32 us (2%)
    ppermute x12, starting transfers between devices, gather_by_shifts(): lax.ppermute(x, axis, [(i, (i + k) % n) for i in range(n)])  61.8 us
    ppermute x4, waiting for transfers between devices, reduce_scatter_by_shifts(): lax.ppermute(part, axis, [(i, (i + k) % n) for i in range(n)])  29.5 us
    ppermute x12, waiting for transfers between devices, gather_by_shifts(): lax.ppermute(x, axis, [(i, (i + k) % n) for i in range(n)])  26.1 us
    all_to_all x1, starting transfers between devices, shards(): lax.all_to_all(jnp.concatenate([pieces, meta], axis=1), COL, 0, 0, tiled=...  16.7 us
    ppermute x1, starting transfers between devices, shards(): gains = lax.ppermute(head_gain, flat, perm).reshape(heads_here, HD)  15.2 us
    ppermute x1, starting transfers between devices, shards(): chosen = lax.ppermute(chosen, flat, perm)  14.1 us
    all_to_all x1, waiting for transfers between devices, shards(): lax.all_to_all(jnp.concatenate([pieces, meta], axis=1), COL, 0, 0, tiled=...  13 us
    ppermute x4, starting transfers between devices, reduce_scatter_by_shifts(): lax.ppermute(part, axis, [(i, (i + k) % n) for i in range(n)])  11.7 us
  transfers between devices with their start and end apart: 21, of which 13 were waited for; matrix products, arithmetic and copies ran while one was open for 8% of the time, Pallas kernels for 0%

profile of v8, /device:TPU:41, one launch (start us, length us, event | category | flops | bytes accessed | tf_op | source)
XLA Modules:
  0.0 258.7 jit_solution(11622403200636864680)
XLA Ops:
  0.8 1.0 convert.39
  1.7 1.0 multiply_convert_fusion.3
  4.3 1.3 fusion.7
  7.5 1.4 copy.20
  8.9 16.7 %all-to-all-start = ((bf16[8,1,22935]{2,1,0:T(2,128)(2,1)}), bf16[8,1,22935]{2,1,0:T(2,128)(2,1)S(1)}, u32[]{:S(2)}, u32[]{:S(2)}) async-start(bf16[8,1,22935]{2,1,0:T(2,128)(2,1)} %copy.20), calls=%async_computation | async-start | bytes 1474560 | tf_op jit(solution)/shard_map/all_to_all | solution.py:85
  25.6 3.1 %collective-permute-start = (bf16[224,288]{0,1:T(8,128)(2,1)S(1)}, bf16[224,288]{0,1:T(8,128)(2,1)S(1)}, u32[]{:S(2)}, u32[]{:S(2)}) collective-permute-start(bf16[224,288]{0,1:T(8,128)(2,1)S(1)} %copy-done.7), channel_id=1, source_target_pairs={{0,8},{8,0},{1,9},{9,1},{2,10},{10,2},{3,11},{11,3},{4,12},{12,4},... | collective-permute-start | bytes 387080 | tf_op jit(solution)/shard_map/ppermute | solution.py:42
  31.2 3.1 %collective-permute-start.1 = (bf16[2,224,288]{1,2,0:T(8,128)(2,1)}, bf16[2,224,288]{1,2,0:T(8,128)(2,1)S(1)}, u32[]{:S(2)}, u32[]{:S(2)}) collective-permute-start(bf16[2,224,288]{1,2,0:T(8,128)(2,1)} %broadcast_select_fusion.1), channel_id=1, source_target_pairs={{0,16},{16,32},{32,48},{48,0},{1,17},{17,33},{33,49},{49,1},{2,18}... | collective-permute-start | bytes 774152 | tf_op jit(solution)/shard_map/ppermute | solution.py:42
  34.3 4.4 %collective-permute-start.2 = (bf16[2,224,288]{1,2,0:T(8,128)(2,1)}, bf16[2,224,288]{1,2,0:T(8,128)(2,1)S(1)}, u32[]{:S(2)}, u32[]{:S(2)}) collective-permute-start(bf16[2,224,288]{1,2,0:T(8,128)(2,1)} %broadcast_select_fusion.1), channel_id=1, source_target_pairs={{0,32},{16,48},{32,0},{48,16},{1,33},{17,49},{33,1},{49,17},{2,34}... | collective-permute-start | bytes 774152 | tf_op jit(solution)/shard_map/ppermute | solution.py:42
  38.7 3.1 %collective-permute-start.3 = (bf16[2,224,288]{1,2,0:T(8,128)(2,1)}, bf16[2,224,288]{1,2,0:T(8,128)(2,1)S(1)}, u32[]{:S(2)}, u32[]{:S(2)}) collective-permute-start(bf16[2,224,288]{1,2,0:T(8,128)(2,1)} %broadcast_select_fusion.1), channel_id=1, source_target_pairs={{0,48},{16,0},{32,16},{48,32},{1,49},{17,1},{33,17},{49,33},{2,50}... | collective-permute-start | bytes 774152 | tf_op jit(solution)/shard_map/ppermute | solution.py:42
  42.7 7.3 %collective-permute-done.2 = bf16[2,224,288]{1,2,0:T(8,128)(2,1)S(1)} collective-permute-done((bf16[2,224,288]{1,2,0:T(8,128)(2,1)}, bf16[2,224,288]{1,2,0:T(8,128)(2,1)S(1)}, u32[]{:S(2)}, u32[]{:S(2)}) %collective-permute-start.2) | collective-permute-done | bytes 258080 | tf_op jit(solution)/shard_map/ppermute | solution.py:42
  50.0 1.3 collective-permute-done.3
  51.3 1.3 pad_maximum_fusion.1
  52.7 1.9 gather_fusion.1
  54.6 13.0 %all-to-all-done = bf16[8,1,22935]{2,1,0:T(2,128)(2,1)S(1)} async-done(((bf16[8,1,22935]{2,1,0:T(2,128)(2,1)}), bf16[8,1,22935]{2,1,0:T(2,128)(2,1)S(1)}, u32[]{:S(2)}, u32[]{:S(2)}) %all-to-all-start) | async-done | bytes 366992 | tf_op jit(solution)/shard_map/all_to_all | solution.py:85
  69.6 5.0 %all-to-all-start.1 = ((bf16[8,3,7644]{2,1,0:T(4,128)(2,1)}), bf16[8,3,7644]{2,1,0:T(4,128)(2,1)S(1)}, u32[]{:S(2)}, u32[]{:S(2)}) async-start(bf16[8,3,7644]{2,1,0:T(4,128)(2,1)} %broadcast_in_dim.159), calls=%async_computation.1 | async-start | bytes 983040 | tf_op jit(solution)/shard_map/all_to_all | solution.py:93
  75.6 1.4 copy-done.1
  77.1 1.2 constant_dynamic-slice_fusion.3
  78.2 3.2 %collective-permute-start.4 = (bf16[576,512]{1,0:T(8,128)(2,1)}, bf16[576,512]{1,0:T(8,128)(2,1)}, u32[]{:S(2)}, u32[]{:S(2)}) collective-permute-start(bf16[576,512]{1,0:T(8,128)(2,1)} %get-tuple-element.11), channel_id=1, source_target_pairs={{0,2},{2,4},{4,6},{6,0},{1,3},{3,5},{5,7},{7,1},{8,10},{10,12},{12... | collective-permute-start | bytes 1769480 | tf_op jit(solution)/shard_map/ppermute | solution.py:53
  81.5 4.7 %collective-permute-start.5 = (bf16[576,512]{1,0:T(8,128)(2,1)}, bf16[576,512]{1,0:T(8,128)(2,1)}, u32[]{:S(2)}, u32[]{:S(2)}) collective-permute-start(bf16[576,512]{1,0:T(8,128)(2,1)} %get-tuple-element.13), channel_id=1, source_target_pairs={{0,4},{2,6},{4,0},{6,2},{1,5},{3,7},{5,1},{7,3},{8,12},{10,14},{12... | collective-permute-start | bytes 1769480 | tf_op jit(solution)/shard_map/ppermute | solution.py:53
  86.1 1.9 collective-permute-start.6
  89.0 10.0 %all-to-all-done.1 = bf16[8,3,7644]{2,1,0:T(4,128)(2,1)S(1)} async-done(((bf16[8,3,7644]{2,1,0:T(4,128)(2,1)}), bf16[8,3,7644]{2,1,0:T(4,128)(2,1)S(1)}, u32[]{:S(2)}, u32[]{:S(2)}) %all-to-all-start.1) | async-done | bytes 366944 | tf_op jit(solution)/shard_map/all_to_all | solution.py:93
  102.1 5.4 %all-to-all-start.2 = ((bf16[8,2,3822]{2,1,0:T(2,128)(2,1)}), bf16[8,2,3822]{2,1,0:T(2,128)(2,1)S(1)}, u32[]{:S(2)}, u32[]{:S(2)}) async-start(bf16[8,2,3822]{2,1,0:T(2,128)(2,1)} %reshape.489), calls=%async_computation.2 | async-start | bytes 245760 | tf_op jit(solution)/shard_map/all_to_all | solution.py:96
  107.5 15.2 %collective-permute-start.9 = (f32[224]{0:T(256)S(1)}, f32[224]{0:T(256)S(1)}, u32[]{:S(2)}, u32[]{:S(2)}) collective-permute-start(f32[224]{0:T(256)S(1)} %copy-done.9), channel_id=1, source_target_pairs={{0,0},{1,8},{2,16},{3,24},{4,32},{5,40},{6,48},{7,56},{8,1},{9,9},... | collective-permute-start | bytes 2696 | tf_op jit(solution)/shard_map/ppermute | solution.py:127
  123.0 1.1 collective-permute-done.9
  124.3 14.1 %collective-permute-start.7 = (bf16[8,7644]{1,0:T(8,128)(2,1)S(1)}, bf16[8,7644]{1,0:T(8,128)(2,1)S(1)}, u32[]{:S(2)}, u32[]{:S(2)}) collective-permute-start(bf16[8,7644]{1,0:T(8,128)(2,1)S(1)} %bitcast.99), channel_id=1, source_target_pairs={{0,0},{1,8},{2,16},{3,24},{4,32},{5,40},{6,48},{7,56},{8,1},{9,9},... | collective-permute-start | bytes 366920 | tf_op jit(solution)/shard_map/ppermute | solution.py:97
  138.5 1.9 add_convert_fusion
  140.9 3.3 %collective-permute-done.7 = bf16[8,7644]{1,0:T(8,128)(2,1)S(1)} collective-permute-done((bf16[8,7644]{1,0:T(8,128)(2,1)S(1)}, bf16[8,7644]{1,0:T(8,128)(2,1)S(1)}, u32[]{:S(2)}, u32[]{:S(2)}) %collective-permute-start.7) | collective-permute-done | bytes 122336 | tf_op jit(solution)/shard_map/ppermute | solution.py:97
  144.5 1.9 collective-permute-start.8
  147.2 29.5 %collective-permute-done.8 = bf16[288,512]{1,0:T(8,128)(2,1)S(1)} collective-permute-done((bf16[288,512]{1,0:T(8,128)(2,1)S(1)}, bf16[288,512]{1,0:T(8,128)(2,1)S(1)}, u32[]{:S(2)}, u32[]{:S(2)}) %collective-permute-start.8) | collective-permute-done | bytes 294944 | tf_op jit(solution)/shard_map/ppermute | solution.py:53
  176.9 1.7 fusion.6
  178.7 1.8 multiply_reduce_fusion
  180.6 2.5 collective-permute-start.10
  183.2 2.1 collective-permute-start.14
  186.7 1.9 collective-permute-start.11
  188.6 10.8 %collective-permute-start.12 = (bf16[2,224,224]{2,1,0:T(8,128)(2,1)}, bf16[2,224,224]{2,1,0:T(8,128)(2,1)S(1)}, u32[]{:S(2)}, u32[]{:S(2)}) collective-permute-start(bf16[2,224,224]{2,1,0:T(8,128)(2,1)} %broadcast_select_fusion.2), channel_id=1, source_target_pairs={{0,32},{16,48},{32,0},{48,16},{1,33},{17,49},{33,1},{49,17},{2,34}... | collective-permute-start | bytes 602120 | tf_op jit(solution)/shard_map/ppermute | solution.py:42
  199.4 1.7 collective-permute-done.14
  202.6 23.3 %collective-permute-start.15 = (bf16[2,512,224]{1,2,0:T(8,128)(2,1)}, bf16[2,512,224]{1,2,0:T(8,128)(2,1)}, u32[]{:S(2)}, u32[]{:S(2)}) collective-permute-start(bf16[2,512,224]{1,2,0:T(8,128)(2,1)} %broadcast_select_fusion), channel_id=1, source_target_pairs={{0,2},{2,4},{4,6},{6,0},{1,3},{3,5},{5,7},{7,1},{8,10},{10,12},{12... | collective-permute-start | bytes 1376264 | tf_op jit(solution)/shard_map/ppermute | solution.py:42
  225.9 1.9 collective-permute-start.16
  227.8 3.7 %collective-permute-start.17 = (bf16[2,512,224]{1,2,0:T(8,128)(2,1)}, bf16[2,512,224]{1,2,0:T(8,128)(2,1)}, u32[]{:S(2)}, u32[]{:S(2)}) collective-permute-start(bf16[2,512,224]{1,2,0:T(8,128)(2,1)} %broadcast_select_fusion), channel_id=1, source_target_pairs={{0,6},{2,0},{4,2},{6,4},{1,7},{3,1},{5,3},{7,5},{8,14},{10,8},{12,... | collective-permute-start | bytes 1376264 | tf_op jit(solution)/shard_map/ppermute | solution.py:42
  231.7 1.9 collective-permute-start.13
  234.5 4.7 %collective-permute-done.13 = bf16[2,224,224]{2,1,0:T(8,128)(2,1)S(1)} collective-permute-done((bf16[2,224,224]{2,1,0:T(8,128)(2,1)}, bf16[2,224,224]{2,1,0:T(8,128)(2,1)S(1)}, u32[]{:S(2)}, u32[]{:S(2)}) %collective-permute-start.13) | collective-permute-done | bytes 200736 | tf_op jit(solution)/shard_map/ppermute | solution.py:42
  239.2 1.3 pad_maximum_fusion.2
  241.0 1.3 copy.22
  242.3 2.8 %collective-permute-done.15 = bf16[2,512,224]{1,2,0:T(8,128)(2,1)} collective-permute-done((bf16[2,512,224]{1,2,0:T(8,128)(2,1)}, bf16[2,512,224]{1,2,0:T(8,128)(2,1)}, u32[]{:S(2)}, u32[]{:S(2)}) %collective-permute-start.15) | collective-permute-done | bytes 458784 | tf_op jit(solution)/shard_map/ppermute | solution.py:42
  245.1 6.8 %collective-permute-done.17 = bf16[2,512,224]{1,2,0:T(8,128)(2,1)} collective-permute-done((bf16[2,512,224]{1,2,0:T(8,128)(2,1)}, bf16[2,512,224]{1,2,0:T(8,128)(2,1)}, u32[]{:S(2)}, u32[]{:S(2)}) %collective-permute-start.17) | collective-permute-done | bytes 458784 | tf_op jit(solution)/shard_map/ppermute | solution.py:42
  251.9 1.7 pad_maximum_fusion
  253.6 1.9 gather_fusion.6
  255.5 1.8 bitcast_select_fusion
  (95 shorter events, 21.2 us)
Async XLA Ops:
  0.0 4.3 %copy-start = (bf16[3,224,1024]{2,1,0:T(8,128)(2,1)S(1)}, bf16[3,224,1024]{2,1,0:T(8,128)(2,1)}, u32[]{:S(2)}) copy-start(bf16[3,224,1024]{2,1,0:T(8,128)(2,1)} %param.13) | copy-start | bytes 4128772
  7.3 18.3 %copy-start.7 = (bf16[224,288]{0,1:T(8,128)(2,1)S(1)}, bf16[224,288]{0,1:T(8,128)(2,1)}, u32[]{:S(2)}) copy-start(bf16[224,288]{0,1:T(8,128)(2,1)} %param.9) | copy-start | bytes 387076
  8.9 58.6 %all-to-all-start = ((bf16[8,1,22935]{2,1,0:T(2,128)(2,1)}), bf16[8,1,22935]{2,1,0:T(2,128)(2,1)S(1)}, u32[]{:S(2)}, u32[]{:S(2)}) async-start(bf16[8,1,22935]{2,1,0:T(2,128)(2,1)} %copy.20), calls=%async_computation | async-start | bytes 1474560 | tf_op jit(solution)/shard_map/all_to_all | solution.py:85
  25.6 4.1 %collective-permute-start = (bf16[224,288]{0,1:T(8,128)(2,1)S(1)}, bf16[224,288]{0,1:T(8,128)(2,1)S(1)}, u32[]{:S(2)}, u32[]{:S(2)}) collective-permute-start(bf16[224,288]{0,1:T(8,128)(2,1)S(1)} %copy-done.7), channel_id=1, source_target_pairs={{0,8},{8,0},{1,9},{9,1},{2,10},{10,2},{3,11},{11,3},{4,12},{12,4},... | collective-permute-start | bytes 387080 | tf_op jit(solution)/shard_map/ppermute | solution.py:42
  31.2 11.5 %collective-permute-start.1 = (bf16[2,224,288]{1,2,0:T(8,128)(2,1)}, bf16[2,224,288]{1,2,0:T(8,128)(2,1)S(1)}, u32[]{:S(2)}, u32[]{:S(2)}) collective-permute-start(bf16[2,224,288]{1,2,0:T(8,128)(2,1)} %broadcast_select_fusion.1), channel_id=1, source_target_pairs={{0,16},{16,32},{32,48},{48,0},{1,17},{17,33},{33,49},{49,1},{2,18}... | collective-permute-start | bytes 774152 | tf_op jit(solution)/shard_map/ppermute | solution.py:42
  34.3 15.7 %collective-permute-start.2 = (bf16[2,224,288]{1,2,0:T(8,128)(2,1)}, bf16[2,224,288]{1,2,0:T(8,128)(2,1)S(1)}, u32[]{:S(2)}, u32[]{:S(2)}) collective-permute-start(bf16[2,224,288]{1,2,0:T(8,128)(2,1)} %broadcast_select_fusion.1), channel_id=1, source_target_pairs={{0,32},{16,48},{32,0},{48,16},{1,33},{17,49},{33,1},{49,17},{2,34}... | collective-permute-start | bytes 774152 | tf_op jit(solution)/shard_map/ppermute | solution.py:42
  38.7 12.7 %collective-permute-start.3 = (bf16[2,224,288]{1,2,0:T(8,128)(2,1)}, bf16[2,224,288]{1,2,0:T(8,128)(2,1)S(1)}, u32[]{:S(2)}, u32[]{:S(2)}) collective-permute-start(bf16[2,224,288]{1,2,0:T(8,128)(2,1)} %broadcast_select_fusion.1), channel_id=1, source_target_pairs={{0,48},{16,0},{32,16},{48,32},{1,49},{17,1},{33,17},{49,33},{2,50}... | collective-permute-start | bytes 774152 | tf_op jit(solution)/shard_map/ppermute | solution.py:42
  67.6 0.7 copy-start.2
  68.7 6.2 %copy-start.4 = (bf16[224,512]{1,0:T(8,128)(2,1)S(1)}, bf16[224,512]{1,0:T(8,128)(2,1)}, u32[]{:S(2)}) copy-start(bf16[224,512]{1,0:T(8,128)(2,1)} %param.8) | copy-start | bytes 688132
  69.6 29.4 %all-to-all-start.1 = ((bf16[8,3,7644]{2,1,0:T(4,128)(2,1)}), bf16[8,3,7644]{2,1,0:T(4,128)(2,1)S(1)}, u32[]{:S(2)}, u32[]{:S(2)}) async-start(bf16[8,3,7644]{2,1,0:T(4,128)(2,1)} %broadcast_in_dim.159), calls=%async_computation.1 | async-start | bytes 983040 | tf_op jit(solution)/shard_map/all_to_all | solution.py:93
  75.6 1.4 copy-start.1
  78.2 29.3 %copy-start.9 = (f32[224]{0:T(256)S(1)}, f32[224]{0:T(256)}, u32[]{:S(2)}) copy-start(f32[224]{0:T(256)} %param.11) | copy-start | bytes 2692
  78.2 60.2 %collective-permute-start.4 = (bf16[576,512]{1,0:T(8,128)(2,1)}, bf16[576,512]{1,0:T(8,128)(2,1)}, u32[]{:S(2)}, u32[]{:S(2)}) collective-permute-start(bf16[576,512]{1,0:T(8,128)(2,1)} %get-tuple-element.11), channel_id=1, source_target_pairs={{0,2},{2,4},{4,6},{6,0},{1,3},{3,5},{5,7},{7,1},{8,10},{10,12},{12... | collective-permute-start | bytes 1769480 | tf_op jit(solution)/shard_map/ppermute | solution.py:53
  81.5 57.0 %collective-permute-start.5 = (bf16[576,512]{1,0:T(8,128)(2,1)}, bf16[576,512]{1,0:T(8,128)(2,1)}, u32[]{:S(2)}, u32[]{:S(2)}) collective-permute-start(bf16[576,512]{1,0:T(8,128)(2,1)} %get-tuple-element.13), channel_id=1, source_target_pairs={{0,4},{2,6},{4,0},{6,2},{1,5},{3,7},{5,1},{7,3},{8,12},{10,14},{12... | collective-permute-start | bytes 1769480 | tf_op jit(solution)/shard_map/ppermute | solution.py:53
  86.1 52.4 %collective-permute-start.6 = (bf16[576,512]{1,0:T(8,128)(2,1)S(1)}, bf16[576,512]{1,0:T(8,128)(2,1)}, u32[]{:S(2)}, u32[]{:S(2)}) collective-permute-start(bf16[576,512]{1,0:T(8,128)(2,1)S(1)} %get-tuple-element.12), channel_id=1, source_target_pairs={{0,6},{2,0},{4,2},{6,4},{1,7},{3,1},{5,3},{7,5},{8,14},{10,8},{12,... | collective-permute-start | bytes 1769480 | tf_op jit(solution)/shard_map/ppermute | solution.py:53
  102.1 22.0 %all-to-all-start.2 = ((bf16[8,2,3822]{2,1,0:T(2,128)(2,1)}), bf16[8,2,3822]{2,1,0:T(2,128)(2,1)S(1)}, u32[]{:S(2)}, u32[]{:S(2)}) async-start(bf16[8,2,3822]{2,1,0:T(2,128)(2,1)} %reshape.489), calls=%async_computation.2 | async-start | bytes 245760 | tf_op jit(solution)/shard_map/all_to_all | solution.py:96
  107.5 16.5 %collective-permute-start.9 = (f32[224]{0:T(256)S(1)}, f32[224]{0:T(256)S(1)}, u32[]{:S(2)}, u32[]{:S(2)}) collective-permute-start(f32[224]{0:T(256)S(1)} %copy-done.9), channel_id=1, source_target_pairs={{0,0},{1,8},{2,16},{3,24},{4,32},{5,40},{6,48},{7,56},{8,1},{9,9},... | collective-permute-start | bytes 2696 | tf_op jit(solution)/shard_map/ppermute | solution.py:127
  124.3 19.9 %collective-permute-start.7 = (bf16[8,7644]{1,0:T(8,128)(2,1)S(1)}, bf16[8,7644]{1,0:T(8,128)(2,1)S(1)}, u32[]{:S(2)}, u32[]{:S(2)}) collective-permute-start(bf16[8,7644]{1,0:T(8,128)(2,1)S(1)} %bitcast.99), channel_id=1, source_target_pairs={{0,0},{1,8},{2,16},{3,24},{4,32},{5,40},{6,48},{7,56},{8,1},{9,9},... | collective-permute-start | bytes 366920 | tf_op jit(solution)/shard_map/ppermute | solution.py:97
  144.5 32.2 %collective-permute-start.8 = (bf16[288,512]{1,0:T(8,128)(2,1)S(1)}, bf16[288,512]{1,0:T(8,128)(2,1)S(1)}, u32[]{:S(2)}, u32[]{:S(2)}) collective-permute-start(bf16[288,512]{1,0:T(8,128)(2,1)S(1)} %constant_dynamic-slice_fusion), channel_id=1, source_target_pairs={{0,1},{1,0},{2,3},{3,2},{4,5},{5,4},{6,7},{7,6},{8,9},{9,8},{10,11... | collective-permute-start | bytes 884744 | tf_op jit(solution)/shard_map/ppermute | solution.py:53
  178.7 2.0 copy-start.8
  180.6 4.6 %collective-permute-start.10 = (bf16[224,224]{1,0:T(8,128)(2,1)S(1)}, bf16[224,224]{1,0:T(8,128)(2,1)S(1)}, u32[]{:S(2)}, u32[]{:S(2)}) collective-permute-start(bf16[224,224]{1,0:T(8,128)(2,1)S(1)} %copy-done.8), channel_id=1, source_target_pairs={{0,8},{8,0},{1,9},{9,1},{2,10},{10,2},{3,11},{11,3},{4,12},{12,4},... | collective-permute-start | bytes 301064 | tf_op jit(solution)/shard_map/ppermute | solution.py:42
  183.2 18.0 %collective-permute-start.14 = (bf16[512,224]{0,1:T(8,128)(2,1)S(1)}, bf16[512,224]{0,1:T(8,128)(2,1)S(1)}, u32[]{:S(2)}, u32[]{:S(2)}) collective-permute-start(bf16[512,224]{0,1:T(8,128)(2,1)S(1)} %bitcast.82), channel_id=1, source_target_pairs={{0,1},{1,0},{2,3},{3,2},{4,5},{5,4},{6,7},{7,6},{8,9},{9,8},{10,11... | collective-permute-start | bytes 688136 | tf_op jit(solution)/shard_map/ppermute | solution.py:42
  186.7 44.9 %collective-permute-start.11 = (bf16[2,224,224]{2,1,0:T(8,128)(2,1)}, bf16[2,224,224]{2,1,0:T(8,128)(2,1)S(1)}, u32[]{:S(2)}, u32[]{:S(2)}) collective-permute-start(bf16[2,224,224]{2,1,0:T(8,128)(2,1)} %broadcast_select_fusion.2), channel_id=1, source_target_pairs={{0,16},{16,32},{32,48},{48,0},{1,17},{17,33},{33,49},{49,1},{2,18}... | collective-permute-start | bytes 602120 | tf_op jit(solution)/shard_map/ppermute | solution.py:42
  188.6 45.9 %collective-permute-start.12 = (bf16[2,224,224]{2,1,0:T(8,128)(2,1)}, bf16[2,224,224]{2,1,0:T(8,128)(2,1)S(1)}, u32[]{:S(2)}, u32[]{:S(2)}) collective-permute-start(bf16[2,224,224]{2,1,0:T(8,128)(2,1)} %broadcast_select_fusion.2), channel_id=1, source_target_pairs={{0,32},{16,48},{32,0},{48,16},{1,33},{17,49},{33,1},{49,17},{2,34}... | collective-permute-start | bytes 602120 | tf_op jit(solution)/shard_map/ppermute | solution.py:42
  202.6 42.5 %collective-permute-start.15 = (bf16[2,512,224]{1,2,0:T(8,128)(2,1)}, bf16[2,512,224]{1,2,0:T(8,128)(2,1)}, u32[]{:S(2)}, u32[]{:S(2)}) collective-permute-start(bf16[2,512,224]{1,2,0:T(8,128)(2,1)} %broadcast_select_fusion), channel_id=1, source_target_pairs={{0,2},{2,4},{4,6},{6,0},{1,3},{3,5},{5,7},{7,1},{8,10},{10,12},{12... | collective-permute-start | bytes 1376264 | tf_op jit(solution)/shard_map/ppermute | solution.py:42
  225.9 19.2 %collective-permute-start.16 = (bf16[2,512,224]{1,2,0:T(8,128)(2,1)}, bf16[2,512,224]{1,2,0:T(8,128)(2,1)}, u32[]{:S(2)}, u32[]{:S(2)}) collective-permute-start(bf16[2,512,224]{1,2,0:T(8,128)(2,1)} %broadcast_select_fusion), channel_id=1, source_target_pairs={{0,4},{2,6},{4,0},{6,2},{1,5},{3,7},{5,1},{7,3},{8,12},{10,14},{12... | collective-permute-start | bytes 1376264 | tf_op jit(solution)/shard_map/ppermute | solution.py:42
  227.8 24.1 %collective-permute-start.17 = (bf16[2,512,224]{1,2,0:T(8,128)(2,1)}, bf16[2,512,224]{1,2,0:T(8,128)(2,1)}, u32[]{:S(2)}, u32[]{:S(2)}) collective-permute-start(bf16[2,512,224]{1,2,0:T(8,128)(2,1)} %broadcast_select_fusion), channel_id=1, source_target_pairs={{0,6},{2,0},{4,2},{6,4},{1,7},{3,1},{5,3},{7,5},{8,14},{10,8},{12,... | collective-permute-start | bytes 1376264 | tf_op jit(solution)/shard_map/ppermute | solution.py:42
  231.6 7.5 %copy-start.5 = (bf16[2,224,224]{2,1,0:T(8,128)(2,1)}, bf16[2,224,224]{2,1,0:T(8,128)(2,1)S(1)}, u32[]{:S(2)}) copy-start(bf16[2,224,224]{2,1,0:T(8,128)(2,1)S(1)} %collective-permute-done.11) | copy-start | bytes 602116
  231.7 7.5 %collective-permute-start.13 = (bf16[2,224,224]{2,1,0:T(8,128)(2,1)}, bf16[2,224,224]{2,1,0:T(8,128)(2,1)S(1)}, u32[]{:S(2)}, u32[]{:S(2)}) collective-permute-start(bf16[2,224,224]{2,1,0:T(8,128)(2,1)} %broadcast_select_fusion.2), channel_id=1, source_target_pairs={{0,48},{16,0},{32,16},{48,32},{1,49},{17,1},{33,17},{49,33},{2,50}... | collective-permute-start | bytes 602120 | tf_op jit(solution)/shard_map/ppermute | solution.py:42
  234.5 4.7 %copy-start.6 = (bf16[2,224,224]{2,1,0:T(8,128)(2,1)}, bf16[2,224,224]{2,1,0:T(8,128)(2,1)S(1)}, u32[]{:S(2)}) copy-start(bf16[2,224,224]{2,1,0:T(8,128)(2,1)S(1)} %collective-permute-done.12) | copy-start | bytes 602116
  255.5 1.8 copy-start.3

commit v9 on v4

--- a/solution.py
+++ b/solution.py
@@ -78,16 +78,31 @@
     )
     state_shape = partial_state.shape[1:]
     piece = partial_state[0].size // n_col
+    n_y = n_col // 2
+    width = pref_here * piece
     pieces = partial_state.astype(jnp.bfloat16).reshape(pref_here, n_col, piece)
-    pieces = jnp.swapaxes(pieces, 0, 1).reshape(n_col, pref_here * piece)
+    pieces = jnp.swapaxes(pieces, 0, 1).reshape(n_y, 2, width)
     meta = jnp.stack([prefix_owner[0], suffix_len[0] // 16, suffix_len[0] % 16])
-    meta = jnp.broadcast_to(meta.astype(jnp.bfloat16)[None], (n_col, 3))
-    got = lax.all_to_all(jnp.concatenate([pieces, meta], axis=1), COL, 0, 0, tiled=True)
-    meta = got[:, pref_here * piece :].astype(jnp.int32)
+    meta = jnp.broadcast_to(meta.astype(jnp.bfloat16)[None, None], (n_y, 2, 3))
+    got = lax.all_to_all(jnp.concatenate([pieces, meta], axis=2), "y", 0, 0, tiled=True)
+    meta_y = got[:, 0, width:]
+    half = jnp.sum(got[:, :, :width].astype(jnp.float32), axis=0).astype(jnp.bfloat16)
+    zh_here = lax.axis_index("zh")
+    mine = lax.dynamic_index_in_dim(half, zh_here, keepdims=False)
+    other = lax.dynamic_index_in_dim(half, 1 - zh_here, keepdims=False)
+    recv = lax.ppermute(
+        jnp.concatenate([other, meta_y.reshape(-1)]), "zh", [(0, 1), (1, 0)]
+    )
+    pieces = (mine.astype(jnp.float32) + recv[:width].astype(jnp.float32)).astype(jnp.bfloat16)
+    pieces = pieces.reshape(pref_here, piece)
+    meta_other = recv[width:].reshape(n_y, 3)
+    meta = jnp.where(
+        zh_here == 0,
+        jnp.stack([meta_y, meta_other], axis=1),
+        jnp.stack([meta_other, meta_y], axis=1),
+    ).reshape(n_col, 3).astype(jnp.int32)
     owners = meta[:, 0]
     lens = meta[:, 1] * 16 + meta[:, 2]
-    pieces = got[:, : pref_here * piece].reshape(n_col, pref_here, piece)
-    pieces = jnp.sum(pieces.astype(jnp.float32), axis=0).astype(jnp.bfloat16)
     n_req = lax.psum(1, "req")
     pieces = jnp.broadcast_to(pieces[None], (n_req,) + pieces.shape)
     pieces = lax.all_to_all(pieces, "req", 0, 0, tiled=True)

time: 245 us -> 241 us (0.984)
  the two profiles are of different devices: /device:TPU:15 before, /device:TPU:1 now
where the time goes in v9:
time: 241 us; the launch traced here: 237 us
  starting transfers between devices  119 us (49%)
  waiting for transfers between devices  58.5 us (24%)
  other arithmetic  26 us (11%)
  local copies, waits for them, and re-layouts  24.3 us (10%)
  matrix products  7.27 us (3%)
    ppermute x12, starting transfers between devices, gather_by_shifts(): lax.ppermute(x, axis, [(i, (i + k) % n) for i in range(n)])  66.3 us
    ppermute x4, waiting for transfers between devices, reduce_scatter_by_shifts(): lax.ppermute(part, axis, [(i, (i + k) % n) for i in range(n)])  22.4 us
    ppermute x12, waiting for transfers between devices, gather_by_shifts(): lax.ppermute(x, axis, [(i, (i + k) % n) for i in range(n)])  12.4 us
    ppermute x1, waiting for transfers between devices, shards(): lax.ppermute(jnp.concatenate([other, meta_y.reshape(-1)]), 'zh', [(0, 1),...  11.9 us
    ppermute x1, starting transfers between devices, shards(): chosen = lax.ppermute(chosen, flat, perm)  11.3 us
    ppermute x1, starting transfers between devices, shards(): gains = lax.ppermute(head_gain, flat, perm).reshape(heads_here, HD)  11 us
    ppermute x4, starting transfers between devices, reduce_scatter_by_shifts(): lax.ppermute(part, axis, [(i, (i + k) % n) for i in range(n)])  10.2 us
    gather x7, local copies, waits for them, and re-layouts, gather_by_shifts(): return jnp.take(stacked, (me - jnp.arange(n)) % n, axis=0)  9.79 us
  transfers between devices with their start and end apart: 22, of which 8 were waited for; matrix products, arithmetic and copies ran while one was open for 15% of the time, Pallas kernels for 0%

profile of v9, /device:TPU:1, one launch (start us, length us, event | category | flops | bytes accessed | tf_op | source)
XLA Modules:
  0.0 237.1 jit_solution(11730639874415143900)
XLA Ops:
  0.8 1.0 convert.42
  1.7 1.0 multiply_convert_fusion.3
  4.9 1.3 fusion.7
  8.0 1.2 pad_maximum_fusion.4
  9.1 5.0 %all-to-all-start = ((bf16[4,2,22935]{2,1,0:T(2,128)(2,1)}), bf16[4,2,22935]{2,1,0:T(2,128)(2,1)S(1)}, u32[]{:S(2)}, u32[]{:S(2)}) async-start(bf16[4,2,22935]{2,1,0:T(2,128)(2,1)} %pad_maximum_fusion.4), calls=%async_computation | async-start | bytes 737280 | tf_op jit(solution)/shard_map/all_to_all | solution.py:87
  14.1 7.2 %collective-permute-start.5 = (bf16[224,288]{0,1:T(8,128)(2,1)S(1)}, bf16[224,288]{0,1:T(8,128)(2,1)S(1)}, u32[]{:S(2)}, u32[]{:S(2)}) collective-permute-start(bf16[224,288]{0,1:T(8,128)(2,1)S(1)} %copy-done.6), channel_id=1, source_target_pairs={{0,8},{8,0},{1,9},{9,1},{2,10},{10,2},{3,11},{11,3},{4,12},{12,4},... | collective-permute-start | bytes 387080 | tf_op jit(solution)/shard_map/ppermute | solution.py:42
  21.3 11.0 %collective-permute-start.14 = (f32[224]{0:T(256)}, f32[224]{0:T(256)}, u32[]{:S(2)}, u32[]{:S(2)}) collective-permute-start(f32[224]{0:T(256)} %param.11), channel_id=1, source_target_pairs={{0,0},{1,8},{2,16},{3,24},{4,32},{5,40},{6,48},{7,56},{8,1},{9,9},... | collective-permute-start | bytes 2696 | tf_op jit(solution)/shard_map/ppermute | solution.py:142
  32.3 1.9 collective-permute-start
  38.8 4.5 %collective-permute-start.6 = (bf16[2,224,288]{1,2,0:T(8,128)(2,1)}, bf16[2,224,288]{1,2,0:T(8,128)(2,1)S(1)}, u32[]{:S(2)}, u32[]{:S(2)}) collective-permute-start(bf16[2,224,288]{1,2,0:T(8,128)(2,1)} %broadcast_select_fusion.1), channel_id=1, source_target_pairs={{0,16},{16,32},{32,48},{48,0},{1,17},{17,33},{33,49},{49,1},{2,18}... | collective-permute-start | bytes 774152 | tf_op jit(solution)/shard_map/ppermute | solution.py:42
  43.3 5.5 %collective-permute-start.7 = (bf16[2,224,288]{1,2,0:T(8,128)(2,1)}, bf16[2,224,288]{1,2,0:T(8,128)(2,1)S(1)}, u32[]{:S(2)}, u32[]{:S(2)}) collective-permute-start(bf16[2,224,288]{1,2,0:T(8,128)(2,1)} %broadcast_select_fusion.1), channel_id=1, source_target_pairs={{0,32},{16,48},{32,0},{48,16},{1,33},{17,49},{33,1},{49,17},{2,34}... | collective-permute-start | bytes 774152 | tf_op jit(solution)/shard_map/ppermute | solution.py:42
  49.8 3.3 %collective-permute-start.4 = (bf16[22944]{0:T(1024)(128)(2,1)S(1)}, bf16[22944]{0:T(1024)(128)(2,1)S(1)}, u32[]{:S(2)}, u32[]{:S(2)}) collective-permute-start(bf16[22944]{0:T(1024)(128)(2,1)S(1)} %pad_maximum_fusion.9), channel_id=1, source_target_pairs={{0,1},{1,0},{2,3},{3,2},{4,5},{5,4},{6,7},{7,6},{8,9},{9,8},{10,11... | collective-permute-start | bytes 137672 | tf_op jit(solution)/shard_map/ppermute | solution.py:93
  53.7 11.9 %collective-permute-done.4 = bf16[22944]{0:T(1024)(128)(2,1)S(1)} collective-permute-done((bf16[22944]{0:T(1024)(128)(2,1)S(1)}, bf16[22944]{0:T(1024)(128)(2,1)S(1)}, u32[]{:S(2)}, u32[]{:S(2)}) %collective-permute-start.4) | collective-permute-done | bytes 45920 | tf_op jit(solution)/shard_map/ppermute | solution.py:93
  65.6 3.4 %collective-permute-start.8 = (bf16[2,224,288]{1,2,0:T(8,128)(2,1)}, bf16[2,224,288]{1,2,0:T(8,128)(2,1)}, u32[]{:S(2)}, u32[]{:S(2)}) collective-permute-start(bf16[2,224,288]{1,2,0:T(8,128)(2,1)} %broadcast_select_fusion.1), channel_id=1, source_target_pairs={{0,48},{16,0},{32,16},{48,32},{1,49},{17,1},{33,17},{49,33},{2,50}... | collective-permute-start | bytes 774152 | tf_op jit(solution)/shard_map/ppermute | solution.py:42
  70.1 3.5 %all-to-all-start.1 = ((bf16[8,3,7644]{2,1,0:T(4,128)(2,1)}), bf16[8,3,7644]{2,1,0:T(4,128)(2,1)S(1)}, u32[]{:S(2)}, u32[]{:S(2)}) async-start(bf16[8,3,7644]{2,1,0:T(4,128)(2,1)} %broadcast_in_dim.163), calls=%async_computation.1 | async-start | bytes 983040 | tf_op jit(solution)/shard_map/all_to_all | solution.py:108
  75.8 2.3 pad_maximum_fusion.1
  78.1 2.0 gather_fusion.3
  81.8 1.4 copy-done.1
  83.3 1.3 constant_dynamic-slice_fusion.3
  84.5 2.0 collective-permute-start.10
  86.6 4.1 %collective-permute-start.11 = (bf16[576,512]{1,0:T(8,128)(2,1)}, bf16[576,512]{1,0:T(8,128)(2,1)}, u32[]{:S(2)}, u32[]{:S(2)}) collective-permute-start(bf16[576,512]{1,0:T(8,128)(2,1)} %get-tuple-element.10), channel_id=1, source_target_pairs={{0,6},{2,0},{4,2},{6,4},{1,7},{3,1},{5,3},{7,5},{8,14},{10,8},{12,... | collective-permute-start | bytes 1769480 | tf_op jit(solution)/shard_map/ppermute | solution.py:53
  90.7 1.9 collective-permute-start.9
  96.6 8.3 %all-to-all-start.2 = ((bf16[8,2,3822]{2,1,0:T(2,128)(2,1)}), bf16[8,2,3822]{2,1,0:T(2,128)(2,1)S(1)}, u32[]{:S(2)}, u32[]{:S(2)}) async-start(bf16[8,2,3822]{2,1,0:T(2,128)(2,1)} %reshape.520), calls=%async_computation.2 | async-start | bytes 245760 | tf_op jit(solution)/shard_map/all_to_all | solution.py:111
  108.6 1.2 constant_dynamic-slice_fusion.4
  109.8 9.2 %all-to-all-done.2 = bf16[8,2,3822]{2,1,0:T(2,128)(2,1)S(1)} async-done(((bf16[8,2,3822]{2,1,0:T(2,128)(2,1)}), bf16[8,2,3822]{2,1,0:T(2,128)(2,1)S(1)}, u32[]{:S(2)}, u32[]{:S(2)}) %all-to-all-start.2) | async-done | bytes 122336 | tf_op jit(solution)/shard_map/all_to_all | solution.py:111
  119.3 11.3 %collective-permute-start.12 = (bf16[8,7644]{1,0:T(8,128)(2,1)S(1)}, bf16[8,7644]{1,0:T(8,128)(2,1)S(1)}, u32[]{:S(2)}, u32[]{:S(2)}) collective-permute-start(bf16[8,7644]{1,0:T(8,128)(2,1)S(1)} %bitcast.91), channel_id=1, source_target_pairs={{0,0},{1,8},{2,16},{3,24},{4,32},{5,40},{6,48},{7,56},{8,1},{9,9},... | collective-permute-start | bytes 366920 | tf_op jit(solution)/shard_map/ppermute | solution.py:112
  130.6 1.9 add_convert_fusion
  132.5 1.7 collective-permute-done.12
  134.3 0.9 reshape.454
  135.3 2.1 collective-permute-start.13
  138.8 22.4 %collective-permute-done.13 = bf16[288,512]{1,0:T(8,128)(2,1)S(1)} collective-permute-done((bf16[288,512]{1,0:T(8,128)(2,1)S(1)}, bf16[288,512]{1,0:T(8,128)(2,1)S(1)}, u32[]{:S(2)}, u32[]{:S(2)}) %collective-permute-start.13) | collective-permute-done | bytes 294944 | tf_op jit(solution)/shard_map/ppermute | solution.py:53
  161.5 2.7 %fusion.6 = f32[2,112,512]{2,1,0:T(8,128)} fusion(pred[512,512]{1,0:T(8,128)(4,1)} %fusion.16, bf16[512,2,144]{0,2,1:T(8,128)(2,1)S(1)} %bitcast.85), kind=kOutput, calls=%fused_computation.19 | convolution fusion | flops 137887744 | bytes 1015808 | tf_op jit(solution)/shard_map/hts,shv->thv/dot_general | solution.py:138
  164.2 1.8 multiply_reduce_fusion
  166.1 1.9 collective-permute-start.15
  168.9 3.4 %collective-permute-start.1 = (bf16[2,224,224]{2,1,0:T(8,128)(2,1)}, bf16[2,224,224]{2,1,0:T(8,128)(2,1)}, u32[]{:S(2)}, u32[]{:S(2)}) collective-permute-start(bf16[2,224,224]{2,1,0:T(8,128)(2,1)} %broadcast_select_fusion.2), channel_id=1, source_target_pairs={{0,16},{16,32},{32,48},{48,0},{1,17},{17,33},{33,49},{49,1},{2,18}... | collective-permute-start | bytes 602120 | tf_op jit(solution)/shard_map/ppermute | solution.py:42
  172.2 7.3 %collective-permute-start.2 = (bf16[2,224,224]{2,1,0:T(8,128)(2,1)}, bf16[2,224,224]{2,1,0:T(8,128)(2,1)}, u32[]{:S(2)}, u32[]{:S(2)}) collective-permute-start(bf16[2,224,224]{2,1,0:T(8,128)(2,1)} %broadcast_select_fusion.2), channel_id=1, source_target_pairs={{0,32},{16,48},{32,0},{48,16},{1,33},{17,49},{33,1},{49,17},{2,34}... | collective-permute-start | bytes 602120 | tf_op jit(solution)/shard_map/ppermute | solution.py:42
  179.5 4.0 %collective-permute-start.3 = (bf16[2,224,224]{2,1,0:T(8,128)(2,1)}, bf16[2,224,224]{2,1,0:T(8,128)(2,1)}, u32[]{:S(2)}, u32[]{:S(2)}) collective-permute-start(bf16[2,224,224]{2,1,0:T(8,128)(2,1)} %broadcast_select_fusion.2), channel_id=1, source_target_pairs={{0,48},{16,0},{32,16},{48,32},{1,49},{17,1},{33,17},{49,33},{2,50}... | collective-permute-start | bytes 602120 | tf_op jit(solution)/shard_map/ppermute | solution.py:42
  183.5 2.9 %collective-permute-done.15 = bf16[512,224]{0,1:T(8,128)(2,1)S(1)} collective-permute-done((bf16[512,224]{0,1:T(8,128)(2,1)S(1)}, bf16[512,224]{0,1:T(8,128)(2,1)S(1)}, u32[]{:S(2)}, u32[]{:S(2)}) %collective-permute-start.15) | collective-permute-done | bytes 229408 | tf_op jit(solution)/shard_map/ppermute | solution.py:42
  187.9 21.0 %collective-permute-start.16 = (bf16[2,512,224]{1,2,0:T(8,128)(2,1)}, bf16[2,512,224]{1,2,0:T(8,128)(2,1)S(1)}, u32[]{:S(2)}, u32[]{:S(2)}) collective-permute-start(bf16[2,512,224]{1,2,0:T(8,128)(2,1)} %broadcast_select_fusion), channel_id=1, source_target_pairs={{0,2},{2,4},{4,6},{6,0},{1,3},{3,5},{5,7},{7,1},{8,10},{10,12},{12... | collective-permute-start | bytes 1376264 | tf_op jit(solution)/shard_map/ppermute | solution.py:42
  208.9 1.9 collective-permute-start.17
  210.9 4.3 %collective-permute-start.18 = (bf16[2,512,224]{1,2,0:T(8,128)(2,1)}, bf16[2,512,224]{1,2,0:T(8,128)(2,1)}, u32[]{:S(2)}, u32[]{:S(2)}) collective-permute-start(bf16[2,512,224]{1,2,0:T(8,128)(2,1)} %broadcast_select_fusion), channel_id=1, source_target_pairs={{0,6},{2,0},{4,2},{6,4},{1,7},{3,1},{5,3},{7,5},{8,14},{10,8},{12,... | collective-permute-start | bytes 1376264 | tf_op jit(solution)/shard_map/ppermute | solution.py:42
  215.3 1.4 pad_maximum_fusion.2
  216.7 1.7 gather_fusion.1
  218.4 2.2 copy.24
  220.7 7.8 %collective-permute-done.17 = bf16[2,512,224]{1,2,0:T(8,128)(2,1)} collective-permute-done((bf16[2,512,224]{1,2,0:T(8,128)(2,1)}, bf16[2,512,224]{1,2,0:T(8,128)(2,1)}, u32[]{:S(2)}, u32[]{:S(2)}) %collective-permute-start.17) | collective-permute-done | bytes 458784 | tf_op jit(solution)/shard_map/ppermute | solution.py:42
  228.5 1.8 collective-permute-done.18
  230.2 1.5 pad_maximum_fusion
  231.8 2.1 gather_fusion.6
  233.8 1.8 bitcast_select_fusion
  (126 shorter events, 27.6 us)
Async XLA Ops:
  0.0 4.3 %copy-start = (bf16[3,224,1024]{2,1,0:T(8,128)(2,1)S(1)}, bf16[3,224,1024]{2,1,0:T(8,128)(2,1)}, u32[]{:S(2)}) copy-start(bf16[3,224,1024]{2,1,0:T(8,128)(2,1)} %param.13) | copy-start | bytes 4128772
  4.3 0.5 copy-start.13
  7.1 7.0 %copy-start.6 = (bf16[224,288]{0,1:T(8,128)(2,1)S(1)}, bf16[224,288]{0,1:T(8,128)(2,1)}, u32[]{:S(2)}) copy-start(bf16[224,288]{0,1:T(8,128)(2,1)} %param.9) | copy-start | bytes 387076
  7.1 25.2 %copy-start.7 = (bf16[224,224]{1,0:T(8,128)(2,1)S(1)}, bf16[224,224]{1,0:T(8,128)(2,1)}, u32[]{:S(2)}) copy-start(bf16[224,224]{1,0:T(8,128)(2,1)} %param.10) | copy-start | bytes 301060
  9.1 39.7 %all-to-all-start = ((bf16[4,2,22935]{2,1,0:T(2,128)(2,1)}), bf16[4,2,22935]{2,1,0:T(2,128)(2,1)S(1)}, u32[]{:S(2)}, u32[]{:S(2)}) async-start(bf16[4,2,22935]{2,1,0:T(2,128)(2,1)} %pad_maximum_fusion.4), calls=%async_computation | async-start | bytes 737280 | tf_op jit(solution)/shard_map/all_to_all | solution.py:87
  14.1 23.2 %collective-permute-start.5 = (bf16[224,288]{0,1:T(8,128)(2,1)S(1)}, bf16[224,288]{0,1:T(8,128)(2,1)S(1)}, u32[]{:S(2)}, u32[]{:S(2)}) collective-permute-start(bf16[224,288]{0,1:T(8,128)(2,1)S(1)} %copy-done.6), channel_id=1, source_target_pairs={{0,8},{8,0},{1,9},{9,1},{2,10},{10,2},{3,11},{11,3},{4,12},{12,4},... | collective-permute-start | bytes 387080 | tf_op jit(solution)/shard_map/ppermute | solution.py:42
  21.3 84.9 %collective-permute-start.14 = (f32[224]{0:T(256)}, f32[224]{0:T(256)}, u32[]{:S(2)}, u32[]{:S(2)}) collective-permute-start(f32[224]{0:T(256)} %param.11), channel_id=1, source_target_pairs={{0,0},{1,8},{2,16},{3,24},{4,32},{5,40},{6,48},{7,56},{8,1},{9,9},... | collective-permute-start | bytes 2696 | tf_op jit(solution)/shard_map/ppermute | solution.py:142
  32.3 74.6 %collective-permute-start = (bf16[224,224]{1,0:T(8,128)(2,1)S(1)}, bf16[224,224]{1,0:T(8,128)(2,1)}, u32[]{:S(2)}, u32[]{:S(2)}) collective-permute-start(bf16[224,224]{1,0:T(8,128)(2,1)S(1)} %copy-done.7), channel_id=1, source_target_pairs={{0,8},{8,0},{1,9},{9,1},{2,10},{10,2},{3,11},{11,3},{4,12},{12,4},... | collective-permute-start | bytes 301064 | tf_op jit(solution)/shard_map/ppermute | solution.py:42
  34.8 18.9 %copy-start.8 = (pred[2]{0:T(512)(128)(4,1)}, pred[2]{0:T(512)(128)(4,1)S(1)}, u32[]{:S(2)}) copy-start(pred[2]{0:T(512)(128)(4,1)S(1)} %get-tuple-element.19) | copy-start | bytes 10
  34.8 14.1 %copy-start.10 = (s32[1024]{0:T(1024)}, s32[1024]{0:T(1024)S(1)}, u32[]{:S(2)}) copy-start(s32[1024]{0:T(1024)S(1)} %pad_clamp_fusion.4) | copy-start | bytes 12292
  38.8 37.0 %collective-permute-start.6 = (bf16[2,224,288]{1,2,0:T(8,128)(2,1)}, bf16[2,224,288]{1,2,0:T(8,128)(2,1)S(1)}, u32[]{:S(2)}, u32[]{:S(2)}) collective-permute-start(bf16[2,224,288]{1,2,0:T(8,128)(2,1)} %broadcast_select_fusion.1), channel_id=1, source_target_pairs={{0,16},{16,32},{32,48},{48,0},{1,17},{17,33},{33,49},{49,1},{2,18}... | collective-permute-start | bytes 774152 | tf_op jit(solution)/shard_map/ppermute | solution.py:42
  43.3 32.5 %collective-permute-start.7 = (bf16[2,224,288]{1,2,0:T(8,128)(2,1)}, bf16[2,224,288]{1,2,0:T(8,128)(2,1)S(1)}, u32[]{:S(2)}, u32[]{:S(2)}) collective-permute-start(bf16[2,224,288]{1,2,0:T(8,128)(2,1)} %broadcast_select_fusion.1), channel_id=1, source_target_pairs={{0,32},{16,48},{32,0},{48,16},{1,33},{17,49},{33,1},{49,17},{2,34}... | collective-permute-start | bytes 774152 | tf_op jit(solution)/shard_map/ppermute | solution.py:42
  49.8 15.8 %collective-permute-start.4 = (bf16[22944]{0:T(1024)(128)(2,1)S(1)}, bf16[22944]{0:T(1024)(128)(2,1)S(1)}, u32[]{:S(2)}, u32[]{:S(2)}) collective-permute-start(bf16[22944]{0:T(1024)(128)(2,1)S(1)} %pad_maximum_fusion.9), channel_id=1, source_target_pairs={{0,1},{1,0},{2,3},{3,2},{4,5},{5,4},{6,7},{7,6},{8,9},{9,8},{10,11... | collective-permute-start | bytes 137672 | tf_op jit(solution)/shard_map/ppermute | solution.py:93
  65.6 10.2 %collective-permute-start.8 = (bf16[2,224,288]{1,2,0:T(8,128)(2,1)}, bf16[2,224,288]{1,2,0:T(8,128)(2,1)}, u32[]{:S(2)}, u32[]{:S(2)}) collective-permute-start(bf16[2,224,288]{1,2,0:T(8,128)(2,1)} %broadcast_select_fusion.1), channel_id=1, source_target_pairs={{0,48},{16,0},{32,16},{48,32},{1,49},{17,1},{33,17},{49,33},{2,50}... | collective-permute-start | bytes 774152 | tf_op jit(solution)/shard_map/ppermute | solution.py:42
  70.1 23.3 %all-to-all-start.1 = ((bf16[8,3,7644]{2,1,0:T(4,128)(2,1)}), bf16[8,3,7644]{2,1,0:T(4,128)(2,1)S(1)}, u32[]{:S(2)}, u32[]{:S(2)}) async-start(bf16[8,3,7644]{2,1,0:T(4,128)(2,1)} %broadcast_in_dim.163), calls=%async_computation.1 | async-start | bytes 983040 | tf_op jit(solution)/shard_map/all_to_all | solution.py:108
  78.1 2.0 copy-start.15
  80.1 0.9 copy-start.3
  81.8 1.4 copy-start.1
  84.5 9.9 %copy-start.12 = (pred[8]{0:T(512)(128)(4,1)S(1)}, pred[8]{0:T(512)(128)(4,1)}, u32[]{:S(2)}) copy-start(pred[8]{0:T(512)(128)(4,1)} %and_reduce_fusion) | copy-start | bytes 28
  84.5 20.3 %copy-start.17 = (s32[2]{0:T(128)S(1)}, s32[2]{0:T(128)}, u32[]{:S(2)}) copy-start(s32[2]{0:T(128)} %fusion.43) | copy-start | bytes 28
  84.5 20.9 %copy-start.18 = (pred[4]{0:T(512)(128)(4,1)S(1)}, pred[4]{0:T(512)(128)(4,1)}, u32[]{:S(2)}) copy-start(pred[4]{0:T(512)(128)(4,1)} %get-tuple-element.20) | copy-start | bytes 16
  84.5 46.1 %collective-permute-start.10 = (bf16[576,512]{1,0:T(8,128)(2,1)}, bf16[576,512]{1,0:T(8,128)(2,1)}, u32[]{:S(2)}, u32[]{:S(2)}) collective-permute-start(bf16[576,512]{1,0:T(8,128)(2,1)} %get-tuple-element.11), channel_id=1, source_target_pairs={{0,4},{2,6},{4,0},{6,2},{1,5},{3,7},{5,1},{7,3},{8,12},{10,14},{12... | collective-permute-start | bytes 1769480 | tf_op jit(solution)/shard_map/ppermute | solution.py:53
  86.6 44.0 %collective-permute-start.11 = (bf16[576,512]{1,0:T(8,128)(2,1)}, bf16[576,512]{1,0:T(8,128)(2,1)}, u32[]{:S(2)}, u32[]{:S(2)}) collective-permute-start(bf16[576,512]{1,0:T(8,128)(2,1)} %get-tuple-element.10), channel_id=1, source_target_pairs={{0,6},{2,0},{4,2},{6,4},{1,7},{3,1},{5,3},{7,5},{8,14},{10,8},{12,... | collective-permute-start | bytes 1769480 | tf_op jit(solution)/shard_map/ppermute | solution.py:53
  90.7 39.9 %collective-permute-start.9 = (bf16[576,512]{1,0:T(8,128)(2,1)}, bf16[576,512]{1,0:T(8,128)(2,1)}, u32[]{:S(2)}, u32[]{:S(2)}) collective-permute-start(bf16[576,512]{1,0:T(8,128)(2,1)} %get-tuple-element.9), channel_id=1, source_target_pairs={{0,2},{2,4},{4,6},{6,0},{1,3},{3,5},{5,7},{7,1},{8,10},{10,12},{12... | collective-permute-start | bytes 1769480 | tf_op jit(solution)/shard_map/ppermute | solution.py:53
  96.6 22.5 %all-to-all-start.2 = ((bf16[8,2,3822]{2,1,0:T(2,128)(2,1)}), bf16[8,2,3822]{2,1,0:T(2,128)(2,1)S(1)}, u32[]{:S(2)}, u32[]{:S(2)}) async-start(bf16[8,2,3822]{2,1,0:T(2,128)(2,1)} %reshape.520), calls=%async_computation.2 | async-start | bytes 245760 | tf_op jit(solution)/shard_map/all_to_all | solution.py:111
  119.3 15.0 %collective-permute-start.12 = (bf16[8,7644]{1,0:T(8,128)(2,1)S(1)}, bf16[8,7644]{1,0:T(8,128)(2,1)S(1)}, u32[]{:S(2)}, u32[]{:S(2)}) collective-permute-start(bf16[8,7644]{1,0:T(8,128)(2,1)S(1)} %bitcast.91), channel_id=1, source_target_pairs={{0,0},{1,8},{2,16},{3,24},{4,32},{5,40},{6,48},{7,56},{8,1},{9,9},... | collective-permute-start | bytes 366920 | tf_op jit(solution)/shard_map/ppermute | solution.py:112
  135.3 26.0 %collective-permute-start.13 = (bf16[288,512]{1,0:T(8,128)(2,1)S(1)}, bf16[288,512]{1,0:T(8,128)(2,1)S(1)}, u32[]{:S(2)}, u32[]{:S(2)}) collective-permute-start(bf16[288,512]{1,0:T(8,128)(2,1)S(1)} %constant_dynamic-slice_fusion), channel_id=1, source_target_pairs={{0,1},{1,0},{2,3},{3,2},{4,5},{5,4},{6,7},{7,6},{8,9},{9,8},{10,11... | collective-permute-start | bytes 884744 | tf_op jit(solution)/shard_map/ppermute | solution.py:53
  161.4 2.8 %copy-start.5 = (f32[2,273,112]{2,1,0:T(8,128)S(1)}, f32[2,273,112]{2,1,0:T(8,128)}, u32[]{:S(2)}) copy-start(f32[2,273,112]{2,1,0:T(8,128)} %reshape.454) | copy-start | bytes 733828
  161.4 2.7 %copy-start.14 = (bf16[273]{0:T(512)(128)(2,1)S(1)}, bf16[273]{0:T(512)(128)(2,1)}, u32[]{:S(2)}) copy-start(bf16[273]{0:T(512)(128)(2,1)} %copy-done.13) | copy-start | bytes 1642
  164.2 3.9 %copy-start.9 = (pred[2]{0:T(512)(128)(4,1)S(1)}, pred[2]{0:T(512)(128)(4,1)}, u32[]{:S(2)}) copy-start(pred[2]{0:T(512)(128)(4,1)} %copy-done.8) | copy-start | bytes 10
  166.0 21.0 %copy-start.11 = (pred[2]{0:T(512)(128)(4,1)S(1)}, pred[2]{0:T(512)(128)(4,1)}, u32[]{:S(2)}) copy-start(pred[2]{0:T(512)(128)(4,1)} %get-tuple-element.18) | copy-start | bytes 10
  166.1 20.2 %collective-permute-start.15 = (bf16[512,224]{0,1:T(8,128)(2,1)S(1)}, bf16[512,224]{0,1:T(8,128)(2,1)S(1)}, u32[]{:S(2)}, u32[]{:S(2)}) collective-permute-start(bf16[512,224]{0,1:T(8,128)(2,1)S(1)} %bitcast.77), channel_id=1, source_target_pairs={{0,1},{1,0},{2,3},{3,2},{4,5},{5,4},{6,7},{7,6},{8,9},{9,8},{10,11... | collective-permute-start | bytes 688136 | tf_op jit(solution)/shard_map/ppermute | solution.py:42
  168.9 42.0 %collective-permute-start.1 = (bf16[2,224,224]{2,1,0:T(8,128)(2,1)}, bf16[2,224,224]{2,1,0:T(8,128)(2,1)}, u32[]{:S(2)}, u32[]{:S(2)}) collective-permute-start(bf16[2,224,224]{2,1,0:T(8,128)(2,1)} %broadcast_select_fusion.2), channel_id=1, source_target_pairs={{0,16},{16,32},{32,48},{48,0},{1,17},{17,33},{33,49},{49,1},{2,18}... | collective-permute-start | bytes 602120 | tf_op jit(solution)/shard_map/ppermute | solution.py:42
  172.2 43.1 %collective-permute-start.2 = (bf16[2,224,224]{2,1,0:T(8,128)(2,1)}, bf16[2,224,224]{2,1,0:T(8,128)(2,1)}, u32[]{:S(2)}, u32[]{:S(2)}) collective-permute-start(bf16[2,224,224]{2,1,0:T(8,128)(2,1)} %broadcast_select_fusion.2), channel_id=1, source_target_pairs={{0,32},{16,48},{32,0},{48,16},{1,33},{17,49},{33,1},{49,17},{2,34}... | collective-permute-start | bytes 602120 | tf_op jit(solution)/shard_map/ppermute | solution.py:42
  179.5 35.8 %collective-permute-start.3 = (bf16[2,224,224]{2,1,0:T(8,128)(2,1)}, bf16[2,224,224]{2,1,0:T(8,128)(2,1)}, u32[]{:S(2)}, u32[]{:S(2)}) collective-permute-start(bf16[2,224,224]{2,1,0:T(8,128)(2,1)} %broadcast_select_fusion.2), channel_id=1, source_target_pairs={{0,48},{16,0},{32,16},{48,32},{1,49},{17,1},{33,17},{49,33},{2,50}... | collective-permute-start | bytes 602120 | tf_op jit(solution)/shard_map/ppermute | solution.py:42
  187.9 32.8 %collective-permute-start.16 = (bf16[2,512,224]{1,2,0:T(8,128)(2,1)}, bf16[2,512,224]{1,2,0:T(8,128)(2,1)S(1)}, u32[]{:S(2)}, u32[]{:S(2)}) collective-permute-start(bf16[2,512,224]{1,2,0:T(8,128)(2,1)} %broadcast_select_fusion), channel_id=1, source_target_pairs={{0,2},{2,4},{4,6},{6,0},{1,3},{3,5},{5,7},{7,1},{8,10},{10,12},{12... | collective-permute-start | bytes 1376264 | tf_op jit(solution)/shard_map/ppermute | solution.py:42
  208.9 19.5 %collective-permute-start.17 = (bf16[2,512,224]{1,2,0:T(8,128)(2,1)}, bf16[2,512,224]{1,2,0:T(8,128)(2,1)}, u32[]{:S(2)}, u32[]{:S(2)}) collective-permute-start(bf16[2,512,224]{1,2,0:T(8,128)(2,1)} %broadcast_select_fusion), channel_id=1, source_target_pairs={{0,4},{2,6},{4,0},{6,2},{1,5},{3,7},{5,1},{7,3},{8,12},{10,14},{12... | collective-permute-start | bytes 1376264 | tf_op jit(solution)/shard_map/ppermute | solution.py:42
  210.9 19.3 %collective-permute-start.18 = (bf16[2,512,224]{1,2,0:T(8,128)(2,1)}, bf16[2,512,224]{1,2,0:T(8,128)(2,1)}, u32[]{:S(2)}, u32[]{:S(2)}) collective-permute-start(bf16[2,512,224]{1,2,0:T(8,128)(2,1)} %broadcast_select_fusion), channel_id=1, source_target_pairs={{0,6},{2,0},{4,2},{6,4},{1,7},{3,1},{5,3},{7,5},{8,14},{10,8},{12,... | collective-permute-start | bytes 1376264 | tf_op jit(solution)/shard_map/ppermute | solution.py:42
  220.7 9.5 %copy-start.4 = (bf16[2,512,224]{1,2,0:T(8,128)(2,1)}, bf16[2,512,224]{1,2,0:T(8,128)(2,1)S(1)}, u32[]{:S(2)}) copy-start(bf16[2,512,224]{1,2,0:T(8,128)(2,1)S(1)} %collective-permute-done.16) | copy-start | bytes 1376260
  231.7 2.1 copy-start.19
  233.8 1.8 copy-start.2
  233.8 1.8 copy-start.16

commit v10 on v9

--- a/solution.py
+++ b/solution.py
@@ -112,8 +112,11 @@
     chosen = lax.ppermute(chosen, flat, perm)
     chosen = chosen.reshape(state_shape).astype(jnp.float32)
 
-    weight_all = gather_by_shifts(gather_by_shifts(qkv_weight, "c", 2), "x", n_row // 2)
-    weight_all = weight_all.reshape((n_row,) + qkv_weight.shape)
+    both = jnp.concatenate([qkv_weight, out_weight], axis=1)
+    both = gather_by_shifts(gather_by_shifts(both, "c", 2), "x", n_row // 2)
+    both = both.reshape((n_row,) + both.shape[2:])
+    weight_all = both[:, :, : qkv_weight.shape[1]]
+    out_w = both[:, :, qkv_weight.shape[1] :]
     partial_proj = jnp.einsum(
         "kdj,dt->kjt", weight_all, tokens, preferred_element_type=jnp.float32
     ).astype(jnp.bfloat16)
@@ -143,8 +146,6 @@
     normed = (attended * inverse_rms * gains).astype(jnp.bfloat16).reshape(SLOTS, heads_here * HD)
     hidden = gather_by_shifts(gather_by_shifts(normed, "zh", 2), "y", n_col // 2)
     hidden = hidden.reshape((n_col,) + normed.shape)
-    out_w = gather_by_shifts(gather_by_shifts(out_weight, "c", 2), "x", n_row // 2)
-    out_w = out_w.reshape((n_row,) + out_weight.shape)
     blocks = jnp.einsum("ktd,kde->ket", hidden, out_w, preferred_element_type=jnp.float32)
     mixed_sums = jnp.sum(blocks.astype(jnp.bfloat16).astype(jnp.float32), axis=0)
     return (tokens.astype(jnp.float32) + mixed_sums).astype(jnp.bfloat16)

time: 241 us -> 237 us (0.983)
  the two profiles are of different devices: /device:TPU:1 before, /device:TPU:38 now
where the time goes in v10:
time: 237 us; the launch traced here: 235 us
  starting transfers between devices  111 us (47%)
  waiting for transfers between devices  81.8 us (35%)
  other arithmetic  16.8 us (7%)
  local copies, waits for them, and re-layouts  15.9 us (7%)
  matrix products  7.47 us (3%)
    ppermute x8, waiting for transfers between devices, gather_by_shifts(): lax.ppermute(x, axis, [(i, (i + k) % n) for i in range(n)])  41.7 us
    ppermute x4, starting transfers between devices, reduce_scatter_by_shifts(): lax.ppermute(part, axis, [(i, (i + k) % n) for i in range(n)])  37.1 us
    ppermute x4, waiting for transfers between devices, reduce_scatter_by_shifts(): lax.ppermute(part, axis, [(i, (i + k) % n) for i in range(n)])  23.8 us
    ppermute x8, starting transfers between devices, gather_by_shifts(): lax.ppermute(x, axis, [(i, (i + k) % n) for i in range(n)])  22.4 us
    ppermute x1, starting transfers between devices, shards(): lax.ppermute(jnp.concatenate([other, meta_y.reshape(-1)]), 'zh', [(0, 1),...  14.8 us
    all_to_all x1, starting transfers between devices, shards(): pieces = lax.all_to_all(pieces, 'req', 0, 0, tiled=True)  10.1 us
    all_to_all x1, starting transfers between devices, shards(): chosen = lax.all_to_all(to_send, COL, 0, 0, tiled=True)  9.46 us
    ppermute x1, starting transfers between devices, shards(): gains = lax.ppermute(head_gain, flat, perm).reshape(heads_here, HD)  7.36 us
  transfers between devices with their start and end apart: 18, of which 10 were waited for; matrix products, arithmetic and copies ran while one was open for 9% of the time, Pallas kernels for 0%

profile of v10, /device:TPU:38, one launch (start us, length us, event | category | flops | bytes accessed | tf_op | source)
XLA Modules:
  0.0 235.5 jit_solution(2832584001270509)
XLA Ops:
  0.8 1.0 convert.42
  1.7 1.0 multiply_convert_fusion.3
  3.4 0.9 multiply_convert_fusion
  4.3 1.3 fusion.7
  5.7 0.9 reshape.434
  7.4 1.2 pad_maximum_fusion.4
  8.6 4.5 %all-to-all-start = ((bf16[4,2,22935]{2,1,0:T(2,128)(2,1)}), bf16[4,2,22935]{2,1,0:T(2,128)(2,1)S(1)}, u32[]{:S(2)}, u32[]{:S(2)}) async-start(bf16[4,2,22935]{2,1,0:T(2,128)(2,1)} %pad_maximum_fusion.4), calls=%async_computation | async-start | bytes 737280 | tf_op jit(solution)/shard_map/all_to_all | solution.py:87
  13.2 1.9 collective-permute-start
  15.5 1.2 collective-permute-done
  17.5 2.4 %collective-permute-start.1 = (bf16[2,224,512]{1,2,0:T(8,128)(2,1)S(1)}, bf16[2,224,512]{1,2,0:T(8,128)(2,1)}, u32[]{:S(2)}, u32[]{:S(2)}) collective-permute-start(bf16[2,224,512]{1,2,0:T(8,128)(2,1)S(1)} %broadcast_select_fusion), channel_id=1, source_target_pairs={{0,16},{16,32},{32,48},{48,0},{1,17},{17,33},{33,49},{49,1},{2,18}... | collective-permute-start | bytes 1376264 | tf_op jit(solution)/shard_map/ppermute | solution.py:42
  19.9 4.3 %collective-permute-start.2 = (bf16[2,224,512]{1,2,0:T(8,128)(2,1)S(1)}, bf16[2,224,512]{1,2,0:T(8,128)(2,1)}, u32[]{:S(2)}, u32[]{:S(2)}) collective-permute-start(bf16[2,224,512]{1,2,0:T(8,128)(2,1)S(1)} %broadcast_select_fusion), channel_id=1, source_target_pairs={{0,32},{16,48},{32,0},{48,16},{1,33},{17,49},{33,1},{49,17},{2,34}... | collective-permute-start | bytes 1376264 | tf_op jit(solution)/shard_map/ppermute | solution.py:42
  24.2 1.9 collective-permute-start.3
  27.1 14.8 %collective-permute-start.4 = (bf16[22944]{0:T(1024)(128)(2,1)S(1)}, bf16[22944]{0:T(1024)(128)(2,1)S(1)}, u32[]{:S(2)}, u32[]{:S(2)}) collective-permute-start(bf16[22944]{0:T(1024)(128)(2,1)S(1)} %pad_maximum_fusion.8), channel_id=1, source_target_pairs={{0,1},{1,0},{2,3},{3,2},{4,5},{5,4},{6,7},{7,6},{8,9},{9,8},{10,11... | collective-permute-start | bytes 137672 | tf_op jit(solution)/shard_map/ppermute | solution.py:93
  41.9 0.9 bitcast_select_fusion.2
  43.2 1.1 collective-permute-done.4
  44.5 0.9 broadcast_in_dim.133
  45.4 10.1 %all-to-all-start.1 = ((bf16[8,3,7644]{2,1,0:T(4,128)(2,1)}), bf16[8,3,7644]{2,1,0:T(4,128)(2,1)}, u32[]{:S(2)}, u32[]{:S(2)}) async-start(bf16[8,3,7644]{2,1,0:T(4,128)(2,1)} %broadcast_in_dim.133), calls=%async_computation.1 | async-start | bytes 983040 | tf_op jit(solution)/shard_map/all_to_all | solution.py:108
  55.9 2.1 pad_maximum_fusion
  58.0 2.0 gather_fusion.1
  60.0 1.9 bitcast_select_fusion
  62.7 1.4 copy-done.1
  64.1 1.2 constant_dynamic-slice_fusion.3
  65.3 4.0 %collective-permute-start.5 = (bf16[576,512]{1,0:T(8,128)(2,1)}, bf16[576,512]{1,0:T(8,128)(2,1)S(1)}, u32[]{:S(2)}, u32[]{:S(2)}) collective-permute-start(bf16[576,512]{1,0:T(8,128)(2,1)} %get-tuple-element.9), channel_id=1, source_target_pairs={{0,2},{2,4},{4,6},{6,0},{1,3},{3,5},{5,7},{7,1},{8,10},{10,12},{12... | collective-permute-start | bytes 1769480 | tf_op jit(solution)/shard_map/ppermute | solution.py:53
  69.4 4.6 %collective-permute-start.6 = (bf16[576,512]{1,0:T(8,128)(2,1)}, bf16[576,512]{1,0:T(8,128)(2,1)}, u32[]{:S(2)}, u32[]{:S(2)}) collective-permute-start(bf16[576,512]{1,0:T(8,128)(2,1)} %get-tuple-element.11), channel_id=1, source_target_pairs={{0,4},{2,6},{4,0},{6,2},{1,5},{3,7},{5,1},{7,3},{8,12},{10,14},{12... | collective-permute-start | bytes 1769480 | tf_op jit(solution)/shard_map/ppermute | solution.py:53
  74.0 3.4 %collective-permute-start.7 = (bf16[576,512]{1,0:T(8,128)(2,1)S(1)}, bf16[576,512]{1,0:T(8,128)(2,1)}, u32[]{:S(2)}, u32[]{:S(2)}) collective-permute-start(bf16[576,512]{1,0:T(8,128)(2,1)S(1)} %get-tuple-element.10), channel_id=1, source_target_pairs={{0,6},{2,0},{4,2},{6,4},{1,7},{3,1},{5,3},{7,5},{8,14},{10,8},{12,... | collective-permute-start | bytes 1769480 | tf_op jit(solution)/shard_map/ppermute | solution.py:53
  77.4 3.7 %all-to-all-done.1 = bf16[8,3,7644]{2,1,0:T(4,128)(2,1)} async-done(((bf16[8,3,7644]{2,1,0:T(4,128)(2,1)}), bf16[8,3,7644]{2,1,0:T(4,128)(2,1)}, u32[]{:S(2)}, u32[]{:S(2)}) %all-to-all-start.1) | async-done | bytes 366944 | tf_op jit(solution)/shard_map/all_to_all | solution.py:108
  81.1 1.3 reshape.437
  85.1 9.5 %all-to-all-start.2 = ((bf16[8,2,3822]{2,1,0:T(2,128)(2,1)}), bf16[8,2,3822]{2,1,0:T(2,128)(2,1)S(1)}, u32[]{:S(2)}, u32[]{:S(2)}) async-start(bf16[8,2,3822]{2,1,0:T(2,128)(2,1)} %reshape.494), calls=%async_computation.2 | async-start | bytes 245760 | tf_op jit(solution)/shard_map/all_to_all | solution.py:111
  94.6 7.4 %collective-permute-start.10 = (f32[224]{0:T(256)S(1)}, f32[224]{0:T(256)S(1)}, u32[]{:S(2)}, u32[]{:S(2)}) collective-permute-start(f32[224]{0:T(256)S(1)} %copy-done.6), channel_id=1, source_target_pairs={{0,0},{1,8},{2,16},{3,24},{4,32},{5,40},{6,48},{7,56},{8,1},{9,9},... | collective-permute-start | bytes 2696 | tf_op jit(solution)/shard_map/ppermute | solution.py:145
  102.0 1.5 collective-permute-done.10
  104.1 6.0 %all-to-all-done.2 = bf16[8,2,3822]{2,1,0:T(2,128)(2,1)S(1)} async-done(((bf16[8,2,3822]{2,1,0:T(2,128)(2,1)}), bf16[8,2,3822]{2,1,0:T(2,128)(2,1)S(1)}, u32[]{:S(2)}, u32[]{:S(2)}) %all-to-all-start.2) | async-done | bytes 122336 | tf_op jit(solution)/shard_map/all_to_all | solution.py:111
  110.3 5.7 %collective-permute-start.8 = (bf16[8,7644]{1,0:T(8,128)(2,1)S(1)}, bf16[8,7644]{1,0:T(8,128)(2,1)S(1)}, u32[]{:S(2)}, u32[]{:S(2)}) collective-permute-start(bf16[8,7644]{1,0:T(8,128)(2,1)S(1)} %bitcast.81), channel_id=1, source_target_pairs={{0,0},{1,8},{2,16},{3,24},{4,32},{5,40},{6,48},{7,56},{8,1},{9,9},... | collective-permute-start | bytes 366920 | tf_op jit(solution)/shard_map/ppermute | solution.py:112
  116.1 1.7 add_convert_fusion
  117.8 3.9 %collective-permute-done.8 = bf16[8,7644]{1,0:T(8,128)(2,1)S(1)} collective-permute-done((bf16[8,7644]{1,0:T(8,128)(2,1)S(1)}, bf16[8,7644]{1,0:T(8,128)(2,1)S(1)}, u32[]{:S(2)}, u32[]{:S(2)}) %collective-permute-start.8) | collective-permute-done | bytes 122336 | tf_op jit(solution)/shard_map/ppermute | solution.py:112
  122.0 25.0 %collective-permute-start.9 = (bf16[288,512]{1,0:T(8,128)(2,1)S(1)}, bf16[288,512]{1,0:T(8,128)(2,1)S(1)}, u32[]{:S(2)}, u32[]{:S(2)}) collective-permute-start(bf16[288,512]{1,0:T(8,128)(2,1)S(1)} %constant_dynamic-slice_fusion), channel_id=1, source_target_pairs={{0,1},{1,0},{2,3},{3,2},{4,5},{5,4},{6,7},{7,6},{8,9},{9,8},{10,11... | collective-permute-start | bytes 884744 | tf_op jit(solution)/shard_map/ppermute | solution.py:53
  147.8 23.8 %collective-permute-done.9 = bf16[288,512]{1,0:T(8,128)(2,1)S(1)} collective-permute-done((bf16[288,512]{1,0:T(8,128)(2,1)S(1)}, bf16[288,512]{1,0:T(8,128)(2,1)S(1)}, u32[]{:S(2)}, u32[]{:S(2)}) %collective-permute-start.9) | collective-permute-done | bytes 294944 | tf_op jit(solution)/shard_map/ppermute | solution.py:53
  171.8 1.7 fusion.6
  173.6 1.8 multiply_reduce_fusion
  175.5 2.9 %collective-permute-start.11 = (bf16[512,224]{0,1:T(8,128)(2,1)S(1)}, bf16[512,224]{0,1:T(8,128)(2,1)S(1)}, u32[]{:S(2)}, u32[]{:S(2)}) collective-permute-start(bf16[512,224]{0,1:T(8,128)(2,1)S(1)} %bitcast.68), channel_id=1, source_target_pairs={{0,1},{1,0},{2,3},{3,2},{4,5},{5,4},{6,7},{7,6},{8,9},{9,8},{10,11... | collective-permute-start | bytes 688136 | tf_op jit(solution)/shard_map/ppermute | solution.py:42
  178.6 21.7 %collective-permute-done.11 = bf16[512,224]{0,1:T(8,128)(2,1)S(1)} collective-permute-done((bf16[512,224]{0,1:T(8,128)(2,1)S(1)}, bf16[512,224]{0,1:T(8,128)(2,1)S(1)}, u32[]{:S(2)}, u32[]{:S(2)}) %collective-permute-start.11) | collective-permute-done | bytes 229408 | tf_op jit(solution)/shard_map/ppermute | solution.py:42
  201.1 1.9 collective-permute-start.12
  203.0 1.9 collective-permute-start.13
  204.9 5.1 %collective-permute-start.14 = (bf16[2,512,224]{1,2,0:T(8,128)(2,1)S(1)}, bf16[2,512,224]{1,2,0:T(8,128)(2,1)S(1)}, u32[]{:S(2)}, u32[]{:S(2)}) collective-permute-start(bf16[2,512,224]{1,2,0:T(8,128)(2,1)S(1)} %broadcast_select_fusion.1), channel_id=1, source_target_pairs={{0,6},{2,0},{4,2},{6,4},{1,7},{3,1},{5,3},{7,5},{8,14},{10,8},{12,... | collective-permute-start | bytes 1376264 | tf_op jit(solution)/shard_map/ppermute | solution.py:42
  210.2 16.2 %collective-permute-done.12 = bf16[2,512,224]{1,2,0:T(8,128)(2,1)S(1)} collective-permute-done((bf16[2,512,224]{1,2,0:T(8,128)(2,1)S(1)}, bf16[2,512,224]{1,2,0:T(8,128)(2,1)S(1)}, u32[]{:S(2)}, u32[]{:S(2)}) %collective-permute-start.12) | collective-permute-done | bytes 458784 | tf_op jit(solution)/shard_map/ppermute | solution.py:42
  226.5 2.5 %collective-permute-done.14 = bf16[2,512,224]{1,2,0:T(8,128)(2,1)S(1)} collective-permute-done((bf16[2,512,224]{1,2,0:T(8,128)(2,1)S(1)}, bf16[2,512,224]{1,2,0:T(8,128)(2,1)S(1)}, u32[]{:S(2)}, u32[]{:S(2)}) %collective-permute-start.14) | collective-permute-done | bytes 458784 | tf_op jit(solution)/shard_map/ppermute | solution.py:42
  229.2 1.9 gather_fusion.4
  231.1 1.7 bitcast_select_fusion.1
  232.9 1.8 convert_reduce_fusion
  (87 shorter events, 11.5 us)
Async XLA Ops:
  0.0 4.3 %copy-start = (bf16[3,224,1024]{2,1,0:T(8,128)(2,1)S(1)}, bf16[3,224,1024]{2,1,0:T(8,128)(2,1)}, u32[]{:S(2)}) copy-start(bf16[3,224,1024]{2,1,0:T(8,128)(2,1)} %param.13) | copy-start | bytes 4128772
  5.6 7.4 %copy-start.5 = (bf16[224,224]{1,0:T(8,128)(2,1)S(1)}, bf16[224,224]{1,0:T(8,128)(2,1)}, u32[]{:S(2)}) copy-start(bf16[224,224]{1,0:T(8,128)(2,1)} %param.10) | copy-start | bytes 301060
  5.7 7.5 %copy-start.4 = (bf16[224,288]{0,1:T(8,128)(2,1)S(1)}, bf16[224,288]{0,1:T(8,128)(2,1)}, u32[]{:S(2)}) copy-start(bf16[224,288]{0,1:T(8,128)(2,1)} %param.9) | copy-start | bytes 387076
  8.6 17.5 %all-to-all-start = ((bf16[4,2,22935]{2,1,0:T(2,128)(2,1)}), bf16[4,2,22935]{2,1,0:T(2,128)(2,1)S(1)}, u32[]{:S(2)}, u32[]{:S(2)}) async-start(bf16[4,2,22935]{2,1,0:T(2,128)(2,1)} %pad_maximum_fusion.4), calls=%async_computation | async-start | bytes 737280 | tf_op jit(solution)/shard_map/all_to_all | solution.py:87
  13.2 3.4 %collective-permute-start = (bf16[224,512]{0,1:T(8,128)(2,1)S(1)}, bf16[224,512]{0,1:T(8,128)(2,1)S(1)}, u32[]{:S(2)}, u32[]{:S(2)}) collective-permute-start(bf16[224,512]{0,1:T(8,128)(2,1)S(1)} %get-tuple-element.15), channel_id=1, source_target_pairs={{0,8},{8,0},{1,9},{9,1},{2,10},{10,2},{3,11},{11,3},{4,12},{12,4},... | collective-permute-start | bytes 688136 | tf_op jit(solution)/shard_map/ppermute | solution.py:42
  17.5 38.4 %collective-permute-start.1 = (bf16[2,224,512]{1,2,0:T(8,128)(2,1)S(1)}, bf16[2,224,512]{1,2,0:T(8,128)(2,1)}, u32[]{:S(2)}, u32[]{:S(2)}) collective-permute-start(bf16[2,224,512]{1,2,0:T(8,128)(2,1)S(1)} %broadcast_select_fusion), channel_id=1, source_target_pairs={{0,16},{16,32},{32,48},{48,0},{1,17},{17,33},{33,49},{49,1},{2,18}... | collective-permute-start | bytes 1376264 | tf_op jit(solution)/shard_map/ppermute | solution.py:42
  19.9 36.1 %collective-permute-start.2 = (bf16[2,224,512]{1,2,0:T(8,128)(2,1)S(1)}, bf16[2,224,512]{1,2,0:T(8,128)(2,1)}, u32[]{:S(2)}, u32[]{:S(2)}) collective-permute-start(bf16[2,224,512]{1,2,0:T(8,128)(2,1)S(1)} %broadcast_select_fusion), channel_id=1, source_target_pairs={{0,32},{16,48},{32,0},{48,16},{1,33},{17,49},{33,1},{49,17},{2,34}... | collective-permute-start | bytes 1376264 | tf_op jit(solution)/shard_map/ppermute | solution.py:42
  24.2 31.7 %collective-permute-start.3 = (bf16[2,224,512]{1,2,0:T(8,128)(2,1)S(1)}, bf16[2,224,512]{1,2,0:T(8,128)(2,1)}, u32[]{:S(2)}, u32[]{:S(2)}) collective-permute-start(bf16[2,224,512]{1,2,0:T(8,128)(2,1)S(1)} %broadcast_select_fusion), channel_id=1, source_target_pairs={{0,48},{16,0},{32,16},{48,32},{1,49},{17,1},{33,17},{49,33},{2,50}... | collective-permute-start | bytes 1376264 | tf_op jit(solution)/shard_map/ppermute | solution.py:42
  27.1 17.3 %collective-permute-start.4 = (bf16[22944]{0:T(1024)(128)(2,1)S(1)}, bf16[22944]{0:T(1024)(128)(2,1)S(1)}, u32[]{:S(2)}, u32[]{:S(2)}) collective-permute-start(bf16[22944]{0:T(1024)(128)(2,1)S(1)} %pad_maximum_fusion.8), channel_id=1, source_target_pairs={{0,1},{1,0},{2,3},{3,2},{4,5},{5,4},{6,7},{7,6},{8,9},{9,8},{10,11... | collective-permute-start | bytes 137672 | tf_op jit(solution)/shard_map/ppermute | solution.py:93
  45.4 35.7 %all-to-all-start.1 = ((bf16[8,3,7644]{2,1,0:T(4,128)(2,1)}), bf16[8,3,7644]{2,1,0:T(4,128)(2,1)}, u32[]{:S(2)}, u32[]{:S(2)}) async-start(bf16[8,3,7644]{2,1,0:T(4,128)(2,1)} %broadcast_in_dim.133), calls=%async_computation.1 | async-start | bytes 983040 | tf_op jit(solution)/shard_map/all_to_all | solution.py:108
  60.0 1.9 copy-start.3
  61.9 3.4 %copy-start.2 = (bf16[8,224,512]{1,2,0:T(8,128)(2,1)}, bf16[8,224,512]{1,2,0:T(8,128)(2,1)S(1)}, u32[]{:S(2)}) copy-start(bf16[8,224,512]{1,2,0:T(8,128)(2,1)S(1)} %bitcast_select_fusion) | copy-start | bytes 5505028
  62.7 1.4 copy-start.1
  65.3 29.3 %copy-start.6 = (f32[224]{0:T(256)S(1)}, f32[224]{0:T(256)}, u32[]{:S(2)}) copy-start(f32[224]{0:T(256)} %param.11) | copy-start | bytes 2692
  65.3 50.7 %collective-permute-start.5 = (bf16[576,512]{1,0:T(8,128)(2,1)}, bf16[576,512]{1,0:T(8,128)(2,1)S(1)}, u32[]{:S(2)}, u32[]{:S(2)}) collective-permute-start(bf16[576,512]{1,0:T(8,128)(2,1)} %get-tuple-element.9), channel_id=1, source_target_pairs={{0,2},{2,4},{4,6},{6,0},{1,3},{3,5},{5,7},{7,1},{8,10},{10,12},{12... | collective-permute-start | bytes 1769480 | tf_op jit(solution)/shard_map/ppermute | solution.py:53
  69.4 46.7 %collective-permute-start.6 = (bf16[576,512]{1,0:T(8,128)(2,1)}, bf16[576,512]{1,0:T(8,128)(2,1)}, u32[]{:S(2)}, u32[]{:S(2)}) collective-permute-start(bf16[576,512]{1,0:T(8,128)(2,1)} %get-tuple-element.11), channel_id=1, source_target_pairs={{0,4},{2,6},{4,0},{6,2},{1,5},{3,7},{5,1},{7,3},{8,12},{10,14},{12... | collective-permute-start | bytes 1769480 | tf_op jit(solution)/shard_map/ppermute | solution.py:53
  74.0 42.1 %collective-permute-start.7 = (bf16[576,512]{1,0:T(8,128)(2,1)S(1)}, bf16[576,512]{1,0:T(8,128)(2,1)}, u32[]{:S(2)}, u32[]{:S(2)}) collective-permute-start(bf16[576,512]{1,0:T(8,128)(2,1)S(1)} %get-tuple-element.10), channel_id=1, source_target_pairs={{0,6},{2,0},{4,2},{6,4},{1,7},{3,1},{5,3},{7,5},{8,14},{10,8},{12,... | collective-permute-start | bytes 1769480 | tf_op jit(solution)/shard_map/ppermute | solution.py:53
  85.1 25.0 %all-to-all-start.2 = ((bf16[8,2,3822]{2,1,0:T(2,128)(2,1)}), bf16[8,2,3822]{2,1,0:T(2,128)(2,1)S(1)}, u32[]{:S(2)}, u32[]{:S(2)}) async-start(bf16[8,2,3822]{2,1,0:T(2,128)(2,1)} %reshape.494), calls=%async_computation.2 | async-start | bytes 245760 | tf_op jit(solution)/shard_map/all_to_all | solution.py:111
  94.6 8.9 %collective-permute-start.10 = (f32[224]{0:T(256)S(1)}, f32[224]{0:T(256)S(1)}, u32[]{:S(2)}, u32[]{:S(2)}) collective-permute-start(f32[224]{0:T(256)S(1)} %copy-done.6), channel_id=1, source_target_pairs={{0,0},{1,8},{2,16},{3,24},{4,32},{5,40},{6,48},{7,56},{8,1},{9,9},... | collective-permute-start | bytes 2696 | tf_op jit(solution)/shard_map/ppermute | solution.py:145
  110.3 11.4 %collective-permute-start.8 = (bf16[8,7644]{1,0:T(8,128)(2,1)S(1)}, bf16[8,7644]{1,0:T(8,128)(2,1)S(1)}, u32[]{:S(2)}, u32[]{:S(2)}) collective-permute-start(bf16[8,7644]{1,0:T(8,128)(2,1)S(1)} %bitcast.81), channel_id=1, source_target_pairs={{0,0},{1,8},{2,16},{3,24},{4,32},{5,40},{6,48},{7,56},{8,1},{9,9},... | collective-permute-start | bytes 366920 | tf_op jit(solution)/shard_map/ppermute | solution.py:112
  122.0 49.6 %collective-permute-start.9 = (bf16[288,512]{1,0:T(8,128)(2,1)S(1)}, bf16[288,512]{1,0:T(8,128)(2,1)S(1)}, u32[]{:S(2)}, u32[]{:S(2)}) collective-permute-start(bf16[288,512]{1,0:T(8,128)(2,1)S(1)} %constant_dynamic-slice_fusion), channel_id=1, source_target_pairs={{0,1},{1,0},{2,3},{3,2},{4,5},{5,4},{6,7},{7,6},{8,9},{9,8},{10,11... | collective-permute-start | bytes 884744 | tf_op jit(solution)/shard_map/ppermute | solution.py:53
  175.5 24.8 %collective-permute-start.11 = (bf16[512,224]{0,1:T(8,128)(2,1)S(1)}, bf16[512,224]{0,1:T(8,128)(2,1)S(1)}, u32[]{:S(2)}, u32[]{:S(2)}) collective-permute-start(bf16[512,224]{0,1:T(8,128)(2,1)S(1)} %bitcast.68), channel_id=1, source_target_pairs={{0,1},{1,0},{2,3},{3,2},{4,5},{5,4},{6,7},{7,6},{8,9},{9,8},{10,11... | collective-permute-start | bytes 688136 | tf_op jit(solution)/shard_map/ppermute | solution.py:42
  201.1 25.4 %collective-permute-start.12 = (bf16[2,512,224]{1,2,0:T(8,128)(2,1)S(1)}, bf16[2,512,224]{1,2,0:T(8,128)(2,1)S(1)}, u32[]{:S(2)}, u32[]{:S(2)}) collective-permute-start(bf16[2,512,224]{1,2,0:T(8,128)(2,1)S(1)} %broadcast_select_fusion.1), channel_id=1, source_target_pairs={{0,2},{2,4},{4,6},{6,0},{1,3},{3,5},{5,7},{7,1},{8,10},{10,12},{12... | collective-permute-start | bytes 1376264 | tf_op jit(solution)/shard_map/ppermute | solution.py:42
  203.0 23.5 %collective-permute-start.13 = (bf16[2,512,224]{1,2,0:T(8,128)(2,1)S(1)}, bf16[2,512,224]{1,2,0:T(8,128)(2,1)S(1)}, u32[]{:S(2)}, u32[]{:S(2)}) collective-permute-start(bf16[2,512,224]{1,2,0:T(8,128)(2,1)S(1)} %broadcast_select_fusion.1), channel_id=1, source_target_pairs={{0,4},{2,6},{4,0},{6,2},{1,5},{3,7},{5,1},{7,3},{8,12},{10,14},{12... | collective-permute-start | bytes 1376264 | tf_op jit(solution)/shard_map/ppermute | solution.py:42
  204.9 24.1 %collective-permute-start.14 = (bf16[2,512,224]{1,2,0:T(8,128)(2,1)S(1)}, bf16[2,512,224]{1,2,0:T(8,128)(2,1)S(1)}, u32[]{:S(2)}, u32[]{:S(2)}) collective-permute-start(bf16[2,512,224]{1,2,0:T(8,128)(2,1)S(1)} %broadcast_select_fusion.1), channel_id=1, source_target_pairs={{0,6},{2,0},{4,2},{6,4},{1,7},{3,1},{5,3},{7,5},{8,14},{10,8},{12,... | collective-permute-start | bytes 1376264 | tf_op jit(solution)/shard_map/ppermute | solution.py:42

commit v11 on v10

--- a/solution.py
+++ b/solution.py
@@ -144,7 +144,13 @@
     inverse_rms = lax.rsqrt(jnp.mean(attended * attended, axis=-1, keepdims=True) + epsilon)
     gains = lax.ppermute(head_gain, flat, perm).reshape(heads_here, HD)
     normed = (attended * inverse_rms * gains).astype(jnp.bfloat16).reshape(SLOTS, heads_here * HD)
-    hidden = gather_by_shifts(gather_by_shifts(normed, "zh", 2), "y", n_col // 2)
+    own_y = gather_by_shifts(normed, "y", n_col // 2)
+    partner = lax.ppermute(normed, "zh", [(0, 1), (1, 0)])
+    partner_y = gather_by_shifts(partner, "y", n_col // 2)
+    zh_first = lax.axis_index("zh") == 0
+    hidden = jnp.where(
+        zh_first, jnp.stack([own_y, partner_y], axis=1), jnp.stack([partner_y, own_y], axis=1)
+    )
     hidden = hidden.reshape((n_col,) + normed.shape)
     blocks = jnp.einsum("ktd,kde->ket", hidden, out_w, preferred_element_type=jnp.float32)
     mixed_sums = jnp.sum(blocks.astype(jnp.bfloat16).astype(jnp.float32), axis=0)

time: 237 us -> 245 us (1.034)
  the two profiles are of different devices: /device:TPU:38 before, /device:TPU:47 now
where the time goes in v11:
time: 245 us; the launch traced here: 244 us
  starting transfers between devices  117 us (48%)
  waiting for transfers between devices  62 us (25%)
  local copies, waits for them, and re-layouts  28.6 us (12%)
  other arithmetic  26.6 us (11%)
  matrix products  7.59 us (3%)
    ppermute x4, waiting for transfers between devices, reduce_scatter_by_shifts(): lax.ppermute(part, axis, [(i, (i + k) % n) for i in range(n)])  30 us
    ppermute x10, starting transfers between devices, gather_by_shifts(): lax.ppermute(x, axis, [(i, (i + k) % n) for i in range(n)])  28.8 us
    ppermute x1, starting transfers between devices, shards(): gains = lax.ppermute(head_gain, flat, perm).reshape(heads_here, HD)  18.4 us
    ppermute x1, starting transfers between devices, shards(): chosen = lax.ppermute(chosen, flat, perm)  17.2 us
    ppermute x1, waiting for transfers between devices, shards(): partner = lax.ppermute(normed, 'zh', [(0, 1), (1, 0)])  15 us
    ppermute x1, starting transfers between devices, shards(): lax.ppermute(jnp.concatenate([other, meta_y.reshape(-1)]), 'zh', [(0, 1),...  14.5 us
    ppermute x4, starting transfers between devices, reduce_scatter_by_shifts(): lax.ppermute(part, axis, [(i, (i + k) % n) for i in range(n)])  11.8 us
    all_to_all x1, starting transfers between devices, shards(): pieces = lax.all_to_all(pieces, 'req', 0, 0, tiled=True)  11.1 us
  transfers between devices with their start and end apart: 21, of which 9 were waited for; matrix products, arithmetic and copies ran while one was open for 14% of the time, Pallas kernels for 0%

profile of v11, /device:TPU:47, one launch (start us, length us, event | category | flops | bytes accessed | tf_op | source)
XLA Modules:
  0.0 243.5 jit_solution(8489940692860059865)
XLA Ops:
  4.3 1.3 fusion.7
  7.4 1.1 pad_maximum_fusion.4
  8.6 4.3 %all-to-all-start = ((bf16[4,2,22935]{2,1,0:T(2,128)(2,1)}), bf16[4,2,22935]{2,1,0:T(2,128)(2,1)S(1)}, u32[]{:S(2)}, u32[]{:S(2)}) async-start(bf16[4,2,22935]{2,1,0:T(2,128)(2,1)} %pad_maximum_fusion.4), calls=%async_computation | async-start | bytes 737280 | tf_op jit(solution)/shard_map/all_to_all | solution.py:87
  13.1 3.1 %collective-permute-start = (bf16[224,512]{0,1:T(8,128)(2,1)S(1)}, bf16[224,512]{0,1:T(8,128)(2,1)S(1)}, u32[]{:S(2)}, u32[]{:S(2)}) collective-permute-start(bf16[224,512]{0,1:T(8,128)(2,1)S(1)} %get-tuple-element.16), channel_id=1, source_target_pairs={{0,8},{8,0},{1,9},{9,1},{2,10},{10,2},{3,11},{11,3},{4,12},{12,4},... | collective-permute-start | bytes 688136 | tf_op jit(solution)/shard_map/ppermute | solution.py:42
  18.2 2.1 collective-permute-start.1
  20.3 4.0 %collective-permute-start.2 = (bf16[2,224,512]{1,2,0:T(8,128)(2,1)S(1)}, bf16[2,224,512]{1,2,0:T(8,128)(2,1)}, u32[]{:S(2)}, u32[]{:S(2)}) collective-permute-start(bf16[2,224,512]{1,2,0:T(8,128)(2,1)S(1)} %broadcast_select_fusion), channel_id=1, source_target_pairs={{0,32},{16,48},{32,0},{48,16},{1,33},{17,49},{33,1},{49,17},{2,34}... | collective-permute-start | bytes 1376264 | tf_op jit(solution)/shard_map/ppermute | solution.py:42
  24.4 1.9 collective-permute-start.3
  27.2 14.5 %collective-permute-start.4 = (bf16[22944]{0:T(1024)(128)(2,1)S(1)}, bf16[22944]{0:T(1024)(128)(2,1)S(1)}, u32[]{:S(2)}, u32[]{:S(2)}) collective-permute-start(bf16[22944]{0:T(1024)(128)(2,1)S(1)} %pad_maximum_fusion.8), channel_id=1, source_target_pairs={{0,1},{1,0},{2,3},{3,2},{4,5},{5,4},{6,7},{7,6},{8,9},{9,8},{10,11... | collective-permute-start | bytes 137672 | tf_op jit(solution)/shard_map/ppermute | solution.py:93
  44.3 11.1 %all-to-all-start.1 = ((bf16[8,3,7644]{2,1,0:T(4,128)(2,1)}), bf16[8,3,7644]{2,1,0:T(4,128)(2,1)}, u32[]{:S(2)}, u32[]{:S(2)}) async-start(bf16[8,3,7644]{2,1,0:T(4,128)(2,1)} %broadcast_in_dim.110), calls=%async_computation.1 | async-start | bytes 983040 | tf_op jit(solution)/shard_map/all_to_all | solution.py:108
  55.9 2.1 pad_maximum_fusion
  57.9 2.0 gather_fusion.1
  60.0 1.9 bitcast_select_fusion
  62.6 1.4 copy-done.1
  64.1 1.3 constant_dynamic-slice_fusion.3
  65.3 3.2 %collective-permute-start.5 = (bf16[576,512]{1,0:T(8,128)(2,1)}, bf16[576,512]{1,0:T(8,128)(2,1)}, u32[]{:S(2)}, u32[]{:S(2)}) collective-permute-start(bf16[576,512]{1,0:T(8,128)(2,1)} %get-tuple-element.10), channel_id=1, source_target_pairs={{0,2},{2,4},{4,6},{6,0},{1,3},{3,5},{5,7},{7,1},{8,10},{10,12},{12... | collective-permute-start | bytes 1769480 | tf_op jit(solution)/shard_map/ppermute | solution.py:53
  68.5 2.5 %collective-permute-start.6 = (bf16[576,512]{1,0:T(8,128)(2,1)}, bf16[576,512]{1,0:T(8,128)(2,1)}, u32[]{:S(2)}, u32[]{:S(2)}) collective-permute-start(bf16[576,512]{1,0:T(8,128)(2,1)} %get-tuple-element.12), channel_id=1, source_target_pairs={{0,4},{2,6},{4,0},{6,2},{1,5},{3,7},{5,1},{7,3},{8,12},{10,14},{12... | collective-permute-start | bytes 1769480 | tf_op jit(solution)/shard_map/ppermute | solution.py:53
  71.1 4.0 %collective-permute-start.7 = (bf16[576,512]{1,0:T(8,128)(2,1)}, bf16[576,512]{1,0:T(8,128)(2,1)}, u32[]{:S(2)}, u32[]{:S(2)}) collective-permute-start(bf16[576,512]{1,0:T(8,128)(2,1)} %get-tuple-element.11), channel_id=1, source_target_pairs={{0,6},{2,0},{4,2},{6,4},{1,7},{3,1},{5,3},{7,5},{8,14},{10,8},{12,... | collective-permute-start | bytes 1769480 | tf_op jit(solution)/shard_map/ppermute | solution.py:53
  75.0 5.1 %all-to-all-done.1 = bf16[8,3,7644]{2,1,0:T(4,128)(2,1)} async-done(((bf16[8,3,7644]{2,1,0:T(4,128)(2,1)}), bf16[8,3,7644]{2,1,0:T(4,128)(2,1)}, u32[]{:S(2)}, u32[]{:S(2)}) %all-to-all-start.1) | async-done | bytes 366944 | tf_op jit(solution)/shard_map/all_to_all | solution.py:108
  80.1 2.1 reshape.329
  82.2 2.4 gather_fusion.2
  84.7 1.6 bitcast_select_fusion.2
  86.9 2.3 reduce.11
  89.1 1.7 reshape.392
  90.8 8.6 %all-to-all-start.2 = ((bf16[8,2,3822]{2,1,0:T(2,128)(2,1)}), bf16[8,2,3822]{2,1,0:T(2,128)(2,1)}, u32[]{:S(2)}, u32[]{:S(2)}) async-start(bf16[8,2,3822]{2,1,0:T(2,128)(2,1)} %reshape.392), calls=%async_computation.2 | async-start | bytes 245760 | tf_op jit(solution)/shard_map/all_to_all | solution.py:111
  99.4 18.4 %collective-permute-start.10 = (f32[224]{0:T(256)S(1)}, f32[224]{0:T(256)S(1)}, u32[]{:S(2)}, u32[]{:S(2)}) collective-permute-start(f32[224]{0:T(256)S(1)} %copy-done.7), channel_id=1, source_target_pairs={{0,0},{1,8},{2,16},{3,24},{4,32},{5,40},{6,48},{7,56},{8,1},{9,9},... | collective-permute-start | bytes 2696 | tf_op jit(solution)/shard_map/ppermute | solution.py:145
  117.8 1.2 collective-permute-done.10
  119.7 1.8 reshape.393
  122.5 17.2 %collective-permute-start.8 = (bf16[8,7644]{1,0:T(8,128)(2,1)S(1)}, bf16[8,7644]{1,0:T(8,128)(2,1)}, u32[]{:S(2)}, u32[]{:S(2)}) collective-permute-start(bf16[8,7644]{1,0:T(8,128)(2,1)S(1)} %bitcast.84), channel_id=1, source_target_pairs={{0,0},{1,8},{2,16},{3,24},{4,32},{5,40},{6,48},{7,56},{8,1},{9,9},... | collective-permute-start | bytes 366920 | tf_op jit(solution)/shard_map/ppermute | solution.py:112
  139.7 2.7 %add_convert_fusion = bf16[576,512]{1,0:T(8,128)(2,1)} fusion(bf16[576,512]{1,0:T(8,128)(2,1)} %collective-permute-done.7, bf16[576,512]{1,0:T(8,128)(2,1)} %collective-permute-done.6, bf16[576,512]{1,0:T(8,128)(2,1)} %collective-permute-done.5, bf16[2304,512]{1,0:T(8,128)(2,1)} %bitcast.65, s32[]{:T(128)S(6)} %select_n.220), kind=kLoop, calls=%fused_computation.24 | loop fusion | flops 2359296 | bytes 2949124 | tf_op jit(solution)/shard_map/convert_element_type | solution.py:125
  142.4 2.8 %collective-permute-done.8 = bf16[8,7644]{1,0:T(8,128)(2,1)} collective-permute-done((bf16[8,7644]{1,0:T(8,128)(2,1)S(1)}, bf16[8,7644]{1,0:T(8,128)(2,1)}, u32[]{:S(2)}, u32[]{:S(2)}) %collective-permute-start.8) | collective-permute-done | bytes 122336 | tf_op jit(solution)/shard_map/ppermute | solution.py:112
  145.2 1.9 reshape.336
  148.0 2.1 collective-permute-start.9
  151.5 30.0 %collective-permute-done.9 = bf16[288,512]{1,0:T(8,128)(2,1)S(1)} collective-permute-done((bf16[288,512]{1,0:T(8,128)(2,1)S(1)}, bf16[288,512]{1,0:T(8,128)(2,1)S(1)}, u32[]{:S(2)}, u32[]{:S(2)}) %collective-permute-start.9) | collective-permute-done | bytes 294944 | tf_op jit(solution)/shard_map/ppermute | solution.py:53
  184.2 2.8 %fusion.6 = f32[2,112,512]{2,1,0:T(8,128)} fusion(pred[512,512]{1,0:T(8,128)(4,1)} %fusion.17, bf16[512,2,144]{0,2,1:T(8,128)(2,1)} %bitcast.79), kind=kOutput, calls=%fused_computation.18 | convolution fusion | flops 137887744 | bytes 1015808 | tf_op jit(solution)/shard_map/hts,shv->thv/dot_general | solution.py:141
  187.1 2.0 multiply_reduce_fusion
  189.2 1.9 collective-permute-start.14
  191.2 1.9 collective-permute-start.11
  193.1 6.5 %collective-permute-start.12 = (bf16[512,224]{0,1:T(8,128)(2,1)S(1)}, bf16[512,224]{0,1:T(8,128)(2,1)S(1)}, u32[]{:S(2)}, u32[]{:S(2)}) collective-permute-start(bf16[512,224]{0,1:T(8,128)(2,1)S(1)} %bitcast.71), channel_id=1, source_target_pairs={{0,4},{2,6},{4,0},{6,2},{1,5},{3,7},{5,1},{7,3},{8,12},{10,14},{12... | collective-permute-start | bytes 688136 | tf_op jit(solution)/shard_map/ppermute | solution.py:42
  199.6 1.9 collective-permute-start.13
  201.6 15.0 %collective-permute-done.14 = bf16[512,224]{0,1:T(8,128)(2,1)} collective-permute-done((bf16[512,224]{0,1:T(8,128)(2,1)S(1)}, bf16[512,224]{0,1:T(8,128)(2,1)}, u32[]{:S(2)}, u32[]{:S(2)}) %collective-permute-start.14) | collective-permute-done | bytes 229408 | tf_op jit(solution)/shard_map/ppermute | solution.py:148
  216.6 1.9 collective-permute-start.15
  218.5 1.9 collective-permute-start.16
  220.4 3.4 %collective-permute-start.17 = (bf16[512,224]{0,1:T(8,128)(2,1)}, bf16[512,224]{0,1:T(8,128)(2,1)}, u32[]{:S(2)}, u32[]{:S(2)}) collective-permute-start(bf16[512,224]{0,1:T(8,128)(2,1)} %collective-permute-done.14), channel_id=1, source_target_pairs={{0,6},{2,0},{4,2},{6,4},{1,7},{3,1},{5,3},{7,5},{8,14},{10,8},{12,... | collective-permute-start | bytes 688136 | tf_op jit(solution)/shard_map/ppermute | solution.py:42
  224.9 2.7 %gather_fusion.3 = bf16[4,512,224]{1,2,0:T(8,128)(2,1)} fusion(bf16[4,512,224]{1,2,0:T(8,128)(2,1)} %pad_maximum_fusion.1, s32[1024]{0:T(1024)S(1)} %pad_clamp_fusion), kind=kCustom, calls=%fused_computation.clone | custom fusion | bytes 1835024 | tf_op jit(solution)/shard_map/jit(_take)/gather | solution.py:44
  228.5 6.1 %collective-permute-done.17 = bf16[512,224]{0,1:T(8,128)(2,1)} collective-permute-done((bf16[512,224]{0,1:T(8,128)(2,1)}, bf16[512,224]{0,1:T(8,128)(2,1)}, u32[]{:S(2)}, u32[]{:S(2)}) %collective-permute-start.17) | collective-permute-done | bytes 229408 | tf_op jit(solution)/shard_map/ppermute | solution.py:42
  234.6 2.4 pad_maximum_fusion.2
  237.0 2.7 %gather_fusion.4 = bf16[4,512,224]{1,2,0:T(8,128)(2,1)} fusion(bf16[4,512,224]{1,2,0:T(8,128)(2,1)} %pad_maximum_fusion.2, s32[1024]{0:T(1024)S(1)} %pad_clamp_fusion), kind=kCustom, calls=%fused_computation.1.clone | custom fusion | bytes 1835024 | tf_op jit(solution)/shard_map/jit(_take)/gather | solution.py:44
  239.7 1.7 select_bitcast_fusion.1
  (91 shorter events, 22.7 us)
Async XLA Ops:
  0.0 4.3 %copy-start = (bf16[3,224,1024]{2,1,0:T(8,128)(2,1)S(1)}, bf16[3,224,1024]{2,1,0:T(8,128)(2,1)}, u32[]{:S(2)}) copy-start(bf16[3,224,1024]{2,1,0:T(8,128)(2,1)} %param.15) | copy-start | bytes 4128772
  5.6 7.3 %copy-start.6 = (bf16[224,224]{1,0:T(8,128)(2,1)S(1)}, bf16[224,224]{1,0:T(8,128)(2,1)}, u32[]{:S(2)}) copy-start(bf16[224,224]{1,0:T(8,128)(2,1)} %param.12) | copy-start | bytes 301060
  5.7 7.4 %copy-start.5 = (bf16[224,288]{0,1:T(8,128)(2,1)S(1)}, bf16[224,288]{0,1:T(8,128)(2,1)}, u32[]{:S(2)}) copy-start(bf16[224,288]{0,1:T(8,128)(2,1)} %param.11) | copy-start | bytes 387076
  8.6 17.7 %all-to-all-start = ((bf16[4,2,22935]{2,1,0:T(2,128)(2,1)}), bf16[4,2,22935]{2,1,0:T(2,128)(2,1)S(1)}, u32[]{:S(2)}, u32[]{:S(2)}) async-start(bf16[4,2,22935]{2,1,0:T(2,128)(2,1)} %pad_maximum_fusion.4), calls=%async_computation | async-start | bytes 737280 | tf_op jit(solution)/shard_map/all_to_all | solution.py:87
  13.1 4.3 %collective-permute-start = (bf16[224,512]{0,1:T(8,128)(2,1)S(1)}, bf16[224,512]{0,1:T(8,128)(2,1)S(1)}, u32[]{:S(2)}, u32[]{:S(2)}) collective-permute-start(bf16[224,512]{0,1:T(8,128)(2,1)S(1)} %get-tuple-element.16), channel_id=1, source_target_pairs={{0,8},{8,0},{1,9},{9,1},{2,10},{10,2},{3,11},{11,3},{4,12},{12,4},... | collective-permute-start | bytes 688136 | tf_op jit(solution)/shard_map/ppermute | solution.py:42
  18.2 37.7 %collective-permute-start.1 = (bf16[2,224,512]{1,2,0:T(8,128)(2,1)S(1)}, bf16[2,224,512]{1,2,0:T(8,128)(2,1)}, u32[]{:S(2)}, u32[]{:S(2)}) collective-permute-start(bf16[2,224,512]{1,2,0:T(8,128)(2,1)S(1)} %broadcast_select_fusion), channel_id=1, source_target_pairs={{0,16},{16,32},{32,48},{48,0},{1,17},{17,33},{33,49},{49,1},{2,18}... | collective-permute-start | bytes 1376264 | tf_op jit(solution)/shard_map/ppermute | solution.py:42
  20.3 35.6 %collective-permute-start.2 = (bf16[2,224,512]{1,2,0:T(8,128)(2,1)S(1)}, bf16[2,224,512]{1,2,0:T(8,128)(2,1)}, u32[]{:S(2)}, u32[]{:S(2)}) collective-permute-start(bf16[2,224,512]{1,2,0:T(8,128)(2,1)S(1)} %broadcast_select_fusion), channel_id=1, source_target_pairs={{0,32},{16,48},{32,0},{48,16},{1,33},{17,49},{33,1},{49,17},{2,34}... | collective-permute-start | bytes 1376264 | tf_op jit(solution)/shard_map/ppermute | solution.py:42
  24.4 31.5 %collective-permute-start.3 = (bf16[2,224,512]{1,2,0:T(8,128)(2,1)S(1)}, bf16[2,224,512]{1,2,0:T(8,128)(2,1)}, u32[]{:S(2)}, u32[]{:S(2)}) collective-permute-start(bf16[2,224,512]{1,2,0:T(8,128)(2,1)S(1)} %broadcast_select_fusion), channel_id=1, source_target_pairs={{0,48},{16,0},{32,16},{48,32},{1,49},{17,1},{33,17},{49,33},{2,50}... | collective-permute-start | bytes 1376264 | tf_op jit(solution)/shard_map/ppermute | solution.py:42
  27.2 16.0 %collective-permute-start.4 = (bf16[22944]{0:T(1024)(128)(2,1)S(1)}, bf16[22944]{0:T(1024)(128)(2,1)S(1)}, u32[]{:S(2)}, u32[]{:S(2)}) collective-permute-start(bf16[22944]{0:T(1024)(128)(2,1)S(1)} %pad_maximum_fusion.8), channel_id=1, source_target_pairs={{0,1},{1,0},{2,3},{3,2},{4,5},{5,4},{6,7},{7,6},{8,9},{9,8},{10,11... | collective-permute-start | bytes 137672 | tf_op jit(solution)/shard_map/ppermute | solution.py:93
  44.3 35.8 %all-to-all-start.1 = ((bf16[8,3,7644]{2,1,0:T(4,128)(2,1)}), bf16[8,3,7644]{2,1,0:T(4,128)(2,1)}, u32[]{:S(2)}, u32[]{:S(2)}) async-start(bf16[8,3,7644]{2,1,0:T(4,128)(2,1)} %broadcast_in_dim.110), calls=%async_computation.1 | async-start | bytes 983040 | tf_op jit(solution)/shard_map/all_to_all | solution.py:108
  60.0 1.9 copy-start.2
  62.6 1.4 copy-start.1
  65.3 34.1 %copy-start.7 = (f32[224]{0:T(256)S(1)}, f32[224]{0:T(256)}, u32[]{:S(2)}) copy-start(f32[224]{0:T(256)} %param.13) | copy-start | bytes 2692
  65.3 74.3 %collective-permute-start.5 = (bf16[576,512]{1,0:T(8,128)(2,1)}, bf16[576,512]{1,0:T(8,128)(2,1)}, u32[]{:S(2)}, u32[]{:S(2)}) collective-permute-start(bf16[576,512]{1,0:T(8,128)(2,1)} %get-tuple-element.10), channel_id=1, source_target_pairs={{0,2},{2,4},{4,6},{6,0},{1,3},{3,5},{5,7},{7,1},{8,10},{10,12},{12... | collective-permute-start | bytes 1769480 | tf_op jit(solution)/shard_map/ppermute | solution.py:53
  68.5 71.1 %collective-permute-start.6 = (bf16[576,512]{1,0:T(8,128)(2,1)}, bf16[576,512]{1,0:T(8,128)(2,1)}, u32[]{:S(2)}, u32[]{:S(2)}) collective-permute-start(bf16[576,512]{1,0:T(8,128)(2,1)} %get-tuple-element.12), channel_id=1, source_target_pairs={{0,4},{2,6},{4,0},{6,2},{1,5},{3,7},{5,1},{7,3},{8,12},{10,14},{12... | collective-permute-start | bytes 1769480 | tf_op jit(solution)/shard_map/ppermute | solution.py:53
  71.1 68.6 %collective-permute-start.7 = (bf16[576,512]{1,0:T(8,128)(2,1)}, bf16[576,512]{1,0:T(8,128)(2,1)}, u32[]{:S(2)}, u32[]{:S(2)}) collective-permute-start(bf16[576,512]{1,0:T(8,128)(2,1)} %get-tuple-element.11), channel_id=1, source_target_pairs={{0,6},{2,0},{4,2},{6,4},{1,7},{3,1},{5,3},{7,5},{8,14},{10,8},{12,... | collective-permute-start | bytes 1769480 | tf_op jit(solution)/shard_map/ppermute | solution.py:53
  90.8 28.9 %all-to-all-start.2 = ((bf16[8,2,3822]{2,1,0:T(2,128)(2,1)}), bf16[8,2,3822]{2,1,0:T(2,128)(2,1)}, u32[]{:S(2)}, u32[]{:S(2)}) async-start(bf16[8,2,3822]{2,1,0:T(2,128)(2,1)} %reshape.392), calls=%async_computation.2 | async-start | bytes 245760 | tf_op jit(solution)/shard_map/all_to_all | solution.py:111
  99.4 19.6 %collective-permute-start.10 = (f32[224]{0:T(256)S(1)}, f32[224]{0:T(256)S(1)}, u32[]{:S(2)}, u32[]{:S(2)}) collective-permute-start(f32[224]{0:T(256)S(1)} %copy-done.7), channel_id=1, source_target_pairs={{0,0},{1,8},{2,16},{3,24},{4,32},{5,40},{6,48},{7,56},{8,1},{9,9},... | collective-permute-start | bytes 2696 | tf_op jit(solution)/shard_map/ppermute | solution.py:145
  122.5 22.7 %collective-permute-start.8 = (bf16[8,7644]{1,0:T(8,128)(2,1)S(1)}, bf16[8,7644]{1,0:T(8,128)(2,1)}, u32[]{:S(2)}, u32[]{:S(2)}) collective-permute-start(bf16[8,7644]{1,0:T(8,128)(2,1)S(1)} %bitcast.84), channel_id=1, source_target_pairs={{0,0},{1,8},{2,16},{3,24},{4,32},{5,40},{6,48},{7,56},{8,1},{9,9},... | collective-permute-start | bytes 366920 | tf_op jit(solution)/shard_map/ppermute | solution.py:112
  148.0 33.5 %collective-permute-start.9 = (bf16[288,512]{1,0:T(8,128)(2,1)S(1)}, bf16[288,512]{1,0:T(8,128)(2,1)S(1)}, u32[]{:S(2)}, u32[]{:S(2)}) collective-permute-start(bf16[288,512]{1,0:T(8,128)(2,1)S(1)} %constant_dynamic-slice_fusion), channel_id=1, source_target_pairs={{0,1},{1,0},{2,3},{3,2},{4,5},{5,4},{6,7},{7,6},{8,9},{9,8},{10,11... | collective-permute-start | bytes 884744 | tf_op jit(solution)/shard_map/ppermute | solution.py:53
  182.6 0.7 copy-start.4
  189.2 27.3 %collective-permute-start.14 = (bf16[512,224]{0,1:T(8,128)(2,1)S(1)}, bf16[512,224]{0,1:T(8,128)(2,1)}, u32[]{:S(2)}, u32[]{:S(2)}) collective-permute-start(bf16[512,224]{0,1:T(8,128)(2,1)S(1)} %bitcast.69), channel_id=1, source_target_pairs={{0,1},{1,0},{2,3},{3,2},{4,5},{5,4},{6,7},{7,6},{8,9},{9,8},{10,11... | collective-permute-start | bytes 688136 | tf_op jit(solution)/shard_map/ppermute | solution.py:148
  191.2 29.2 %collective-permute-start.11 = (bf16[512,224]{0,1:T(8,128)(2,1)S(1)}, bf16[512,224]{0,1:T(8,128)(2,1)S(1)}, u32[]{:S(2)}, u32[]{:S(2)}) collective-permute-start(bf16[512,224]{0,1:T(8,128)(2,1)S(1)} %bitcast.70), channel_id=1, source_target_pairs={{0,2},{2,4},{4,6},{6,0},{1,3},{3,5},{5,7},{7,1},{8,10},{10,12},{12... | collective-permute-start | bytes 688136 | tf_op jit(solution)/shard_map/ppermute | solution.py:42
  193.1 30.7 %collective-permute-start.12 = (bf16[512,224]{0,1:T(8,128)(2,1)S(1)}, bf16[512,224]{0,1:T(8,128)(2,1)S(1)}, u32[]{:S(2)}, u32[]{:S(2)}) collective-permute-start(bf16[512,224]{0,1:T(8,128)(2,1)S(1)} %bitcast.71), channel_id=1, source_target_pairs={{0,4},{2,6},{4,0},{6,2},{1,5},{3,7},{5,1},{7,3},{8,12},{10,14},{12... | collective-permute-start | bytes 688136 | tf_op jit(solution)/shard_map/ppermute | solution.py:42
  199.6 24.2 %collective-permute-start.13 = (bf16[512,224]{0,1:T(8,128)(2,1)S(1)}, bf16[512,224]{0,1:T(8,128)(2,1)S(1)}, u32[]{:S(2)}, u32[]{:S(2)}) collective-permute-start(bf16[512,224]{0,1:T(8,128)(2,1)S(1)} %bitcast.72), channel_id=1, source_target_pairs={{0,6},{2,0},{4,2},{6,4},{1,7},{3,1},{5,3},{7,5},{8,14},{10,8},{12,... | collective-permute-start | bytes 688136 | tf_op jit(solution)/shard_map/ppermute | solution.py:42
  216.6 11.1 %collective-permute-start.15 = (bf16[512,224]{0,1:T(8,128)(2,1)}, bf16[512,224]{0,1:T(8,128)(2,1)}, u32[]{:S(2)}, u32[]{:S(2)}) collective-permute-start(bf16[512,224]{0,1:T(8,128)(2,1)} %collective-permute-done.14), channel_id=1, source_target_pairs={{0,2},{2,4},{4,6},{6,0},{1,3},{3,5},{5,7},{7,1},{8,10},{10,12},{12... | collective-permute-start | bytes 688136 | tf_op jit(solution)/shard_map/ppermute | solution.py:42
  218.5 10.0 %collective-permute-start.16 = (bf16[512,224]{0,1:T(8,128)(2,1)}, bf16[512,224]{0,1:T(8,128)(2,1)}, u32[]{:S(2)}, u32[]{:S(2)}) collective-permute-start(bf16[512,224]{0,1:T(8,128)(2,1)} %collective-permute-done.14), channel_id=1, source_target_pairs={{0,4},{2,6},{4,0},{6,2},{1,5},{3,7},{5,1},{7,3},{8,12},{10,14},{12... | collective-permute-start | bytes 688136 | tf_op jit(solution)/shard_map/ppermute | solution.py:42
  220.4 14.2 %collective-permute-start.17 = (bf16[512,224]{0,1:T(8,128)(2,1)}, bf16[512,224]{0,1:T(8,128)(2,1)}, u32[]{:S(2)}, u32[]{:S(2)}) collective-permute-start(bf16[512,224]{0,1:T(8,128)(2,1)} %collective-permute-done.14), channel_id=1, source_target_pairs={{0,6},{2,0},{4,2},{6,4},{1,7},{3,1},{5,3},{7,5},{8,14},{10,8},{12,... | collective-permute-start | bytes 688136 | tf_op jit(solution)/shard_map/ppermute | solution.py:42
  241.9 0.9 copy-start.3

commit v12 on v10

--- a/solution.py
+++ b/solution.py
@@ -109,7 +109,16 @@
     pieces = pieces.reshape((-1, piece))
     to_send = jnp.take(pieces, owners, axis=0)
     chosen = lax.all_to_all(to_send, COL, 0, 0, tiled=True)
-    chosen = lax.ppermute(chosen, flat, perm)
+    g_hi = lax.reduce_precision(head_gain, exponent_bits=8, mantissa_bits=7)
+    g_rest = head_gain - g_hi
+    g_mid = lax.reduce_precision(g_rest, exponent_bits=8, mantissa_bits=7)
+    g_lo = lax.reduce_precision(g_rest - g_mid, exponent_bits=8, mantissa_bits=7)
+    g_parts = jnp.concatenate([g_hi, g_mid, g_lo]).astype(jnp.bfloat16)
+    n_state = chosen.size
+    moved = lax.ppermute(jnp.concatenate([chosen.reshape(-1), g_parts]), flat, perm)
+    chosen = moved[:n_state].reshape(chosen.shape)
+    g_parts = moved[n_state:].reshape(3, -1).astype(jnp.float32)
+    gains_moved = g_parts[0] + g_parts[1] + g_parts[2]
     chosen = chosen.reshape(state_shape).astype(jnp.float32)
 
     both = jnp.concatenate([qkv_weight, out_weight], axis=1)
@@ -142,7 +151,7 @@
     active = (positions < length)[:, None, None]
     attended = jnp.where(active, carried + within, 0.0)
     inverse_rms = lax.rsqrt(jnp.mean(attended * attended, axis=-1, keepdims=True) + epsilon)
-    gains = lax.ppermute(head_gain, flat, perm).reshape(heads_here, HD)
+    gains = gains_moved.reshape(heads_here, HD)
     normed = (attended * inverse_rms * gains).astype(jnp.bfloat16).reshape(SLOTS, heads_here * HD)
     hidden = gather_by_shifts(gather_by_shifts(normed, "zh", 2), "y", n_col // 2)
     hidden = hidden.reshape((n_col,) + normed.shape)

time: 237 us -> 229 us (0.966)
  the two profiles are of different devices: /device:TPU:38 before, /device:TPU:65 now
where the time goes in v12:
time: 229 us; the launch traced here: 228 us
  starting transfers between devices  106 us (46%)
  waiting for transfers between devices  73.4 us (32%)
  local copies, waits for them, and re-layouts  20.3 us (9%)
  other arithmetic  19.2 us (8%)
  matrix products  7.47 us (3%)
    ppermute x8, starting transfers between devices, gather_by_shifts(): lax.ppermute(x, axis, [(i, (i + k) % n) for i in range(n)])  48.7 us
    ppermute x8, waiting for transfers between devices, gather_by_shifts(): lax.ppermute(x, axis, [(i, (i + k) % n) for i in range(n)])  32.1 us
    ppermute x4, waiting for transfers between devices, reduce_scatter_by_shifts(): lax.ppermute(part, axis, [(i, (i + k) % n) for i in range(n)])  19.2 us
    ppermute x1, starting transfers between devices, shards(): lax.ppermute(jnp.concatenate([other, meta_y.reshape(-1)]), 'zh', [(0, 1),...  13.6 us
    all_to_all x1, waiting for transfers between devices, shards(): chosen = lax.all_to_all(to_send, COL, 0, 0, tiled=True)  12.2 us
    ppermute x4, starting transfers between devices, reduce_scatter_by_shifts(): lax.ppermute(part, axis, [(i, (i + k) % n) for i in range(n)])  11.9 us
    all_to_all x1, starting transfers between devices, shards(): pieces = lax.all_to_all(pieces, 'req', 0, 0, tiled=True)  11.4 us
    all_to_all x1, starting transfers between devices, shards(): chosen = lax.all_to_all(to_send, COL, 0, 0, tiled=True)  9.14 us
  transfers between devices with their start and end apart: 17, of which 9 were waited for; matrix products, arithmetic and copies ran while one was open for 12% of the time, Pallas kernels for 0%

profile of v12, /device:TPU:65, one launch (start us, length us, event | category | flops | bytes accessed | tf_op | source)
XLA Modules:
  0.0 228.0 jit_solution(4118377830952915721)
XLA Ops:
  0.0 1.1 convert.54
  1.1 1.0 multiply_convert_fusion.3
  2.7 0.9 multiply_convert_fusion
  3.6 1.3 fusion.7
  5.0 0.9 reshape.468
  7.4 1.1 pad_maximum_fusion.4
  8.6 4.2 %all-to-all-start = ((bf16[4,2,22935]{2,1,0:T(2,128)(2,1)}), bf16[4,2,22935]{2,1,0:T(2,128)(2,1)S(1)}, u32[]{:S(2)}, u32[]{:S(2)}) async-start(bf16[4,2,22935]{2,1,0:T(2,128)(2,1)} %pad_maximum_fusion.4), calls=%async_computation | async-start | bytes 737280 | tf_op jit(solution)/shard_map/all_to_all | solution.py:87
  12.9 2.9 %collective-permute-start = (bf16[224,512]{0,1:T(8,128)(2,1)S(1)}, bf16[224,512]{0,1:T(8,128)(2,1)S(1)}, u32[]{:S(2)}, u32[]{:S(2)}) collective-permute-start(bf16[224,512]{0,1:T(8,128)(2,1)S(1)} %get-tuple-element.15), channel_id=1, source_target_pairs={{0,8},{8,0},{1,9},{9,1},{2,10},{10,2},{3,11},{11,3},{4,12},{12,4},... | collective-permute-start | bytes 688136 | tf_op jit(solution)/shard_map/ppermute | solution.py:42
  16.1 0.8 collective-permute-done
  17.7 4.4 %collective-permute-start.3 = (bf16[2,224,512]{1,2,0:T(8,128)(2,1)S(1)}, bf16[2,224,512]{1,2,0:T(8,128)(2,1)}, u32[]{:S(2)}, u32[]{:S(2)}) collective-permute-start(bf16[2,224,512]{1,2,0:T(8,128)(2,1)S(1)} %broadcast_select_fusion), channel_id=1, source_target_pairs={{0,48},{16,0},{32,16},{48,32},{1,49},{17,1},{33,17},{49,33},{2,50}... | collective-permute-start | bytes 1376264 | tf_op jit(solution)/shard_map/ppermute | solution.py:42
  22.1 2.4 %collective-permute-start.2 = (bf16[2,224,512]{1,2,0:T(8,128)(2,1)S(1)}, bf16[2,224,512]{1,2,0:T(8,128)(2,1)}, u32[]{:S(2)}, u32[]{:S(2)}) collective-permute-start(bf16[2,224,512]{1,2,0:T(8,128)(2,1)S(1)} %broadcast_select_fusion), channel_id=1, source_target_pairs={{0,32},{16,48},{32,0},{48,16},{1,33},{17,49},{33,1},{49,17},{2,34}... | collective-permute-start | bytes 1376264 | tf_op jit(solution)/shard_map/ppermute | solution.py:42
  24.6 2.5 %collective-permute-start.1 = (bf16[2,224,512]{1,2,0:T(8,128)(2,1)S(1)}, bf16[2,224,512]{1,2,0:T(8,128)(2,1)}, u32[]{:S(2)}, u32[]{:S(2)}) collective-permute-start(bf16[2,224,512]{1,2,0:T(8,128)(2,1)S(1)} %broadcast_select_fusion), channel_id=1, source_target_pairs={{0,16},{16,32},{32,48},{48,0},{1,17},{17,33},{33,49},{49,1},{2,18}... | collective-permute-start | bytes 1376264 | tf_op jit(solution)/shard_map/ppermute | solution.py:42
  28.0 13.6 %collective-permute-start.4 = (bf16[22944]{0:T(1024)(128)(2,1)S(1)}, bf16[22944]{0:T(1024)(128)(2,1)S(1)}, u32[]{:S(2)}, u32[]{:S(2)}) collective-permute-start(bf16[22944]{0:T(1024)(128)(2,1)S(1)} %pad_maximum_fusion.8), channel_id=1, source_target_pairs={{0,1},{1,0},{2,3},{3,2},{4,5},{5,4},{6,7},{7,6},{8,9},{9,8},{10,11... | collective-permute-start | bytes 137672 | tf_op jit(solution)/shard_map/ppermute | solution.py:93
  41.7 0.9 bitcast_select_fusion.2
  43.5 0.9 broadcast_in_dim.133
  44.4 11.4 %all-to-all-start.1 = ((bf16[8,3,7644]{2,1,0:T(4,128)(2,1)}), bf16[8,3,7644]{2,1,0:T(4,128)(2,1)}, u32[]{:S(2)}, u32[]{:S(2)}) async-start(bf16[8,3,7644]{2,1,0:T(4,128)(2,1)} %broadcast_in_dim.133), calls=%async_computation.1 | async-start | bytes 983040 | tf_op jit(solution)/shard_map/all_to_all | solution.py:108
  56.1 2.1 pad_maximum_fusion
  58.1 2.0 gather_fusion.1
  60.2 1.9 bitcast_select_fusion
  62.9 1.4 copy-done.1
  64.3 1.2 constant_dynamic-slice_fusion.3
  65.4 5.0 %collective-permute-start.7 = (bf16[576,512]{1,0:T(8,128)(2,1)}, bf16[576,512]{1,0:T(8,128)(2,1)S(1)}, u32[]{:S(2)}, u32[]{:S(2)}) collective-permute-start(bf16[576,512]{1,0:T(8,128)(2,1)} %get-tuple-element.10), channel_id=1, source_target_pairs={{0,6},{2,0},{4,2},{6,4},{1,7},{3,1},{5,3},{7,5},{8,14},{10,8},{12,... | collective-permute-start | bytes 1769480 | tf_op jit(solution)/shard_map/ppermute | solution.py:53
  70.4 2.5 %collective-permute-start.6 = (bf16[576,512]{1,0:T(8,128)(2,1)}, bf16[576,512]{1,0:T(8,128)(2,1)}, u32[]{:S(2)}, u32[]{:S(2)}) collective-permute-start(bf16[576,512]{1,0:T(8,128)(2,1)} %get-tuple-element.11), channel_id=1, source_target_pairs={{0,4},{2,6},{4,0},{6,2},{1,5},{3,7},{5,1},{7,3},{8,12},{10,14},{12... | collective-permute-start | bytes 1769480 | tf_op jit(solution)/shard_map/ppermute | solution.py:53
  72.9 2.5 %collective-permute-start.5 = (bf16[576,512]{1,0:T(8,128)(2,1)S(1)}, bf16[576,512]{1,0:T(8,128)(2,1)}, u32[]{:S(2)}, u32[]{:S(2)}) collective-permute-start(bf16[576,512]{1,0:T(8,128)(2,1)S(1)} %get-tuple-element.9), channel_id=1, source_target_pairs={{0,2},{2,4},{4,6},{6,0},{1,3},{3,5},{5,7},{7,1},{8,10},{10,12},{12... | collective-permute-start | bytes 1769480 | tf_op jit(solution)/shard_map/ppermute | solution.py:53
  75.4 2.9 %all-to-all-done.1 = bf16[8,3,7644]{2,1,0:T(4,128)(2,1)} async-done(((bf16[8,3,7644]{2,1,0:T(4,128)(2,1)}), bf16[8,3,7644]{2,1,0:T(4,128)(2,1)}, u32[]{:S(2)}, u32[]{:S(2)}) %all-to-all-start.1) | async-done | bytes 366944 | tf_op jit(solution)/shard_map/all_to_all | solution.py:108
  78.3 1.3 reshape.471
  81.6 0.8 reshape.530
  82.4 9.1 %all-to-all-start.2 = ((bf16[8,2,3822]{2,1,0:T(2,128)(2,1)}), bf16[8,2,3822]{2,1,0:T(2,128)(2,1)S(1)}, u32[]{:S(2)}, u32[]{:S(2)}) async-start(bf16[8,2,3822]{2,1,0:T(2,128)(2,1)} %reshape.530), calls=%async_computation.2 | async-start | bytes 245760 | tf_op jit(solution)/shard_map/all_to_all | solution.py:111
  92.7 0.8 fusion.17
  93.5 12.2 %all-to-all-done.2 = bf16[8,2,3822]{2,1,0:T(2,128)(2,1)S(1)} async-done(((bf16[8,2,3822]{2,1,0:T(2,128)(2,1)}), bf16[8,2,3822]{2,1,0:T(2,128)(2,1)S(1)}, u32[]{:S(2)}, u32[]{:S(2)}) %all-to-all-start.2) | async-done | bytes 122336 | tf_op jit(solution)/shard_map/all_to_all | solution.py:111
  106.9 3.6 %concatenate.32 = bf16[61824]{0:T(1024)(128)(2,1)} concatenate(bf16[61152]{0:T(1024)(128)(2,1)S(1)} %reshape.472, bf16[224]{0:T(256)(128)(2,1)S(1)} %get-tuple-element.20, bf16[224]{0:T(256)(128)(2,1)S(1)} %get-tuple-element.19, bf16[224]{0:T(256)(128)(2,1)S(1)} %get-tuple-element.18), dimensions={0} | concatenate | bytes 247296 | tf_op jit(solution)/shard_map/concatenate | solution.py:118
  110.4 6.7 %collective-permute-start.8 = (bf16[61824]{0:T(1024)(128)(2,1)}, bf16[61824]{0:T(1024)(128)(2,1)S(1)}, u32[]{:S(2)}, u32[]{:S(2)}) collective-permute-start(bf16[61824]{0:T(1024)(128)(2,1)} %concatenate.32), channel_id=1, source_target_pairs={{0,0},{1,8},{2,16},{3,24},{4,32},{5,40},{6,48},{7,56},{8,1},{9,9},... | collective-permute-start | bytes 370952 | tf_op jit(solution)/shard_map/ppermute | solution.py:118
  117.2 1.7 add_convert_fusion
  118.9 6.8 %collective-permute-done.8 = bf16[61824]{0:T(1024)(128)(2,1)S(1)} collective-permute-done((bf16[61824]{0:T(1024)(128)(2,1)}, bf16[61824]{0:T(1024)(128)(2,1)S(1)}, u32[]{:S(2)}, u32[]{:S(2)}) %collective-permute-start.8) | collective-permute-done | bytes 123680 | tf_op jit(solution)/shard_map/ppermute | solution.py:118
  126.7 1.9 collective-permute-start.9
  129.5 19.1 %collective-permute-done.9 = bf16[288,512]{1,0:T(8,128)(2,1)S(1)} collective-permute-done((bf16[288,512]{1,0:T(8,128)(2,1)S(1)}, bf16[288,512]{1,0:T(8,128)(2,1)S(1)}, u32[]{:S(2)}, u32[]{:S(2)}) %collective-permute-start.9) | collective-permute-done | bytes 294944 | tf_op jit(solution)/shard_map/ppermute | solution.py:53
  148.8 1.7 fusion.6
  150.6 1.8 multiply_reduce_fusion
  152.6 2.7 %collective-permute-start.10 = (bf16[512,224]{0,1:T(8,128)(2,1)S(1)}, bf16[512,224]{0,1:T(8,128)(2,1)S(1)}, u32[]{:S(2)}, u32[]{:S(2)}) collective-permute-start(bf16[512,224]{0,1:T(8,128)(2,1)S(1)} %bitcast.65), channel_id=1, source_target_pairs={{0,1},{1,0},{2,3},{3,2},{4,5},{5,4},{6,7},{7,6},{8,9},{9,8},{10,11... | collective-permute-start | bytes 688136 | tf_op jit(solution)/shard_map/ppermute | solution.py:42
  155.5 12.8 %collective-permute-done.10 = bf16[512,224]{0,1:T(8,128)(2,1)S(1)} collective-permute-done((bf16[512,224]{0,1:T(8,128)(2,1)S(1)}, bf16[512,224]{0,1:T(8,128)(2,1)S(1)}, u32[]{:S(2)}, u32[]{:S(2)}) %collective-permute-start.10) | collective-permute-done | bytes 229408 | tf_op jit(solution)/shard_map/ppermute | solution.py:42
  169.0 26.9 %collective-permute-start.13 = (bf16[2,512,224]{1,2,0:T(8,128)(2,1)S(1)}, bf16[2,512,224]{1,2,0:T(8,128)(2,1)S(1)}, u32[]{:S(2)}, u32[]{:S(2)}) collective-permute-start(bf16[2,512,224]{1,2,0:T(8,128)(2,1)S(1)} %broadcast_select_fusion.1), channel_id=1, source_target_pairs={{0,6},{2,0},{4,2},{6,4},{1,7},{3,1},{5,3},{7,5},{8,14},{10,8},{12,... | collective-permute-start | bytes 1376264 | tf_op jit(solution)/shard_map/ppermute | solution.py:42
  195.9 4.2 %collective-permute-start.12 = (bf16[2,512,224]{1,2,0:T(8,128)(2,1)S(1)}, bf16[2,512,224]{1,2,0:T(8,128)(2,1)S(1)}, u32[]{:S(2)}, u32[]{:S(2)}) collective-permute-start(bf16[2,512,224]{1,2,0:T(8,128)(2,1)S(1)} %broadcast_select_fusion.1), channel_id=1, source_target_pairs={{0,4},{2,6},{4,0},{6,2},{1,5},{3,7},{5,1},{7,3},{8,12},{10,14},{12... | collective-permute-start | bytes 1376264 | tf_op jit(solution)/shard_map/ppermute | solution.py:42
  200.1 2.8 %collective-permute-start.11 = (bf16[2,512,224]{1,2,0:T(8,128)(2,1)S(1)}, bf16[2,512,224]{1,2,0:T(8,128)(2,1)S(1)}, u32[]{:S(2)}, u32[]{:S(2)}) collective-permute-start(bf16[2,512,224]{1,2,0:T(8,128)(2,1)S(1)} %broadcast_select_fusion.1), channel_id=1, source_target_pairs={{0,2},{2,4},{4,6},{6,0},{1,3},{3,5},{5,7},{7,1},{8,10},{10,12},{12... | collective-permute-start | bytes 1376264 | tf_op jit(solution)/shard_map/ppermute | solution.py:42
  203.0 12.0 %collective-permute-done.13 = bf16[2,512,224]{1,2,0:T(8,128)(2,1)S(1)} collective-permute-done((bf16[2,512,224]{1,2,0:T(8,128)(2,1)S(1)}, bf16[2,512,224]{1,2,0:T(8,128)(2,1)S(1)}, u32[]{:S(2)}, u32[]{:S(2)}) %collective-permute-start.13) | collective-permute-done | bytes 458784 | tf_op jit(solution)/shard_map/ppermute | solution.py:42
  215.0 6.5 %collective-permute-done.11 = bf16[2,512,224]{1,2,0:T(8,128)(2,1)S(1)} collective-permute-done((bf16[2,512,224]{1,2,0:T(8,128)(2,1)S(1)}, bf16[2,512,224]{1,2,0:T(8,128)(2,1)S(1)}, u32[]{:S(2)}, u32[]{:S(2)}) %collective-permute-start.11) | collective-permute-done | bytes 458784 | tf_op jit(solution)/shard_map/ppermute | solution.py:42
  221.8 1.9 gather_fusion.4
  223.7 1.7 bitcast_select_fusion.1
  225.4 1.8 convert_reduce_fusion
  (95 shorter events, 13.2 us)
Async XLA Ops:
  0.0 3.6 %copy-start = (bf16[3,224,1024]{2,1,0:T(8,128)(2,1)S(1)}, bf16[3,224,1024]{2,1,0:T(8,128)(2,1)}, u32[]{:S(2)}) copy-start(bf16[3,224,1024]{2,1,0:T(8,128)(2,1)} %param.13) | copy-start | bytes 4128772
  4.9 7.8 %copy-start.7 = (bf16[224,224]{1,0:T(8,128)(2,1)S(1)}, bf16[224,224]{1,0:T(8,128)(2,1)}, u32[]{:S(2)}) copy-start(bf16[224,224]{1,0:T(8,128)(2,1)} %param.10) | copy-start | bytes 301060
  5.0 7.9 %copy-start.5 = (bf16[224,288]{0,1:T(8,128)(2,1)S(1)}, bf16[224,288]{0,1:T(8,128)(2,1)}, u32[]{:S(2)}) copy-start(bf16[224,288]{0,1:T(8,128)(2,1)} %param.9) | copy-start | bytes 387076
  8.6 18.5 %all-to-all-start = ((bf16[4,2,22935]{2,1,0:T(2,128)(2,1)}), bf16[4,2,22935]{2,1,0:T(2,128)(2,1)S(1)}, u32[]{:S(2)}, u32[]{:S(2)}) async-start(bf16[4,2,22935]{2,1,0:T(2,128)(2,1)} %pad_maximum_fusion.4), calls=%async_computation | async-start | bytes 737280 | tf_op jit(solution)/shard_map/all_to_all | solution.py:87
  12.9 4.0 %collective-permute-start = (bf16[224,512]{0,1:T(8,128)(2,1)S(1)}, bf16[224,512]{0,1:T(8,128)(2,1)S(1)}, u32[]{:S(2)}, u32[]{:S(2)}) collective-permute-start(bf16[224,512]{0,1:T(8,128)(2,1)S(1)} %get-tuple-element.15), channel_id=1, source_target_pairs={{0,8},{8,0},{1,9},{9,1},{2,10},{10,2},{3,11},{11,3},{4,12},{12,4},... | collective-permute-start | bytes 688136 | tf_op jit(solution)/shard_map/ppermute | solution.py:42
  17.7 38.3 %collective-permute-start.3 = (bf16[2,224,512]{1,2,0:T(8,128)(2,1)S(1)}, bf16[2,224,512]{1,2,0:T(8,128)(2,1)}, u32[]{:S(2)}, u32[]{:S(2)}) collective-permute-start(bf16[2,224,512]{1,2,0:T(8,128)(2,1)S(1)} %broadcast_select_fusion), channel_id=1, source_target_pairs={{0,48},{16,0},{32,16},{48,32},{1,49},{17,1},{33,17},{49,33},{2,50}... | collective-permute-start | bytes 1376264 | tf_op jit(solution)/shard_map/ppermute | solution.py:42
  22.1 33.9 %collective-permute-start.2 = (bf16[2,224,512]{1,2,0:T(8,128)(2,1)S(1)}, bf16[2,224,512]{1,2,0:T(8,128)(2,1)}, u32[]{:S(2)}, u32[]{:S(2)}) collective-permute-start(bf16[2,224,512]{1,2,0:T(8,128)(2,1)S(1)} %broadcast_select_fusion), channel_id=1, source_target_pairs={{0,32},{16,48},{32,0},{48,16},{1,33},{17,49},{33,1},{49,17},{2,34}... | collective-permute-start | bytes 1376264 | tf_op jit(solution)/shard_map/ppermute | solution.py:42
  24.6 31.5 %collective-permute-start.1 = (bf16[2,224,512]{1,2,0:T(8,128)(2,1)S(1)}, bf16[2,224,512]{1,2,0:T(8,128)(2,1)}, u32[]{:S(2)}, u32[]{:S(2)}) collective-permute-start(bf16[2,224,512]{1,2,0:T(8,128)(2,1)S(1)} %broadcast_select_fusion), channel_id=1, source_target_pairs={{0,16},{16,32},{32,48},{48,0},{1,17},{17,33},{33,49},{49,1},{2,18}... | collective-permute-start | bytes 1376264 | tf_op jit(solution)/shard_map/ppermute | solution.py:42
  28.0 15.1 %collective-permute-start.4 = (bf16[22944]{0:T(1024)(128)(2,1)S(1)}, bf16[22944]{0:T(1024)(128)(2,1)S(1)}, u32[]{:S(2)}, u32[]{:S(2)}) collective-permute-start(bf16[22944]{0:T(1024)(128)(2,1)S(1)} %pad_maximum_fusion.8), channel_id=1, source_target_pairs={{0,1},{1,0},{2,3},{3,2},{4,5},{5,4},{6,7},{7,6},{8,9},{9,8},{10,11... | collective-permute-start | bytes 137672 | tf_op jit(solution)/shard_map/ppermute | solution.py:93
  44.4 33.9 %all-to-all-start.1 = ((bf16[8,3,7644]{2,1,0:T(4,128)(2,1)}), bf16[8,3,7644]{2,1,0:T(4,128)(2,1)}, u32[]{:S(2)}, u32[]{:S(2)}) async-start(bf16[8,3,7644]{2,1,0:T(4,128)(2,1)} %broadcast_in_dim.133), calls=%async_computation.1 | async-start | bytes 983040 | tf_op jit(solution)/shard_map/all_to_all | solution.py:108
  60.2 1.9 copy-start.3
  62.1 3.4 %copy-start.2 = (bf16[8,224,512]{1,2,0:T(8,128)(2,1)}, bf16[8,224,512]{1,2,0:T(8,128)(2,1)S(1)}, u32[]{:S(2)}) copy-start(bf16[8,224,512]{1,2,0:T(8,128)(2,1)S(1)} %bitcast_select_fusion) | copy-start | bytes 5505028
  62.9 1.4 copy-start.1
  65.4 26.1 %copy-start.8 = (f32[224]{0:T(256)S(1)}, f32[224]{0:T(256)}, u32[]{:S(2)}) copy-start(f32[224]{0:T(256)} %param.11) | copy-start | bytes 2692
  65.4 51.7 %collective-permute-start.7 = (bf16[576,512]{1,0:T(8,128)(2,1)}, bf16[576,512]{1,0:T(8,128)(2,1)S(1)}, u32[]{:S(2)}, u32[]{:S(2)}) collective-permute-start(bf16[576,512]{1,0:T(8,128)(2,1)} %get-tuple-element.10), channel_id=1, source_target_pairs={{0,6},{2,0},{4,2},{6,4},{1,7},{3,1},{5,3},{7,5},{8,14},{10,8},{12,... | collective-permute-start | bytes 1769480 | tf_op jit(solution)/shard_map/ppermute | solution.py:53
  70.4 46.8 %collective-permute-start.6 = (bf16[576,512]{1,0:T(8,128)(2,1)}, bf16[576,512]{1,0:T(8,128)(2,1)}, u32[]{:S(2)}, u32[]{:S(2)}) collective-permute-start(bf16[576,512]{1,0:T(8,128)(2,1)} %get-tuple-element.11), channel_id=1, source_target_pairs={{0,4},{2,6},{4,0},{6,2},{1,5},{3,7},{5,1},{7,3},{8,12},{10,14},{12... | collective-permute-start | bytes 1769480 | tf_op jit(solution)/shard_map/ppermute | solution.py:53
  72.9 44.3 %collective-permute-start.5 = (bf16[576,512]{1,0:T(8,128)(2,1)S(1)}, bf16[576,512]{1,0:T(8,128)(2,1)}, u32[]{:S(2)}, u32[]{:S(2)}) collective-permute-start(bf16[576,512]{1,0:T(8,128)(2,1)S(1)} %get-tuple-element.9), channel_id=1, source_target_pairs={{0,2},{2,4},{4,6},{6,0},{1,3},{3,5},{5,7},{7,1},{8,10},{10,12},{12... | collective-permute-start | bytes 1769480 | tf_op jit(solution)/shard_map/ppermute | solution.py:53
  82.4 23.4 %all-to-all-start.2 = ((bf16[8,2,3822]{2,1,0:T(2,128)(2,1)}), bf16[8,2,3822]{2,1,0:T(2,128)(2,1)S(1)}, u32[]{:S(2)}, u32[]{:S(2)}) async-start(bf16[8,2,3822]{2,1,0:T(2,128)(2,1)} %reshape.530), calls=%async_computation.2 | async-start | bytes 245760 | tf_op jit(solution)/shard_map/all_to_all | solution.py:111
  110.4 38.4 %copy-start.4 = (pred[512,512]{1,0:T(8,128)(4,1)S(1)}, pred[512,512]{1,0:T(8,128)(4,1)}, u32[]{:S(2)}) copy-start(pred[512,512]{1,0:T(8,128)(4,1)} %fusion.17) | copy-start | bytes 786436
  110.4 15.3 %collective-permute-start.8 = (bf16[61824]{0:T(1024)(128)(2,1)}, bf16[61824]{0:T(1024)(128)(2,1)S(1)}, u32[]{:S(2)}, u32[]{:S(2)}) collective-permute-start(bf16[61824]{0:T(1024)(128)(2,1)} %concatenate.32), channel_id=1, source_target_pairs={{0,0},{1,8},{2,16},{3,24},{4,32},{5,40},{6,48},{7,56},{8,1},{9,9},... | collective-permute-start | bytes 370952 | tf_op jit(solution)/shard_map/ppermute | solution.py:118
  125.7 0.6 copy-start.6
  126.7 22.0 %collective-permute-start.9 = (bf16[288,512]{1,0:T(8,128)(2,1)S(1)}, bf16[288,512]{1,0:T(8,128)(2,1)S(1)}, u32[]{:S(2)}, u32[]{:S(2)}) collective-permute-start(bf16[288,512]{1,0:T(8,128)(2,1)S(1)} %constant_dynamic-slice_fusion), channel_id=1, source_target_pairs={{0,1},{1,0},{2,3},{3,2},{4,5},{5,4},{6,7},{7,6},{8,9},{9,8},{10,11... | collective-permute-start | bytes 884744 | tf_op jit(solution)/shard_map/ppermute | solution.py:53
  152.6 15.7 %collective-permute-start.10 = (bf16[512,224]{0,1:T(8,128)(2,1)S(1)}, bf16[512,224]{0,1:T(8,128)(2,1)S(1)}, u32[]{:S(2)}, u32[]{:S(2)}) collective-permute-start(bf16[512,224]{0,1:T(8,128)(2,1)S(1)} %bitcast.65), channel_id=1, source_target_pairs={{0,1},{1,0},{2,3},{3,2},{4,5},{5,4},{6,7},{7,6},{8,9},{9,8},{10,11... | collective-permute-start | bytes 688136 | tf_op jit(solution)/shard_map/ppermute | solution.py:42
  169.0 46.0 %collective-permute-start.13 = (bf16[2,512,224]{1,2,0:T(8,128)(2,1)S(1)}, bf16[2,512,224]{1,2,0:T(8,128)(2,1)S(1)}, u32[]{:S(2)}, u32[]{:S(2)}) collective-permute-start(bf16[2,512,224]{1,2,0:T(8,128)(2,1)S(1)} %broadcast_select_fusion.1), channel_id=1, source_target_pairs={{0,6},{2,0},{4,2},{6,4},{1,7},{3,1},{5,3},{7,5},{8,14},{10,8},{12,... | collective-permute-start | bytes 1376264 | tf_op jit(solution)/shard_map/ppermute | solution.py:42
  195.9 19.2 %collective-permute-start.12 = (bf16[2,512,224]{1,2,0:T(8,128)(2,1)S(1)}, bf16[2,512,224]{1,2,0:T(8,128)(2,1)S(1)}, u32[]{:S(2)}, u32[]{:S(2)}) collective-permute-start(bf16[2,512,224]{1,2,0:T(8,128)(2,1)S(1)} %broadcast_select_fusion.1), channel_id=1, source_target_pairs={{0,4},{2,6},{4,0},{6,2},{1,5},{3,7},{5,1},{7,3},{8,12},{10,14},{12... | collective-permute-start | bytes 1376264 | tf_op jit(solution)/shard_map/ppermute | solution.py:42
  200.1 21.4 %collective-permute-start.11 = (bf16[2,512,224]{1,2,0:T(8,128)(2,1)S(1)}, bf16[2,512,224]{1,2,0:T(8,128)(2,1)S(1)}, u32[]{:S(2)}, u32[]{:S(2)}) collective-permute-start(bf16[2,512,224]{1,2,0:T(8,128)(2,1)S(1)} %broadcast_select_fusion.1), channel_id=1, source_target_pairs={{0,2},{2,4},{4,6},{6,0},{1,3},{3,5},{5,7},{7,1},{8,10},{10,12},{12... | collective-permute-start | bytes 1376264 | tf_op jit(solution)/shard_map/ppermute | solution.py:42
